TPU v7x, 256 devices: a whole 4x4x8 slice. The times are simulated.
256 devices in a mesh: ctx: 16 (over x_lo, z), fsdp: 4 (over y), head: 4 (over x_hi, core).
Axes of the slice: x: 4 (x_hi: 2, x_lo: 2; x = x_hi * 2 + x_lo), y: 4, z: 8, core: 2. Of those that a mesh axis runs over, the one named last changes fastest.
Arguments:
- queries: bfloat16 [4, 8192, 2048], P('fsdp', 'ctx', 'head'), may hold values from -6 to 6
- keys: bfloat16 [4, 8192, 2048], P('fsdp', 'ctx', 'head'), may hold values from -6 to 6
- values: bfloat16 [4, 8192, 2048], P('fsdp', 'ctx', 'head'), may hold values from -6 to 6
- gate_pre: bfloat16 [4, 8192, 2048], P('fsdp', 'ctx', 'head'), may hold values from -6 to 6
- log_decay: float32 [4, 8192, 16], P('fsdp', 'ctx', 'head'), may hold values from -2 to 0, as said below
- out_grad: bfloat16 [4, 8192, 4096], P('fsdp', 'ctx', 'head'), may hold values from -6 to 6
- out_weight: float32 [4096, 2048], P(('ctx', 'fsdp'), 'head'), may hold values from -0.125 to 0.125
- moment_one: float32 [4096, 2048], P(('ctx', 'fsdp'), 'head'), may hold values from -2 to 2
- moment_two: float32 [4096, 2048], P(('ctx', 'fsdp'), 'head'), may hold values from 0.05 to 1
- group_ids: int32 [128], P(('ctx', 'fsdp')), may hold values from 0 to 2
- step_count: int32 [1], replicated, may hold values from 1 to 40
Outputs:
- query_grad: bfloat16 [4, 8192, 2048], P('fsdp', 'ctx', 'head')
- key_grad: bfloat16 [4, 8192, 2048], P('fsdp', 'ctx', 'head')
- value_grad: bfloat16 [4, 8192, 2048], P('fsdp', 'ctx', 'head')
- new_moment_one: float32 [4096, 2048], P(('ctx', 'fsdp'), 'head')
- new_moment_two: float32 [4096, 2048], P(('ctx', 'fsdp'), 'head')
- weight_step: float32 [4096, 2048], P(('ctx', 'fsdp'), 'head')
Inputs may be any that keep to these rules, and one draw needn't show every extreme that they name: `log_decay`: Log-decays per token and head, never positive. `group_ids`: 0 for a frozen block of rows, 1 for one updated without weight decay, 2 for one updated with it.
All inputs are finite; a program needn't handle non-finite values.
Results may differ from a plain program's by a relative error of at most 0.017.
Values may be sent and summed in bfloat16 or wider, within the bound.
No kernel may reach another device: no remote copies, remote signals or barrier semaphores. Data moves between devices by JAX's collectives and lax.ppermute only.
A program may use at most 128 MiB of HBM per device.

v0:
```python
import jax
import jax.numpy as jnp
from jax import lax
from jax.sharding import PartitionSpec as P

HEAD_DIM = 128
SPAN = 256
ROW_BLOCK = 32


NORM_EPS = 1e-06
BETA_ONE = 0.9
BETA_TWO = 0.95
ADAM_EPS = 1e-08
WEIGHT_DECAY = 0.1


def entering(array, axis, combine, identity):
    peers, place = (lax.axis_size(axis), lax.axis_index(axis))
    everything = jax.tree.map(lambda part: lax.all_gather(part, axis), array)
    start = jax.tree.map(
        lambda part, zero: jnp.broadcast_to(jnp.asarray(zero, part.dtype), part.shape),
        array,
        identity,
    )

    def hop(k, before):
        reached = k < place
        new = combine(before, jax.tree.map(lambda part: part[k], everything))
        return jax.tree.map(lambda a, b: jnp.where(reached, a, b), new, before)

    return lax.fori_loop(0, peers, hop, start)


def entering_2(array, axis, join, neutral):
    count = lax.axis_size(axis)
    place = lax.axis_index(axis)
    ahead = count - 1 - place
    gathered = jax.tree.map(
        lambda a, kind: lax.all_gather(a.astype(kind), axis), array, (jnp.bfloat16, jnp.bfloat16)
    )
    state = jax.tree.map(lambda a, e: jnp.zeros_like(a) + jnp.asarray(e, a.dtype), array, neutral)

    def one(hop, state):
        source = count - 1 - hop
        return join(
            state,
            jax.tree.map(
                lambda a, own: lax.dynamic_index_in_dim(a, source, 0, False).astype(own.dtype),
                gathered,
                array,
            ),
        )

    return lax.fori_loop(0, ahead, one, state)


def decay_mask(cumul):
    along = jnp.swapaxes(cumul, 1, 2)
    spread = along[:, :, :, None] - along[:, :, None, :]
    length = cumul.shape[1]
    lower = jnp.tril(jnp.ones((length, length), jnp.float32))
    return jnp.exp(jnp.minimum(spread, 0.0)) * lower


def forward_join(earlier, later):
    return (earlier[0] * later[0], later[0][:, None, None] * earlier[1] + later[1])


def backward_join(earlier, later):
    return (earlier[0] * later[0], later[1] + later[0][:, None, None] * earlier[1])


def per_device(
    queries,
    keys,
    values,
    gate_pre,
    log_decay,
    out_grad,
    out_weight,
    moment_one,
    moment_two,
    group_ids,
    step_count,
):
    tok_local = queries.shape[1]
    head_local = log_decay.shape[2]
    width_local = queries.shape[2]
    blocks = tok_local // SPAN
    shaped = (blocks, SPAN, head_local, HEAD_DIM)
    query_c = queries.reshape(shaped)
    key_c = keys.reshape(shaped)
    value_c = values.reshape(shaped)
    cumul = jnp.cumsum(log_decay.reshape(blocks, SPAN, head_local), axis=1)
    totals = cumul[:, -1, :]
    masking = decay_mask(cumul)
    decay_in = jnp.exp(cumul)[..., None]
    decay_out = jnp.exp(totals[:, None, :] - cumul)[..., None]
    scores = jnp.einsum("cthe,cuhe->chtu", query_c, key_c, preferred_element_type=jnp.float32)
    probs = (scores * masking).astype(jnp.bfloat16)
    intra = jnp.einsum("chtu,cuhe->cthe", probs, value_c, preferred_element_type=jnp.float32)
    scaled = (decay_out * key_c).astype(jnp.bfloat16)
    updates = jnp.einsum("cthe,cthf->chef", scaled, value_c, preferred_element_type=jnp.float32)
    running = jnp.zeros((head_local, HEAD_DIM, HEAD_DIM), jnp.float32)
    leading = jnp.zeros((head_local,), jnp.float32)
    start_list = []
    lead_list = []
    for block in range(blocks):
        start_list.append(running)
        lead_list.append(leading)
        running = jnp.exp(totals[block])[:, None, None] * running + updates[block]
        leading = leading + totals[block]
    local_start = jnp.stack(start_list)
    lead_sums = jnp.stack(lead_list)
    empty_state = jnp.zeros((head_local, HEAD_DIM, HEAD_DIM), jnp.float32)
    ones_gain = jnp.ones((head_local,), jnp.float32)
    _, incoming = entering(
        (jnp.exp(leading), running), "ctx", forward_join, (ones_gain, empty_state)
    )
    states = local_start + jnp.exp(lead_sums)[:, :, None, None] * incoming[None]
    rounded = states.astype(jnp.bfloat16)
    inter = decay_in * jnp.einsum(
        "cthe,chef->cthf", query_c, rounded, preferred_element_type=jnp.float32
    )
    attn = intra + inter
    square = jnp.mean(attn * attn, axis=-1, keepdims=True)
    inverse = lax.rsqrt(square + NORM_EPS)
    normed = attn * inverse
    silu_gate = jax.nn.silu(gate_pre.reshape(shaped).astype(jnp.float32))
    mixed = (normed * silu_gate).astype(jnp.bfloat16).reshape(tok_local, width_local)
    features = lax.all_gather(out_grad, "head", axis=2, tiled=True)[0]
    weight_b = out_weight.astype(jnp.bfloat16)
    columns = features
    mixed_grad = jnp.dot(
        columns,
        lax.all_gather(weight_b, ("ctx", "fsdp"), axis=0, tiled=True),
        preferred_element_type=jnp.float32,
    )
    columns = features
    grad_rows = lax.psum_scatter(
        jnp.einsum("td,th->dh", columns, mixed, preferred_element_type=jnp.float32),
        ("ctx", "fsdp"),
        scatter_dimension=0,
        tiled=True,
    )
    normed_grad = mixed_grad.reshape(shaped) * silu_gate
    inner = jnp.mean(normed_grad * normed, axis=-1, keepdims=True)
    attn_grad = (inverse * (normed_grad - normed * inner)).astype(jnp.bfloat16)
    inners = jnp.einsum("cthf,cuhf->chtu", attn_grad, value_c, preferred_element_type=jnp.float32)
    dprobs = (inners * masking).astype(jnp.bfloat16)
    qgrad = jnp.einsum("chtu,cuhe->cthe", dprobs, key_c, preferred_element_type=jnp.float32)
    kgrad = jnp.einsum("chtu,cthe->cuhe", dprobs, query_c, preferred_element_type=jnp.float32)
    vgrad = jnp.einsum("chtu,cthf->cuhf", probs, attn_grad, preferred_element_type=jnp.float32)
    weighted = (decay_in * query_c).astype(jnp.bfloat16)
    back_updates = jnp.einsum(
        "cthe,cthf->chef", weighted, attn_grad, preferred_element_type=jnp.float32
    )
    backing = jnp.zeros((head_local, HEAD_DIM, HEAD_DIM), jnp.float32)
    trailing = jnp.zeros((head_local,), jnp.float32)
    after_list = [None] * blocks
    trail_list = [None] * blocks
    for block in reversed(range(blocks)):
        after_list[block] = backing
        trail_list[block] = trailing
        backing = jnp.exp(totals[block])[:, None, None] * backing + back_updates[block]
        trailing = trailing + totals[block]
    local_after = jnp.stack(after_list)
    trail_sums = jnp.stack(trail_list)
    _, arriving = entering_2(
        (jnp.exp(leading), backing), "ctx", backward_join, (ones_gain, empty_state)
    )
    after_full = local_after + jnp.exp(trail_sums)[:, :, None, None] * arriving[None]
    back_b = after_full.astype(jnp.bfloat16)
    qgrad = qgrad + decay_in * jnp.einsum(
        "cthf,chef->cthe", attn_grad, rounded, preferred_element_type=jnp.float32
    )
    kgrad = kgrad + decay_out * jnp.einsum(
        "cuhf,chef->cuhe", value_c, back_b, preferred_element_type=jnp.float32
    )
    vgrad = vgrad + decay_out * jnp.einsum(
        "cuhe,chef->cuhf", key_c, back_b, preferred_element_type=jnp.float32
    )
    query_grad = qgrad.astype(jnp.bfloat16).reshape(1, tok_local, width_local)
    key_grad = kgrad.astype(jnp.bfloat16).reshape(1, tok_local, width_local)
    value_grad = vgrad.astype(jnp.bfloat16).reshape(1, tok_local, width_local)
    token_count = tok_local * lax.axis_size("ctx") * lax.axis_size("fsdp")
    grad = grad_rows / jnp.sqrt(jnp.float32(token_count))
    row_group = jnp.repeat(group_ids, ROW_BLOCK)[:, None]
    stepped = step_count[0].astype(jnp.float32)
    first = BETA_ONE * moment_one + (1.0 - BETA_ONE) * grad
    second = BETA_TWO * moment_two + (1.0 - BETA_TWO) * grad * grad
    correct_one = 1.0 - jnp.power(BETA_ONE, stepped)
    correct_two = 1.0 - jnp.power(BETA_TWO, stepped)
    active = row_group >= 1
    decayed = (row_group == 2).astype(jnp.float32)
    direction = (
        first / correct_one / (jnp.sqrt(second / correct_two) + ADAM_EPS)
        + WEIGHT_DECAY * decayed * out_weight
    )
    new_moment_one = jnp.where(active, first, moment_one)
    new_moment_two = jnp.where(active, second, moment_two)
    weight_step = jnp.where(active, direction, 0.0)
    return (query_grad, key_grad, value_grad, new_moment_one, new_moment_two, weight_step)


def solution(mesh):
    in_specs = (
        P("fsdp", "ctx", "head"),
        P("fsdp", "ctx", "head"),
        P("fsdp", "ctx", "head"),
        P("fsdp", "ctx", "head"),
        P("fsdp", "ctx", "head"),
        P("fsdp", "ctx", "head"),
        P(("ctx", "fsdp"), "head"),
        P(("ctx", "fsdp"), "head"),
        P(("ctx", "fsdp"), "head"),
        P(("ctx", "fsdp")),
        P(),
    )
    out_specs = (
        P("fsdp", "ctx", "head"),
        P("fsdp", "ctx", "head"),
        P("fsdp", "ctx", "head"),
        P(("ctx", "fsdp"), "head"),
        P(("ctx", "fsdp"), "head"),
        P(("ctx", "fsdp"), "head"),
    )
    return jax.shard_map(
        per_device, mesh=mesh, in_specs=in_specs, out_specs=out_specs, check_vma=False
    )
```

profile of v0, /device:TPU:2, one launch (start us, length us, event | category | flops | bytes accessed | tf_op | source)
XLA Modules:
  0.0 862.8 jit_solution(1575633204360036188)
XLA Ops:
  8.0 2.4 reduce-window.6
  20.6 2.3 reshape.204
  23.0 2.6 copy.210
  25.6 35.4 %all-gather = f32[16,1,4]{2,1,0:T(1,128)S(1)} all-gather(f32[1,1,4]{2,1,0:T(1,128)S(1)} %get-tuple-element.320), channel_id=1, replica_groups=mesh['ctx'=16,'fsdp'=4,'head'=4] {'ctx'}, dimensions={0}, use_global_device_ids=true | all-gather | bytes 272 | tf_op jit(solution)/shard_map/all_gather | solution.py:20
  61.0 33.5 %all-gather.7.cloned.1.call-done = f32[16,4,128,128]{3,2,1,0:T(8,128)} async-done(((f32[1,4,128,128]{3,2,1,0:T(8,128)}), f32[16,4,128,128]{3,2,1,0:T(8,128)}) %all-gather.7.cloned.1.call-update) | async-done | bytes 4194320 | tf_op jit(solution)/shard_map/all_gather | solution.py:20
  94.4 17.5 %while.29 = (s32[]{:T(128)}, f32[4,128,128]{2,1,0:T(8,128)S(1)}, s32[]{:T(128)}, f32[16,4]{1,0:T(8,128)S(1)}, f32[16,4,128,128]{3,2,1,0:T(8,128)}, /*index=5*/s32[]{:T(128)}, s32[]{:T(128)}) while((s32[]{:T(128)}, f32[4,128,128]{2,1,0:T(8,128)S(1)}, s32[]{:T(128)}, f32[16,4]{1,0:T(8,128)S(1)}, f32[16,4,128,128]{3,2,1,0:T(8,128)}, ...), condition=%wide.region_3.4_spmd.clone, body=%wide.region_2.3_spmd.clone.sunk | while | flops 262148 | bytes 786593 | solution.py:32
  112.0 1.4 multiply_reduce_fusion.1
  113.5 283.4 %all-gather.11.cloned.1.call-done = bf16[4096,512]{1,0:T(8,128)(2,1)} async-done(((bf16[64,512]{1,0:T(8,128)(2,1)}), bf16[4096,512]{1,0:T(8,128)(2,1)}) %all-gather.11.cloned.1.call-update) | async-done | bytes 4194320 | tf_op jit(solution)/shard_map/all_gather | solution.py:137
  396.9 6.5 copy.208
  403.4 34.0 %all-gather.9.cloned.1.call-done = bf16[1,512,4096]{2,1,0:T(8,128)(2,1)} async-done(((bf16[1,512,1024]{2,1,0:T(8,128)(2,1)}), bf16[1,512,4096]{2,1,0:T(8,128)(2,1)}) %all-gather.9.cloned.1.call-update) | async-done | bytes 4194320 | tf_op jit(solution)/shard_map/all_gather | solution.py:132
  437.4 6.3 multiply_reduce_fusion
  443.7 1.9 multiply_convert_fusion.2
  447.2 7.8 convolution_bitcast_fusion
  455.0 9.1 %copy.254 = f32[4096,512]{1,0:T(8,128)} copy(f32[4096,512]{0,1:T(8,128)} %convolution_bitcast_fusion) | data formatting | bytes 16777216
  465.0 33.9 %all-gather.1 = bf16[16,1,4]{2,1,0:T(2,128)(2,1)S(1)} all-gather(bf16[1,1,4]{2,1,0:T(2,128)(2,1)S(1)} %copy-done.25), channel_id=1, replica_groups=mesh['ctx'=16,'fsdp'=4,'head'=4] {'ctx'}, dimensions={0}, use_global_device_ids=true | all-gather | bytes 136 | tf_op jit(solution)/shard_map/all_gather | solution.py:40
  501.9 1.7 multiply_convert_fusion
  505.6 2.1 copy.216
  507.7 2.0 reshape.198
  509.8 1.6 convolution_bitcast_fusion.6
  511.3 1.7 convolution_bitcast_fusion.5
  513.1 4.8 all-gather.13.cloned.1.call-done
  517.8 7.4 while.28
  525.3 1.6 fusion.11
  530.1 322.5 %reduce-scatter.4.cloned.1.call-done = f32[64,512]{1,0:T(8,128)} async-done(((f32[4096,512]{1,0:T(8,128)}), f32[64,512]{1,0:T(8,128)}) %reduce-scatter.4.cloned.1.call-update) | async-done | bytes 131088
  (174 shorter events, 48.5 us)
Async XLA Ops:
  7.2 87.3 %all-gather.7.cloned.1.call-start = ((), (), s32[]{:S(2)}) async-start(), calls=%async_computation.1 | async-start | bytes 4456448 | tf_op jit(solution)/shard_map/all_gather | solution.py:20
  10.8 7.3 copy-start.15
  11.7 4.3 copy-start.19
  11.7 4.3 copy-start.21
  12.9 3.2 copy-start.10
  14.2 3.5 copy-start.11
  16.1 95.9 %copy-start.3 = (f32[1,4,128,128]{3,2,1,0:T(8,128)}, f32[1,4,128,128]{3,2,1,0:T(8,128)S(1)}, u32[]{:S(2)}) copy-start(f32[1,4,128,128]{3,2,1,0:T(8,128)S(1)} %get-tuple-element.311) | copy-start | bytes 786436
  16.1 380.8 %all-gather.11.cloned.1.call-start = ((), (), s32[]{:S(2)}) async-start(), calls=%async_computation.3 | async-start | bytes 4259840 | tf_op jit(solution)/shard_map/all_gather | solution.py:137
  16.9 420.5 %all-gather.9.cloned.1.call-start = ((), (), s32[]{:S(2)}) async-start(), calls=%async_computation.2 | async-start | bytes 5242880 | tf_op jit(solution)/shard_map/all_gather | solution.py:132
  17.6 500.2 %all-gather.13.cloned.1.call-start = ((), (), s32[]{:S(2)}) async-start(), calls=%async_computation.4 | async-start | bytes 2228224 | tf_op jit(solution)/shard_map/all_gather | solution.py:40
  19.3 41.6 %copy-start.27 = (f32[4]{0:T(128)S(1)}, f32[4]{0:T(128)}, u32[]{:S(2)}) copy-start(f32[4]{0:T(128)} %get-tuple-element.286) | copy-start | bytes 52
  61.0 52.5 %copy-start.17 = (f32[2,4]{1,0:T(2,128)}, f32[2,4]{1,0:T(2,128)S(1)}, u32[]{:S(2)}) copy-start(f32[2,4]{1,0:T(2,128)S(1)} %pad_exponential_fusion.1) | copy-start | bytes 100
  113.4 323.9 %copy-start.16 = (f32[2,256,4]{1,2,0:T(4,128)}, f32[2,256,4]{1,2,0:T(4,128)S(1)}, u32[]{:S(2)}) copy-start(f32[2,256,4]{1,2,0:T(4,128)S(1)} %add_rsqrt_fusion) | copy-start | bytes 24580
  396.9 40.5 %copy-start.1 = (f32[2,256,4,128]{1,3,2,0:T(8,128)S(1)}, f32[2,256,4,128]{1,3,2,0:T(8,128)}, u32[]{:S(2)}) copy-start(f32[2,256,4,128]{1,3,2,0:T(8,128)} %copy.210) | copy-start | bytes 3145732
  437.4 6.3 copy-start.2
  446.9 405.8 %reduce-scatter.4.cloned.1.call-start = ((), (), s32[]{:S(2)}) async-start(), calls=%async_computation.5 | async-start | bytes 8519680
  464.1 35.0 %copy-start.13 = (f32[64,512]{1,0:T(8,128)S(1)}, f32[64,512]{1,0:T(8,128)}, u32[]{:S(2)}) copy-start(f32[64,512]{1,0:T(8,128)} %param.22) | copy-start | bytes 393220
  464.1 35.8 %copy-start.14 = (f32[64,512]{1,0:T(8,128)S(1)}, f32[64,512]{1,0:T(8,128)}, u32[]{:S(2)}) copy-start(f32[64,512]{1,0:T(8,128)} %param.23) | copy-start | bytes 393220
  464.1 36.7 %copy-start.29 = (s32[2]{0:T(128)S(1)}, s32[2]{0:T(128)}, u32[]{:S(2)}) copy-start(s32[2]{0:T(128)} %param.24) | copy-start | bytes 28
  464.1 37.8 %copy-start.24 = (f32[4]{0:T(128)S(1)}, f32[4]{0:T(128)}, u32[]{:S(2)}) copy-start(f32[4]{0:T(128)} %get-tuple-element.285) | copy-start | bytes 52
  513.0 12.2 %copy-start.5 = (f32[1,4,128,128]{3,2,1,0:T(8,128)S(1)}, f32[1,4,128,128]{3,2,1,0:T(8,128)}, u32[]{:S(2)}) copy-start(f32[1,4,128,128]{3,2,1,0:T(8,128)} %get-tuple-element.309) | copy-start | bytes 786436
  528.3 325.3 %copy-start.7 = (f32[64,512]{0,1:T(8,128)S(1)}, f32[64,512]{0,1:T(8,128)}, u32[]{:S(2)}) copy-start(f32[64,512]{0,1:T(8,128)} %copy.236) | copy-start | bytes 393220
  528.3 325.3 %copy-start.8 = (f32[64,512]{0,1:T(8,128)S(1)}, f32[64,512]{0,1:T(8,128)}, u32[]{:S(2)}) copy-start(f32[64,512]{0,1:T(8,128)} %copy.231) | copy-start | bytes 393220
  528.3 325.4 %copy-start.9 = (f32[64,512]{0,1:T(8,128)S(1)}, f32[64,512]{0,1:T(8,128)}, u32[]{:S(2)}) copy-start(f32[64,512]{0,1:T(8,128)} %copy.234) | copy-start | bytes 393220
  (11 other events, 13.5 us)
Sparse Core Ops, SparseCore 0:
  16.2 78.1 all-gather.6
  96.8 300.0 all-gather.10
  398.7 38.6 all-gather.8
  447.0 70.7 all-gather.12
  520.2 332.3 reduce-scatter.3
where the time goes:
time: 865 us; the launch traced here: 863 us
  waiting for transfers between devices  679 us (78%)
  blocking collectives  69.3 us (8%)
  local copies, waits for them, and re-layouts  39.7 us (5%)
  other arithmetic  32.3 us (4%)
  matrix products  26.6 us (3%)
  between operations  15 us (2%)
    unnamed x6, waiting for transfers between devices  323 us
    all_gather x1, waiting for transfers between devices, per_device(): lax.all_gather(weight_b, ('ctx', 'fsdp'), axis=0, tiled=True)  283 us
    all_gather x1, blocking collectives, entering(): everything = jax.tree.map(lambda part: lax.all_gather(part, axis), array)  35.4 us
    all_gather x1, waiting for transfers between devices, per_device(): features = lax.all_gather(out_grad, 'head', axis=2, tiled=True)[0]  34 us
    all_gather x1, blocking collectives, entering_2(): lax.all_gather(a.astype(kind), axis)  33.9 us
    all_gather x1, waiting for transfers between devices, entering(): everything = jax.tree.map(lambda part: lax.all_gather(part, axis), array)  33.5 us
  transfers between devices with their start and end apart: 5, of which 5 were waited for; matrix products, arithmetic and copies ran while one was open for 9% of the time, Pallas kernels for 0%

commit v1 on v0

--- a/solution.py
+++ b/solution.py
@@ -15,44 +15,38 @@
 WEIGHT_DECAY = 0.1
 
 
-def entering(array, axis, combine, identity):
-    peers, place = (lax.axis_size(axis), lax.axis_index(axis))
-    everything = jax.tree.map(lambda part: lax.all_gather(part, axis), array)
-    start = jax.tree.map(
-        lambda part, zero: jnp.broadcast_to(jnp.asarray(zero, part.dtype), part.shape),
-        array,
-        identity,
-    )
-
-    def hop(k, before):
-        reached = k < place
-        new = combine(before, jax.tree.map(lambda part: part[k], everything))
-        return jax.tree.map(lambda a, b: jnp.where(reached, a, b), new, before)
-
-    return lax.fori_loop(0, peers, hop, start)
-
-
-def entering_2(array, axis, join, neutral):
+def prefix_scan(gain, state, axis):
     count = lax.axis_size(axis)
     place = lax.axis_index(axis)
-    ahead = count - 1 - place
-    gathered = jax.tree.map(
-        lambda a, kind: lax.all_gather(a.astype(kind), axis), array, (jnp.bfloat16, jnp.bfloat16)
-    )
-    state = jax.tree.map(lambda a, e: jnp.zeros_like(a) + jnp.asarray(e, a.dtype), array, neutral)
-
-    def one(hop, state):
-        source = count - 1 - hop
-        return join(
-            state,
-            jax.tree.map(
-                lambda a, own: lax.dynamic_index_in_dim(a, source, 0, False).astype(own.dtype),
-                gathered,
-                array,
-            ),
+    gain, state = lax.ppermute((gain, state), axis, [(i, i + 1) for i in range(count - 1)])
+    gain = jnp.where(place >= 1, gain, 1.0)
+    step = 1
+    while step < count:
+        got_gain, got_state = lax.ppermute(
+            (gain, state), axis, [(i, i + step) for i in range(count - step)]
         )
-
-    return lax.fori_loop(0, ahead, one, state)
+        reached = place >= step
+        state = jnp.where(reached, gain[:, None, None] * got_state + state, state)
+        gain = jnp.where(reached, got_gain * gain, gain)
+        step *= 2
+    return state
+
+
+def suffix_scan(gain, state, axis):
+    count = lax.axis_size(axis)
+    place = lax.axis_index(axis)
+    gain, state = lax.ppermute((gain, state), axis, [(i + 1, i) for i in range(count - 1)])
+    gain = jnp.where(place <= count - 2, gain, 1.0)
+    step = 1
+    while step < count:
+        got_gain, got_state = lax.ppermute(
+            (gain, state), axis, [(i + step, i) for i in range(count - step)]
+        )
+        reached = place + step <= count - 1
+        state = jnp.where(reached, state + gain[:, None, None] * got_state, state)
+        gain = jnp.where(reached, gain * got_gain, gain)
+        step *= 2
+    return state
 
 
 def decay_mask(cumul):
@@ -61,14 +55,6 @@
     length = cumul.shape[1]
     lower = jnp.tril(jnp.ones((length, length), jnp.float32))
     return jnp.exp(jnp.minimum(spread, 0.0)) * lower
-
-
-def forward_join(earlier, later):
-    return (earlier[0] * later[0], later[0][:, None, None] * earlier[1] + later[1])
-
-
-def backward_join(earlier, later):
-    return (earlier[0] * later[0], later[1] + later[0][:, None, None] * earlier[1])
 
 
 def per_device(
@@ -113,11 +99,7 @@
         leading = leading + totals[block]
     local_start = jnp.stack(start_list)
     lead_sums = jnp.stack(lead_list)
-    empty_state = jnp.zeros((head_local, HEAD_DIM, HEAD_DIM), jnp.float32)
-    ones_gain = jnp.ones((head_local,), jnp.float32)
-    _, incoming = entering(
-        (jnp.exp(leading), running), "ctx", forward_join, (ones_gain, empty_state)
-    )
+    incoming = prefix_scan(jnp.exp(leading), running, "ctx")
     states = local_start + jnp.exp(lead_sums)[:, :, None, None] * incoming[None]
     rounded = states.astype(jnp.bfloat16)
     inter = decay_in * jnp.einsum(
@@ -134,13 +116,20 @@
     columns = features
     mixed_grad = jnp.dot(
         columns,
-        lax.all_gather(weight_b, ("ctx", "fsdp"), axis=0, tiled=True),
+        lax.all_gather(
+            lax.all_gather(weight_b, "fsdp", axis=0, tiled=True), "ctx", axis=0, tiled=True
+        ),
         preferred_element_type=jnp.float32,
     )
     columns = features
     grad_rows = lax.psum_scatter(
-        jnp.einsum("td,th->dh", columns, mixed, preferred_element_type=jnp.float32),
-        ("ctx", "fsdp"),
+        lax.psum_scatter(
+            jnp.einsum("td,th->dh", columns, mixed, preferred_element_type=jnp.float32),
+            "ctx",
+            scatter_dimension=0,
+            tiled=True,
+        ),
+        "fsdp",
         scatter_dimension=0,
         tiled=True,
     )
@@ -167,9 +156,7 @@
         trailing = trailing + totals[block]
     local_after = jnp.stack(after_list)
     trail_sums = jnp.stack(trail_list)
-    _, arriving = entering_2(
-        (jnp.exp(leading), backing), "ctx", backward_join, (ones_gain, empty_state)
-    )
+    arriving = suffix_scan(jnp.exp(leading), backing, "ctx")
     after_full = local_after + jnp.exp(trail_sums)[:, :, None, None] * arriving[None]
     back_b = after_full.astype(jnp.bfloat16)
     qgrad = qgrad + decay_in * jnp.einsum(

time: 865 us -> 344 us (0.40)
  waiting for transfers between devices: 679 us -> 164 us
  starting transfers between devices: 0.2 us -> 82.1 us
  blocking collectives: 69.3 us -> 13.5 us
  other arithmetic: 32.3 us -> 13.7 us
  local copies, waits for them, and re-layouts: 39.7 us -> 29.1 us
    all_gather x3 -> x1, waiting for transfers between devices: 322 us -> 0.02 us  [per_device(): lax.all_gather(lax.all_gather(weight_b, 'fsdp', axis=0, tiled=True), 'ctx...]
    unnamed x6 -> x5, waiting for transfers between devices: 323 us -> 19.9 us
    ppermute x0 -> x18, waiting for transfers between devices: none -> 109 us  [the longest x7 49.8 us: suffix_scan(): lax.ppermute((gain, state), axis, [(i + step, i) for i in range(count - s...]
    ppermute x0 -> x18, starting transfers between devices: none -> 82 us  [the longest x7 30.1 us: suffix_scan(): lax.ppermute((gain, state), axis, [(i + step, i) for i in range(count - s...]
    all_gather x2 -> x1, blocking collectives: 69.3 us -> 13.5 us  [per_device(): lax.all_gather(weight_b, 'fsdp', axis=0, tiled=True)]
    reduce_scatter x0 -> x1, waiting for transfers between devices: none -> 15.6 us  [per_device(): lax.psum_scatter(jnp.einsum('td,th->dh', columns, mixed, preferred_elemen...]
    all_gather x1, waiting for transfers between devices: 34 us -> 19.5 us  [per_device(): features = lax.all_gather(out_grad, 'head', axis=2, tiled=True)[0]]
    select_n x16, other arithmetic: 16.9 us -> 7.28 us  [the longest x4 5.09 us: prefix_scan(): state = jnp.where(reached, gain[:, None, None] * got_state + state, state)]
  transfers between devices with their start and end apart: 5 -> 22, of which waited for: 5 -> 16; matrix products, arithmetic and copies ran while one was open for 9% -> 13% of each run, Pallas kernels for 0% -> 0%
where the time goes in v1:
time: 344 us; the launch traced here: 343 us
  waiting for transfers between devices  164 us (48%)
  starting transfers between devices  82.1 us (24%)
  local copies, waits for them, and re-layouts  29.1 us (8%)
  matrix products  25.5 us (7%)
  between operations  15.2 us (4%)
  other arithmetic  13.7 us (4%)
  blocking collectives  13.5 us (4%)
    ppermute x7, waiting for transfers between devices, suffix_scan(): lax.ppermute((gain, state), axis, [(i + step, i) for i in range(count - s...  49.8 us
    ppermute x7, waiting for transfers between devices, prefix_scan(): lax.ppermute((gain, state), axis, [(i, i + step) for i in range(count - s...  42 us
    ppermute x7, starting transfers between devices, suffix_scan(): lax.ppermute((gain, state), axis, [(i + step, i) for i in range(count - s...  30.1 us
    ppermute x7, starting transfers between devices, prefix_scan(): lax.ppermute((gain, state), axis, [(i, i + step) for i in range(count - s...  29 us
    unnamed x5, waiting for transfers between devices  19.9 us
    all_gather x1, waiting for transfers between devices, per_device(): features = lax.all_gather(out_grad, 'head', axis=2, tiled=True)[0]  19.5 us
    reduce_scatter x1, waiting for transfers between devices, per_device(): lax.psum_scatter(jnp.einsum('td,th->dh', columns, mixed, preferred_elemen...  15.6 us
    ppermute x2, starting transfers between devices, suffix_scan(): lax.ppermute((gain, state), axis, [(i + 1, i) for i in range(count - 1)])  15.2 us
  transfers between devices with their start and end apart: 22, of which 16 were waited for; matrix products, arithmetic and copies ran while one was open for 13% of the time, Pallas kernels for 0%

profile of v1, /device:TPU:2, one launch (start us, length us, event | category | flops | bytes accessed | tf_op | source)
XLA Modules:
  0.0 343.1 jit_solution(14694287635345457942)
XLA Ops:
  8.2 13.5 %all_gather.10 = bf16[256,512]{1,0:T(8,128)(2,1)} all-gather(bf16[64,512]{1,0:T(8,128)(2,1)S(1)} %convert_element_type.57), channel_id=1, replica_groups=mesh['ctx'=16,'fsdp'=4,'head'=4] {'fsdp'}, dimensions={0}, use_global_device_ids=true | all-gather | bytes 327680 | tf_op jit(solution)/shard_map/all_gather | solution.py:120
  36.9 8.1 %collective-permute-done.4 = f32[4,128,128]{2,1,0:T(8,128)S(1)} collective-permute-done((f32[4,128,128]{2,1,0:T(8,128)}, f32[4,128,128]{2,1,0:T(8,128)S(1)}, u32[]{:S(2)}, u32[]{:S(2)}) %collective-permute-start.4) | collective-permute-done | bytes 262176 | tf_op jit(solution)/shard_map/ppermute | solution.py:21
  47.7 14.9 %collective-permute-done.5 = f32[4,128,128]{2,1,0:T(8,128)} collective-permute-done((f32[4,128,128]{2,1,0:T(8,128)S(1)}, f32[4,128,128]{2,1,0:T(8,128)}, u32[]{:S(2)}, u32[]{:S(2)}) %collective-permute-start.5) | collective-permute-done | bytes 262176 | tf_op jit(solution)/shard_map/ppermute | solution.py:25
  67.1 6.6 %collective-permute-start.1 = (f32[4]{0:T(128)S(1)}, f32[4]{0:T(128)S(1)}, u32[]{:S(2)}, u32[]{:S(2)}) collective-permute-start(f32[4]{0:T(128)S(1)} %broadcast_select_fusion.5), channel_id=1, source_target_pairs={{0,16},{16,32},{32,48},{48,64},{64,80},{80,96},{96,112},{112,128},... | collective-permute-start | bytes 56 | tf_op jit(solution)/shard_map/ppermute | solution.py:25
  73.7 7.4 %collective-permute-done.1 = f32[4]{0:T(128)S(1)} collective-permute-done((f32[4]{0:T(128)S(1)}, f32[4]{0:T(128)S(1)}, u32[]{:S(2)}, u32[]{:S(2)}) %collective-permute-start.1) | collective-permute-done | bytes 48 | tf_op jit(solution)/shard_map/ppermute | solution.py:25
  86.6 11.2 %collective-permute-start.7 = (f32[4,128,128]{2,1,0:T(8,128)}, f32[4,128,128]{2,1,0:T(8,128)}, u32[]{:S(2)}, u32[]{:S(2)}) collective-permute-start(f32[4,128,128]{2,1,0:T(8,128)} %add_select_fusion.6), channel_id=1, source_target_pairs={{0,64},{16,80},{32,96},{48,112},{64,128},{80,144},{96,160},{112,17... | collective-permute-start | bytes 786440 | tf_op jit(solution)/shard_map/ppermute | solution.py:25
  99.8 10.0 %collective-permute-done.2 = f32[4]{0:T(128)S(1)} collective-permute-done((f32[4]{0:T(128)S(1)}, f32[4]{0:T(128)S(1)}, u32[]{:S(2)}, u32[]{:S(2)}) %collective-permute-start.2) | collective-permute-done | bytes 48 | tf_op jit(solution)/shard_map/ppermute | solution.py:25
  121.5 6.0 %collective-permute-done.3 = f32[4]{0:T(128)S(1)} collective-permute-done((f32[4]{0:T(128)S(1)}, f32[4]{0:T(128)S(1)}, u32[]{:S(2)}, u32[]{:S(2)}) %collective-permute-start.3) | collective-permute-done | bytes 48 | tf_op jit(solution)/shard_map/ppermute | solution.py:25
  130.2 6.8 %copy.190 = bf16[512,4096]{1,0:T(8,128)(2,1)} copy(bf16[512,4096]{0,1:T(8,128)(2,1)} %bitcast.105) | data formatting | bytes 8388608 | tf_op jit(solution)/shard_map/dot_general | solution.py:117
  137.0 19.5 %all-gather.3.cloned.1.call-done = bf16[1,512,4096]{2,1,0:T(8,128)(2,1)} async-done(((bf16[1,512,1024]{2,1,0:T(8,128)(2,1)}), bf16[1,512,4096]{2,1,0:T(8,128)(2,1)}) %all-gather.3.cloned.1.call-update) | async-done | bytes 4194320 | tf_op jit(solution)/shard_map/all_gather | solution.py:114
  156.4 6.3 %multiply_reduce_fusion = (f32[2,256,4]{1,2,0:T(4,128)S(1)}, f32[2,256,4,128]{1,3,2,0:T(8,128)S(1)}) fusion(f32[2,256,4,128]{1,3,2,0:T(8,128)} %get-tuple-element.49, f32[2,256,4]{1,2,0:T(4,128)S(1)} %add_rsqrt_fusion, f32[2,256,4,128]{1,3,2,0:T(8,128)S(1)} %copy-done.3, bf16[2,256,4096,1]{2,1,3,0:T(8,128)(2,1)} %bitcast.104, ...), kind=kOutput, calls=%fused_computation.28 | convolution fusion | flops 2149578752 | bytes 11550720 | tf_op jit(solution)/shard_map/dot_general | solution.py:117
  165.3 7.8 %convolution_bitcast_fusion = f32[4096,512]{0,1:T(8,128)} fusion(bf16[1,512,4096]{2,1,0:T(8,128)(2,1)} %all-gather.3.cloned.1.call-done, bf16[64,8,4,128]{3,2,1,0:T(4,128)(2,1)S(1)} %bitcast.107), kind=kOutput, calls=%fused_computation | convolution fusion | flops 2147483648 | bytes 13107200 | tf_op jit(solution)/shard_map/td,th->dh/dot_general | solution.py:127
  173.2 6.2 %collective-permute-start.10 = (f32[4]{0:T(128)S(1)}, f32[4]{0:T(128)S(1)}, u32[]{:S(2)}, u32[]{:S(2)}) collective-permute-start(f32[4]{0:T(128)S(1)} %get-tuple-element.37), channel_id=1, source_target_pairs={{16,0},{32,16},{48,32},{64,48},{80,64},{96,80},{112,96},{128,112},... | collective-permute-start | bytes 56 | tf_op jit(solution)/shard_map/ppermute | solution.py:38
  195.1 4.7 %collective-permute-start.16 = (f32[4]{0:T(128)S(1)}, f32[4]{0:T(128)S(1)}, u32[]{:S(2)}, u32[]{:S(2)}) collective-permute-start(f32[4]{0:T(128)S(1)} %broadcast_select_fusion.1), channel_id=1, source_target_pairs={{64,0},{80,16},{96,32},{112,48},{128,64},{144,80},{160,96},{176,11... | collective-permute-start | bytes 56 | tf_op jit(solution)/shard_map/ppermute | solution.py:42
  199.9 4.8 %collective-permute-done.16 = f32[4]{0:T(128)S(1)} collective-permute-done((f32[4]{0:T(128)S(1)}, f32[4]{0:T(128)S(1)}, u32[]{:S(2)}, u32[]{:S(2)}) %collective-permute-start.16) | collective-permute-done | bytes 48 | tf_op jit(solution)/shard_map/ppermute | solution.py:42
  205.7 9.0 %collective-permute-start.9 = (f32[4,128,128]{2,1,0:T(8,128)S(1)}, f32[4,128,128]{2,1,0:T(8,128)S(1)}, u32[]{:S(2)}, u32[]{:S(2)}) collective-permute-start(f32[4,128,128]{2,1,0:T(8,128)S(1)} %fusion.26), channel_id=1, source_target_pairs={{16,0},{32,16},{48,32},{64,48},{80,64},{96,80},{112,96},{128,112},... | collective-permute-start | bytes 786440 | tf_op jit(solution)/shard_map/ppermute | solution.py:38
  216.4 9.1 %collective-permute-done.9 = f32[4,128,128]{2,1,0:T(8,128)S(1)} collective-permute-done((f32[4,128,128]{2,1,0:T(8,128)S(1)}, f32[4,128,128]{2,1,0:T(8,128)S(1)}, u32[]{:S(2)}, u32[]{:S(2)}) %collective-permute-start.9) | collective-permute-done | bytes 262176 | tf_op jit(solution)/shard_map/ppermute | solution.py:38
  225.5 6.7 %collective-permute-start.11 = (f32[4,128,128]{2,1,0:T(8,128)S(1)}, f32[4,128,128]{2,1,0:T(8,128)S(1)}, u32[]{:S(2)}, u32[]{:S(2)}) collective-permute-start(f32[4,128,128]{2,1,0:T(8,128)S(1)} %collective-permute-done.9), channel_id=1, source_target_pairs={{16,0},{32,16},{48,32},{64,48},{80,64},{96,80},{112,96},{128,112},... | collective-permute-start | bytes 786440 | tf_op jit(solution)/shard_map/ppermute | solution.py:42
  232.9 9.8 %collective-permute-done.11 = f32[4,128,128]{2,1,0:T(8,128)S(1)} collective-permute-done((f32[4,128,128]{2,1,0:T(8,128)S(1)}, f32[4,128,128]{2,1,0:T(8,128)S(1)}, u32[]{:S(2)}, u32[]{:S(2)}) %collective-permute-start.11) | collective-permute-done | bytes 262176 | tf_op jit(solution)/shard_map/ppermute | solution.py:42
  248.2 13.9 %collective-permute-done.13 = f32[4,128,128]{2,1,0:T(8,128)S(1)} collective-permute-done((f32[4,128,128]{2,1,0:T(8,128)S(1)}, f32[4,128,128]{2,1,0:T(8,128)S(1)}, u32[]{:S(2)}, u32[]{:S(2)}) %collective-permute-start.13) | collective-permute-done | bytes 262176 | tf_op jit(solution)/shard_map/ppermute | solution.py:42
  262.1 5.0 %collective-permute-start.15 = (f32[4,128,128]{2,1,0:T(8,128)S(1)}, f32[4,128,128]{2,1,0:T(8,128)S(1)}, u32[]{:S(2)}, u32[]{:S(2)}) collective-permute-start(f32[4,128,128]{2,1,0:T(8,128)S(1)} %add_select_fusion.2), channel_id=1, source_target_pairs={{64,0},{80,16},{96,32},{112,48},{128,64},{144,80},{160,96},{176,11... | collective-permute-start | bytes 786440 | tf_op jit(solution)/shard_map/ppermute | solution.py:42
  267.7 17.2 %collective-permute-done.15 = f32[4,128,128]{2,1,0:T(8,128)S(1)} collective-permute-done((f32[4,128,128]{2,1,0:T(8,128)S(1)}, f32[4,128,128]{2,1,0:T(8,128)S(1)}, u32[]{:S(2)}, u32[]{:S(2)}) %collective-permute-start.15) | collective-permute-done | bytes 262176 | tf_op jit(solution)/shard_map/ppermute | solution.py:42
  291.2 15.6 %reduce-scatter.5.cloned.1.call-done = f32[256,512]{0,1:T(8,128)} async-done(((f32[4096,512]{0,1:T(8,128)}), f32[256,512]{0,1:T(8,128)}) %reduce-scatter.5.cloned.1.call-update) | async-done | bytes 524304 | tf_op jit(solution)/shard_map/reduce_scatter | solution.py:126
  313.8 19.2 %reduce-scatter.7.cloned.1.call-done = f32[64,512]{1,0:T(8,128)} async-done(((f32[256,512]{1,0:T(8,128)}), f32[64,512]{1,0:T(8,128)}) %reduce-scatter.7.cloned.1.call-update) | async-done | bytes 131088
  (155 shorter events, 88.7 us)
Async XLA Ops:
  7.2 122.9 %all-gather.5.cloned.1.call-start = ((), (), s32[]{:S(2)}) async-start(), calls=%async_computation.3 | async-start | bytes 4456448 | tf_op jit(solution)/shard_map/all_gather | solution.py:119
  21.8 134.7 %all-gather.3.cloned.1.call-start = ((), (), s32[]{:S(2)}) async-start(), calls=%async_computation.2 | async-start | bytes 5242880 | tf_op jit(solution)/shard_map/all_gather | solution.py:114
  22.5 284.3 %reduce-scatter.5.cloned.1.call-start = ((), (), s32[]{:S(2)}) async-start(), calls=%async_computation.4 | async-start | bytes 8912896 | tf_op jit(solution)/shard_map/reduce_scatter | solution.py:126
  28.8 16.2 %collective-permute-start.4 = (f32[4,128,128]{2,1,0:T(8,128)}, f32[4,128,128]{2,1,0:T(8,128)S(1)}, u32[]{:S(2)}, u32[]{:S(2)}) collective-permute-start(f32[4,128,128]{2,1,0:T(8,128)} %fusion.27), channel_id=1, source_target_pairs={{0,16},{16,32},{32,48},{48,64},{64,80},{80,96},{96,112},{112,128},... | collective-permute-start | bytes 786440 | tf_op jit(solution)/shard_map/ppermute | solution.py:21
  32.6 15.1 %collective-permute-start = (f32[4]{0:T(128)S(1)}, f32[4]{0:T(128)S(1)}, u32[]{:S(2)}, u32[]{:S(2)}) collective-permute-start(f32[4]{0:T(128)S(1)} %get-tuple-element.37), channel_id=1, source_target_pairs={{0,16},{16,32},{32,48},{48,64},{64,80},{80,96},{96,112},{112,128},... | collective-permute-start | bytes 56 | tf_op jit(solution)/shard_map/ppermute | solution.py:21
  45.0 17.6 %collective-permute-start.5 = (f32[4,128,128]{2,1,0:T(8,128)S(1)}, f32[4,128,128]{2,1,0:T(8,128)}, u32[]{:S(2)}, u32[]{:S(2)}) collective-permute-start(f32[4,128,128]{2,1,0:T(8,128)S(1)} %collective-permute-done.4), channel_id=1, source_target_pairs={{0,16},{16,32},{32,48},{48,64},{64,80},{80,96},{96,112},{112,128},... | collective-permute-start | bytes 786440 | tf_op jit(solution)/shard_map/ppermute | solution.py:25
  47.7 38.9 %copy-start.1 = (bf16[2,4,256,256]{3,2,1,0:T(8,128)(2,1)}, bf16[2,4,256,256]{3,2,1,0:T(8,128)(2,1)S(1)}, u32[]{:S(2)}) copy-start(bf16[2,4,256,256]{3,2,1,0:T(8,128)(2,1)S(1)} %multiply_convert_fusion.1) | copy-start | bytes 3145732
  63.7 21.1 %collective-permute-start.6 = (f32[4,128,128]{2,1,0:T(8,128)S(1)}, f32[4,128,128]{2,1,0:T(8,128)}, u32[]{:S(2)}, u32[]{:S(2)}) collective-permute-start(f32[4,128,128]{2,1,0:T(8,128)S(1)} %add_select_fusion.7), channel_id=1, source_target_pairs={{0,32},{16,48},{32,64},{48,80},{64,96},{80,112},{96,128},{112,144}... | collective-permute-start | bytes 786440 | tf_op jit(solution)/shard_map/ppermute | solution.py:25
  67.1 13.9 %collective-permute-start.1 = (f32[4]{0:T(128)S(1)}, f32[4]{0:T(128)S(1)}, u32[]{:S(2)}, u32[]{:S(2)}) collective-permute-start(f32[4]{0:T(128)S(1)} %broadcast_select_fusion.5), channel_id=1, source_target_pairs={{0,16},{16,32},{32,48},{48,64},{64,80},{80,96},{96,112},{112,128},... | collective-permute-start | bytes 56 | tf_op jit(solution)/shard_map/ppermute | solution.py:25
  86.6 23.3 %collective-permute-start.7 = (f32[4,128,128]{2,1,0:T(8,128)}, f32[4,128,128]{2,1,0:T(8,128)}, u32[]{:S(2)}, u32[]{:S(2)}) collective-permute-start(f32[4,128,128]{2,1,0:T(8,128)} %add_select_fusion.6), channel_id=1, source_target_pairs={{0,64},{16,80},{32,96},{48,112},{64,128},{80,144},{96,160},{112,17... | collective-permute-start | bytes 786440 | tf_op jit(solution)/shard_map/ppermute | solution.py:25
  97.9 11.9 %collective-permute-start.2 = (f32[4]{0:T(128)S(1)}, f32[4]{0:T(128)S(1)}, u32[]{:S(2)}, u32[]{:S(2)}) collective-permute-start(f32[4]{0:T(128)S(1)} %broadcast_select_fusion.4), channel_id=1, source_target_pairs={{0,32},{16,48},{32,64},{48,80},{64,96},{80,112},{96,128},{112,144}... | collective-permute-start | bytes 56 | tf_op jit(solution)/shard_map/ppermute | solution.py:25
  111.0 16.6 %collective-permute-start.8 = (f32[4,128,128]{2,1,0:T(8,128)S(1)}, f32[4,128,128]{2,1,0:T(8,128)}, u32[]{:S(2)}, u32[]{:S(2)}) collective-permute-start(f32[4,128,128]{2,1,0:T(8,128)S(1)} %add_select_fusion.5), channel_id=1, source_target_pairs={{0,128},{16,144},{32,160},{48,176},{64,192},{80,208},{96,224},{112... | collective-permute-start | bytes 786440 | tf_op jit(solution)/shard_map/ppermute | solution.py:25
  117.3 10.3 %collective-permute-start.3 = (f32[4]{0:T(128)S(1)}, f32[4]{0:T(128)S(1)}, u32[]{:S(2)}, u32[]{:S(2)}) collective-permute-start(f32[4]{0:T(128)S(1)} %broadcast_select_fusion.6), channel_id=1, source_target_pairs={{0,64},{16,80},{32,96},{48,112},{64,128},{80,144},{96,160},{112,17... | collective-permute-start | bytes 56 | tf_op jit(solution)/shard_map/ppermute | solution.py:25
  173.2 159.8 %reduce-scatter.7.cloned.1.call-start = ((), (), s32[]{:S(2)}) async-start(), calls=%async_computation.5 | async-start | bytes 655360
  173.2 9.8 %collective-permute-start.10 = (f32[4]{0:T(128)S(1)}, f32[4]{0:T(128)S(1)}, u32[]{:S(2)}, u32[]{:S(2)}) collective-permute-start(f32[4]{0:T(128)S(1)} %get-tuple-element.37), channel_id=1, source_target_pairs={{16,0},{32,16},{48,32},{64,48},{80,64},{96,80},{112,96},{128,112},... | collective-permute-start | bytes 56 | tf_op jit(solution)/shard_map/ppermute | solution.py:38
  183.1 5.5 %collective-permute-start.12 = (f32[4]{0:T(128)S(1)}, f32[4]{0:T(128)S(1)}, u32[]{:S(2)}, u32[]{:S(2)}) collective-permute-start(f32[4]{0:T(128)S(1)} %broadcast_select_fusion.3), channel_id=1, source_target_pairs={{16,0},{32,16},{48,32},{64,48},{80,64},{96,80},{112,96},{128,112},... | collective-permute-start | bytes 56 | tf_op jit(solution)/shard_map/ppermute | solution.py:42
  188.6 6.5 %collective-permute-start.14 = (f32[4]{0:T(128)S(1)}, f32[4]{0:T(128)S(1)}, u32[]{:S(2)}, u32[]{:S(2)}) collective-permute-start(f32[4]{0:T(128)S(1)} %broadcast_select_fusion.2), channel_id=1, source_target_pairs={{32,0},{48,16},{64,32},{80,48},{96,64},{112,80},{128,96},{144,112}... | collective-permute-start | bytes 56 | tf_op jit(solution)/shard_map/ppermute | solution.py:42
  195.1 9.5 %collective-permute-start.16 = (f32[4]{0:T(128)S(1)}, f32[4]{0:T(128)S(1)}, u32[]{:S(2)}, u32[]{:S(2)}) collective-permute-start(f32[4]{0:T(128)S(1)} %broadcast_select_fusion.1), channel_id=1, source_target_pairs={{64,0},{80,16},{96,32},{112,48},{128,64},{144,80},{160,96},{176,11... | collective-permute-start | bytes 56 | tf_op jit(solution)/shard_map/ppermute | solution.py:42
  205.7 19.7 %collective-permute-start.9 = (f32[4,128,128]{2,1,0:T(8,128)S(1)}, f32[4,128,128]{2,1,0:T(8,128)S(1)}, u32[]{:S(2)}, u32[]{:S(2)}) collective-permute-start(f32[4,128,128]{2,1,0:T(8,128)S(1)} %fusion.26), channel_id=1, source_target_pairs={{16,0},{32,16},{48,32},{64,48},{80,64},{96,80},{112,96},{128,112},... | collective-permute-start | bytes 786440 | tf_op jit(solution)/shard_map/ppermute | solution.py:38
  225.5 17.2 %collective-permute-start.11 = (f32[4,128,128]{2,1,0:T(8,128)S(1)}, f32[4,128,128]{2,1,0:T(8,128)S(1)}, u32[]{:S(2)}, u32[]{:S(2)}) collective-permute-start(f32[4,128,128]{2,1,0:T(8,128)S(1)} %collective-permute-done.9), channel_id=1, source_target_pairs={{16,0},{32,16},{48,32},{64,48},{80,64},{96,80},{112,96},{128,112},... | collective-permute-start | bytes 786440 | tf_op jit(solution)/shard_map/ppermute | solution.py:42
  242.8 19.2 %collective-permute-start.13 = (f32[4,128,128]{2,1,0:T(8,128)S(1)}, f32[4,128,128]{2,1,0:T(8,128)S(1)}, u32[]{:S(2)}, u32[]{:S(2)}) collective-permute-start(f32[4,128,128]{2,1,0:T(8,128)S(1)} %add_select_fusion.3), channel_id=1, source_target_pairs={{32,0},{48,16},{64,32},{80,48},{96,64},{112,80},{128,96},{144,112}... | collective-permute-start | bytes 786440 | tf_op jit(solution)/shard_map/ppermute | solution.py:42
  248.2 39.5 %copy-start.8 = (f32[4,128,128]{2,1,0:T(8,128)S(1)}, f32[4,128,128]{2,1,0:T(8,128)}, u32[]{:S(2)}) copy-start(f32[4,128,128]{2,1,0:T(8,128)} %copy-done.7) | copy-start | bytes 786436
  262.1 22.7 %collective-permute-start.15 = (f32[4,128,128]{2,1,0:T(8,128)S(1)}, f32[4,128,128]{2,1,0:T(8,128)S(1)}, u32[]{:S(2)}, u32[]{:S(2)}) collective-permute-start(f32[4,128,128]{2,1,0:T(8,128)S(1)} %add_select_fusion.2), channel_id=1, source_target_pairs={{64,0},{80,16},{96,32},{112,48},{128,64},{144,80},{160,96},{176,11... | collective-permute-start | bytes 786440 | tf_op jit(solution)/shard_map/ppermute | solution.py:42
  285.7 23.3 %collective-permute-start.17 = (f32[4,128,128]{2,1,0:T(8,128)}, f32[4,128,128]{2,1,0:T(8,128)}, u32[]{:S(2)}, u32[]{:S(2)}) collective-permute-start(f32[4,128,128]{2,1,0:T(8,128)} %add_select_fusion.1), channel_id=1, source_target_pairs={{128,0},{144,16},{160,32},{176,48},{192,64},{208,80},{224,96},{240... | collective-permute-start | bytes 786440 | tf_op jit(solution)/shard_map/ppermute | solution.py:42
  (20 other events, 259.0 us)
Sparse Core Ops, SparseCore 0:
  21.9 92.8 all-gather.4
  116.6 39.8 all-gather.2
  173.3 133.4 reduce-scatter.4
  309.2 23.7 reduce-scatter.6

commit v2 on v1

--- a/solution.py
+++ b/solution.py
@@ -15,38 +15,29 @@
 WEIGHT_DECAY = 0.1
 
 
-def prefix_scan(gain, state, axis):
+def window_scan(gain, state, axis, sign):
     count = lax.axis_size(axis)
     place = lax.axis_index(axis)
-    gain, state = lax.ppermute((gain, state), axis, [(i, i + 1) for i in range(count - 1)])
-    gain = jnp.where(place >= 1, gain, 1.0)
-    step = 1
-    while step < count:
-        got_gain, got_state = lax.ppermute(
-            (gain, state), axis, [(i, i + step) for i in range(count - step)]
-        )
-        reached = place >= step
-        state = jnp.where(reached, gain[:, None, None] * got_state + state, state)
-        gain = jnp.where(reached, got_gain * gain, gain)
-        step *= 2
-    return state
-
-
-def suffix_scan(gain, state, axis):
-    count = lax.axis_size(axis)
-    place = lax.axis_index(axis)
-    gain, state = lax.ppermute((gain, state), axis, [(i + 1, i) for i in range(count - 1)])
-    gain = jnp.where(place <= count - 2, gain, 1.0)
-    step = 1
-    while step < count:
-        got_gain, got_state = lax.ppermute(
-            (gain, state), axis, [(i + step, i) for i in range(count - step)]
-        )
-        reached = place + step <= count - 1
-        state = jnp.where(reached, state + gain[:, None, None] * got_state, state)
-        gain = jnp.where(reached, gain * got_gain, gain)
-        step *= 2
-    return state
+
+    def join(near, far):
+        return (near[0] * far[0], near[1] + near[0][:, None, None] * far[1])
+
+    def fetch(value, step):
+        pairs = [(i, i + sign * step) for i in range(count) if 0 <= i + sign * step < count]
+        got = lax.ppermute(value, axis, pairs)
+        source = place - sign * step
+        present = (source >= 0) & (source < count)
+        return jax.tree.map(lambda g, e: jnp.where(present, g, e), got, identity)
+
+    own = (gain, state)
+    identity = (jnp.ones_like(gain), jnp.zeros_like(state))
+    near = [fetch(own, step) for step in (1, 2, 3)]
+    inner = join(join(near[0], near[1]), near[2])
+    window = join(own, inner)
+    total = inner
+    for step in (4, 8, 12):
+        total = join(total, fetch(window, step))
+    return total[1]
 
 
 def decay_mask(cumul):
@@ -99,7 +90,7 @@
         leading = leading + totals[block]
     local_start = jnp.stack(start_list)
     lead_sums = jnp.stack(lead_list)
-    incoming = prefix_scan(jnp.exp(leading), running, "ctx")
+    incoming = window_scan(jnp.exp(leading), running, "ctx", 1)
     states = local_start + jnp.exp(lead_sums)[:, :, None, None] * incoming[None]
     rounded = states.astype(jnp.bfloat16)
     inter = decay_in * jnp.einsum(
@@ -124,11 +115,13 @@
     columns = features
     grad_rows = lax.psum_scatter(
         lax.psum_scatter(
-            jnp.einsum("td,th->dh", columns, mixed, preferred_element_type=jnp.float32),
+            jnp.einsum("td,th->dh", columns, mixed, preferred_element_type=jnp.float32).astype(
+                jnp.bfloat16
+            ),
             "ctx",
             scatter_dimension=0,
             tiled=True,
-        ),
+        ).astype(jnp.float32),
         "fsdp",
         scatter_dimension=0,
         tiled=True,
@@ -156,7 +149,7 @@
         trailing = trailing + totals[block]
     local_after = jnp.stack(after_list)
     trail_sums = jnp.stack(trail_list)
-    arriving = suffix_scan(jnp.exp(leading), backing, "ctx")
+    arriving = window_scan(jnp.exp(leading), backing, "ctx", -1)
     after_full = local_after + jnp.exp(trail_sums)[:, :, None, None] * arriving[None]
     back_b = after_full.astype(jnp.bfloat16)
     qgrad = qgrad + decay_in * jnp.einsum(

time: 344 us -> 351 us (1.020)
  waiting for transfers between devices: 164 us -> 184 us
  starting transfers between devices: 82.1 us -> 71.3 us
    all_gather x1, waiting for transfers between devices: 19.5 us -> 40.7 us  [per_device(): features = lax.all_gather(out_grad, 'head', axis=2, tiled=True)[0]]
    ppermute x18 -> x22, waiting for transfers between devices: 109 us -> 91 us  [fetch(): got = lax.ppermute(value, axis, pairs)]
    reduce_scatter x1, waiting for transfers between devices: 15.6 us -> 29.1 us  [per_device(): lax.psum_scatter(jnp.einsum('td,th->dh', columns, mixed, preferred_elemen...]
    ppermute x18 -> x22, starting transfers between devices: 82 us -> 71.2 us  [fetch(): got = lax.ppermute(value, axis, pairs)]
    select_n x16 -> x0, other arithmetic: 7.28 us -> none  [the longest x4 5.09 us: prefix_scan(): state = jnp.where(reached, gain[:, None, None] * got_state + state, state)]
    add x0 -> x4, other arithmetic: none -> 5.27 us  [join(): return (near[0] * far[0], near[1] + near[0][:, None, None] * far[1])]
    unnamed x52 -> x50, local copies, waits for them, and re-layouts: 8.63 us -> 10.3 us
  transfers between devices with their start and end apart: 22 -> 26, of which waited for: 16 -> 12; matrix products, arithmetic and copies ran while one was open for 13% -> 12% of each run, Pallas kernels for 0% -> 0%
where the time goes in v2:
time: 351 us; the launch traced here: 350 us
  waiting for transfers between devices  184 us (52%)
  starting transfers between devices  71.3 us (20%)
  local copies, waits for them, and re-layouts  29.4 us (8%)
  matrix products  24.4 us (7%)
  between operations  15.2 us (4%)
  blocking collectives  13.5 us (4%)
  other arithmetic  11.8 us (3%)
    ppermute x22, waiting for transfers between devices, fetch(): got = lax.ppermute(value, axis, pairs)  91 us
    ppermute x22, starting transfers between devices, fetch(): got = lax.ppermute(value, axis, pairs)  71.2 us
    all_gather x1, waiting for transfers between devices, per_device(): features = lax.all_gather(out_grad, 'head', axis=2, tiled=True)[0]  40.7 us
    reduce_scatter x1, waiting for transfers between devices, per_device(): lax.psum_scatter(jnp.einsum('td,th->dh', columns, mixed, preferred_elemen...  29.1 us
    unnamed x5, waiting for transfers between devices  22.6 us
    all_gather x1, blocking collectives, per_device(): lax.all_gather(weight_b, 'fsdp', axis=0, tiled=True)  13.5 us
    unnamed x50, local copies, waits for them, and re-layouts  10.3 us
  transfers between devices with their start and end apart: 26, of which 12 were waited for; matrix products, arithmetic and copies ran while one was open for 12% of the time, Pallas kernels for 0%

profile of v2, /device:TPU:2, one launch (start us, length us, event | category | flops | bytes accessed | tf_op | source)
XLA Modules:
  0.0 349.9 jit_solution(11883345295995269854)
XLA Ops:
  8.2 13.5 %all_gather.10 = bf16[256,512]{1,0:T(8,128)(2,1)} all-gather(bf16[64,512]{1,0:T(8,128)(2,1)S(1)} %convert_element_type.66), channel_id=1, replica_groups=mesh['ctx'=16,'fsdp'=4,'head'=4] {'fsdp'}, dimensions={0}, use_global_device_ids=true | all-gather | bytes 327680 | tf_op jit(solution)/shard_map/all_gather | solution.py:111
  26.5 8.8 %collective-permute-start.16 = (f32[4]{0:T(128)S(1)}, f32[4]{0:T(128)S(1)}, u32[]{:S(2)}, u32[]{:S(2)}) collective-permute-start(f32[4]{0:T(128)S(1)} %get-tuple-element.40), channel_id=1, source_target_pairs={{48,0},{64,16},{80,32},{96,48},{112,64},{128,80},{144,96},{160,112... | collective-permute-start | bytes 56 | tf_op jit(solution)/shard_map/ppermute | solution.py:27
  40.0 4.7 %collective-permute-start.4 = (f32[4,128,128]{2,1,0:T(8,128)}, f32[4,128,128]{2,1,0:T(8,128)}, u32[]{:S(2)}, u32[]{:S(2)}) collective-permute-start(f32[4,128,128]{2,1,0:T(8,128)} %fusion.28), channel_id=1, source_target_pairs={{0,48},{16,64},{32,80},{48,96},{64,112},{80,128},{96,144},{112,160... | collective-permute-start | bytes 786440 | tf_op jit(solution)/shard_map/ppermute | solution.py:27
  46.7 4.1 %collective-permute-start = (f32[4,128,128]{2,1,0:T(8,128)}, f32[4,128,128]{2,1,0:T(8,128)}, u32[]{:S(2)}, u32[]{:S(2)}) collective-permute-start(f32[4,128,128]{2,1,0:T(8,128)} %fusion.28), channel_id=1, source_target_pairs={{0,16},{16,32},{32,48},{48,64},{64,80},{80,96},{96,112},{112,128},... | collective-permute-start | bytes 786440 | tf_op jit(solution)/shard_map/ppermute | solution.py:27
  53.7 5.5 %collective-permute-start.12 = (f32[4]{0:T(128)S(1)}, f32[4]{0:T(128)S(1)}, u32[]{:S(2)}, u32[]{:S(2)}) collective-permute-start(f32[4]{0:T(128)S(1)} %get-tuple-element.40), channel_id=1, source_target_pairs={{16,0},{32,16},{48,32},{64,48},{80,64},{96,80},{112,96},{128,112},... | collective-permute-start | bytes 56 | tf_op jit(solution)/shard_map/ppermute | solution.py:27
  63.0 33.1 %collective-permute-done.5 = f32[4]{0:T(128)S(1)} collective-permute-done((f32[4]{0:T(128)S(1)}, f32[4]{0:T(128)S(1)}, u32[]{:S(2)}, u32[]{:S(2)}) %collective-permute-start.5) | collective-permute-done | bytes 48 | tf_op jit(solution)/shard_map/ppermute | solution.py:27
  96.1 4.1 %collective-permute-start.1 = (f32[4]{0:T(128)S(1)}, f32[4]{0:T(128)S(1)}, u32[]{:S(2)}, u32[]{:S(2)}) collective-permute-start(f32[4]{0:T(128)S(1)} %get-tuple-element.40), channel_id=1, source_target_pairs={{0,16},{16,32},{32,48},{48,64},{64,80},{80,96},{96,112},{112,128},... | collective-permute-start | bytes 56 | tf_op jit(solution)/shard_map/ppermute | solution.py:27
  100.2 3.5 collective-permute-done.1
  118.0 8.6 %collective-permute-done.9 = f32[4]{0:T(128)S(1)} collective-permute-done((f32[4]{0:T(128)S(1)}, f32[4]{0:T(128)S(1)}, u32[]{:S(2)}, u32[]{:S(2)}) %collective-permute-start.9) | collective-permute-done | bytes 48 | tf_op jit(solution)/shard_map/ppermute | solution.py:27
  133.7 6.5 %copy.190 = bf16[512,4096]{1,0:T(8,128)(2,1)} copy(bf16[512,4096]{0,1:T(8,128)(2,1)} %bitcast.113) | data formatting | bytes 8388608 | tf_op jit(solution)/shard_map/dot_general | solution.py:108
  140.2 40.7 %all-gather.3.cloned.1.call-done = bf16[1,512,4096]{2,1,0:T(8,128)(2,1)} async-done(((bf16[1,512,1024]{2,1,0:T(8,128)(2,1)}), bf16[1,512,4096]{2,1,0:T(8,128)(2,1)}) %all-gather.3.cloned.1.call-update) | async-done | bytes 4194320 | tf_op jit(solution)/shard_map/all_gather | solution.py:105
  180.9 6.3 %multiply_reduce_fusion = (f32[2,256,4]{1,2,0:T(4,128)S(1)}, f32[2,256,4,128]{1,3,2,0:T(8,128)S(1)}) fusion(f32[2,256,4,128]{1,3,2,0:T(8,128)} %get-tuple-element.69, f32[2,256,4]{1,2,0:T(4,128)S(1)} %add_rsqrt_fusion, f32[2,256,4,128]{1,3,2,0:T(8,128)S(1)} %copy-done.3, bf16[2,256,4096,1]{2,1,3,0:T(8,128)(2,1)} %bitcast.112, ...), kind=kOutput, calls=%fused_computation.29 | convolution fusion | flops 2149578752 | bytes 11550720 | tf_op jit(solution)/shard_map/dot_general | solution.py:108
  189.7 6.6 %fusion = bf16[4096,512]{0,1:T(8,128)(2,1)} fusion(bf16[1,512,4096]{2,1,0:T(8,128)(2,1)} %all-gather.3.cloned.1.call-done, bf16[64,8,4,128]{3,2,1,0:T(4,128)(2,1)S(1)} %bitcast.115), kind=kOutput, calls=%fused_computation.1 | convolution fusion | flops 2149580800 | bytes 8912896 | tf_op jit(solution)/shard_map/td,th->dh/dot_general | solution.py:118
  200.9 3.4 collective-permute-start.20
  204.2 6.5 %collective-permute-start.18 = (f32[4]{0:T(128)S(1)}, f32[4]{0:T(128)S(1)}, u32[]{:S(2)}, u32[]{:S(2)}) collective-permute-start(f32[4]{0:T(128)S(1)} %get-tuple-element.43), channel_id=1, source_target_pairs={{64,0},{80,16},{96,32},{112,48},{128,64},{144,80},{160,96},{176,11... | collective-permute-start | bytes 56 | tf_op jit(solution)/shard_map/ppermute | solution.py:27
  210.7 2.9 collective-permute-done.18
  214.0 6.7 %collective-permute-start.15 = (f32[4,128,128]{2,1,0:T(8,128)S(1)}, f32[4,128,128]{2,1,0:T(8,128)S(1)}, u32[]{:S(2)}, u32[]{:S(2)}) collective-permute-start(f32[4,128,128]{2,1,0:T(8,128)S(1)} %fusion.27), channel_id=1, source_target_pairs={{48,0},{64,16},{80,32},{96,48},{112,64},{128,80},{144,96},{160,112... | collective-permute-start | bytes 786440 | tf_op jit(solution)/shard_map/ppermute | solution.py:27
  223.0 3.1 collective-permute-start.11
  231.2 13.1 %collective-permute-done.15 = f32[4,128,128]{2,1,0:T(8,128)S(1)} collective-permute-done((f32[4,128,128]{2,1,0:T(8,128)S(1)}, f32[4,128,128]{2,1,0:T(8,128)S(1)}, u32[]{:S(2)}, u32[]{:S(2)}) %collective-permute-start.15) | collective-permute-done | bytes 262176 | tf_op jit(solution)/shard_map/ppermute | solution.py:27
  244.3 15.9 %collective-permute-done.13 = f32[4,128,128]{2,1,0:T(8,128)S(1)} collective-permute-done((f32[4,128,128]{2,1,0:T(8,128)S(1)}, f32[4,128,128]{2,1,0:T(8,128)S(1)}, u32[]{:S(2)}, u32[]{:S(2)}) %collective-permute-start.13) | collective-permute-done | bytes 262176 | tf_op jit(solution)/shard_map/ppermute | solution.py:27
  260.2 11.2 %collective-permute-done.11 = f32[4,128,128]{2,1,0:T(8,128)S(1)} collective-permute-done((f32[4,128,128]{2,1,0:T(8,128)S(1)}, f32[4,128,128]{2,1,0:T(8,128)S(1)}, u32[]{:S(2)}, u32[]{:S(2)}) %collective-permute-start.11) | collective-permute-done | bytes 262176 | tf_op jit(solution)/shard_map/ppermute | solution.py:27
  275.8 3.3 collective-permute-start.17
  280.7 29.1 %reduce-scatter.5.cloned.1.call-done = bf16[256,512]{0,1:T(8,128)(2,1)} async-done(((bf16[4096,512]{0,1:T(8,128)(2,1)}), bf16[256,512]{0,1:T(8,128)(2,1)}) %reduce-scatter.5.cloned.1.call-update) | async-done | bytes 262160 | tf_op jit(solution)/shard_map/reduce_scatter | solution.py:117
  317.9 21.8 %reduce-scatter.7.cloned.1.call-done = f32[64,512]{1,0:T(8,128)} async-done(((f32[256,512]{1,0:T(8,128)}), f32[64,512]{1,0:T(8,128)}) %reduce-scatter.7.cloned.1.call-update) | async-done | bytes 131088
  (152 shorter events, 71.8 us)
Async XLA Ops:
  7.2 126.5 %all-gather.5.cloned.1.call-start = ((), (), s32[]{:S(2)}) async-start(), calls=%async_computation.3 | async-start | bytes 4456448 | tf_op jit(solution)/shard_map/all_gather | solution.py:110
  21.8 159.1 %all-gather.3.cloned.1.call-start = ((), (), s32[]{:S(2)}) async-start(), calls=%async_computation.2 | async-start | bytes 5242880 | tf_op jit(solution)/shard_map/all_gather | solution.py:105
  22.5 287.3 %reduce-scatter.5.cloned.1.call-start = ((), (), s32[]{:S(2)}) async-start(), calls=%async_computation.4 | async-start | bytes 4456448 | tf_op jit(solution)/shard_map/reduce_scatter | solution.py:117
  26.5 27.2 %collective-permute-start.16 = (f32[4]{0:T(128)S(1)}, f32[4]{0:T(128)S(1)}, u32[]{:S(2)}, u32[]{:S(2)}) collective-permute-start(f32[4]{0:T(128)S(1)} %get-tuple-element.40), channel_id=1, source_target_pairs={{48,0},{64,16},{80,32},{96,48},{112,64},{128,80},{144,96},{160,112... | collective-permute-start | bytes 56 | tf_op jit(solution)/shard_map/ppermute | solution.py:27
  35.2 23.9 %collective-permute-start.14 = (f32[4]{0:T(128)S(1)}, f32[4]{0:T(128)S(1)}, u32[]{:S(2)}, u32[]{:S(2)}) collective-permute-start(f32[4]{0:T(128)S(1)} %get-tuple-element.40), channel_id=1, source_target_pairs={{32,0},{48,16},{64,32},{80,48},{96,64},{112,80},{128,96},{144,112}... | collective-permute-start | bytes 56 | tf_op jit(solution)/shard_map/ppermute | solution.py:27
  40.0 63.6 %collective-permute-start.4 = (f32[4,128,128]{2,1,0:T(8,128)}, f32[4,128,128]{2,1,0:T(8,128)}, u32[]{:S(2)}, u32[]{:S(2)}) collective-permute-start(f32[4,128,128]{2,1,0:T(8,128)} %fusion.28), channel_id=1, source_target_pairs={{0,48},{16,64},{32,80},{48,96},{64,112},{80,128},{96,144},{112,160... | collective-permute-start | bytes 786440 | tf_op jit(solution)/shard_map/ppermute | solution.py:27
  44.8 58.9 %collective-permute-start.2 = (f32[4,128,128]{2,1,0:T(8,128)}, f32[4,128,128]{2,1,0:T(8,128)}, u32[]{:S(2)}, u32[]{:S(2)}) collective-permute-start(f32[4,128,128]{2,1,0:T(8,128)} %fusion.28), channel_id=1, source_target_pairs={{0,32},{16,48},{32,64},{48,80},{64,96},{80,112},{96,128},{112,144}... | collective-permute-start | bytes 786440 | tf_op jit(solution)/shard_map/ppermute | solution.py:27
  46.7 57.0 %collective-permute-start = (f32[4,128,128]{2,1,0:T(8,128)}, f32[4,128,128]{2,1,0:T(8,128)}, u32[]{:S(2)}, u32[]{:S(2)}) collective-permute-start(f32[4,128,128]{2,1,0:T(8,128)} %fusion.28), channel_id=1, source_target_pairs={{0,16},{16,32},{32,48},{48,64},{64,80},{80,96},{96,112},{112,128},... | collective-permute-start | bytes 786440 | tf_op jit(solution)/shard_map/ppermute | solution.py:27
  59.2 36.9 %collective-permute-start.5 = (f32[4]{0:T(128)S(1)}, f32[4]{0:T(128)S(1)}, u32[]{:S(2)}, u32[]{:S(2)}) collective-permute-start(f32[4]{0:T(128)S(1)} %get-tuple-element.40), channel_id=1, source_target_pairs={{0,48},{16,64},{32,80},{48,96},{64,112},{80,128},{96,144},{112,160... | collective-permute-start | bytes 56 | tf_op jit(solution)/shard_map/ppermute | solution.py:27
  61.1 39.1 %collective-permute-start.3 = (f32[4]{0:T(128)S(1)}, f32[4]{0:T(128)S(1)}, u32[]{:S(2)}, u32[]{:S(2)}) collective-permute-start(f32[4]{0:T(128)S(1)} %get-tuple-element.40), channel_id=1, source_target_pairs={{0,32},{16,48},{32,64},{48,80},{64,96},{80,112},{96,128},{112,144}... | collective-permute-start | bytes 56 | tf_op jit(solution)/shard_map/ppermute | solution.py:27
  105.8 23.6 %collective-permute-start.10 = (f32[4,128,128]{2,1,0:T(8,128)}, f32[4,128,128]{2,1,0:T(8,128)S(1)}, u32[]{:S(2)}, u32[]{:S(2)}) collective-permute-start(f32[4,128,128]{2,1,0:T(8,128)} %get-tuple-element.55), channel_id=1, source_target_pairs={{0,192},{16,208},{32,224},{48,240},{1,193},{17,209},{33,225},{49,2... | collective-permute-start | bytes 786440 | tf_op jit(solution)/shard_map/ppermute | solution.py:27
  106.6 22.8 %collective-permute-start.8 = (f32[4,128,128]{2,1,0:T(8,128)}, f32[4,128,128]{2,1,0:T(8,128)}, u32[]{:S(2)}, u32[]{:S(2)}) collective-permute-start(f32[4,128,128]{2,1,0:T(8,128)} %get-tuple-element.55), channel_id=1, source_target_pairs={{0,128},{16,144},{32,160},{48,176},{64,192},{80,208},{96,224},{112... | collective-permute-start | bytes 786440 | tf_op jit(solution)/shard_map/ppermute | solution.py:27
  107.9 21.5 %collective-permute-start.6 = (f32[4,128,128]{2,1,0:T(8,128)}, f32[4,128,128]{2,1,0:T(8,128)}, u32[]{:S(2)}, u32[]{:S(2)}) collective-permute-start(f32[4,128,128]{2,1,0:T(8,128)} %get-tuple-element.55), channel_id=1, source_target_pairs={{0,64},{16,80},{32,96},{48,112},{64,128},{80,144},{96,160},{112,17... | collective-permute-start | bytes 786440 | tf_op jit(solution)/shard_map/ppermute | solution.py:27
  114.8 11.9 %collective-permute-start.9 = (f32[4]{0:T(128)S(1)}, f32[4]{0:T(128)S(1)}, u32[]{:S(2)}, u32[]{:S(2)}) collective-permute-start(f32[4]{0:T(128)S(1)} %get-tuple-element.64), channel_id=1, source_target_pairs={{0,128},{16,144},{32,160},{48,176},{64,192},{80,208},{96,224},{112... | collective-permute-start | bytes 56 | tf_op jit(solution)/shard_map/ppermute | solution.py:27
  116.1 13.2 %collective-permute-start.7 = (f32[4]{0:T(128)S(1)}, f32[4]{0:T(128)S(1)}, u32[]{:S(2)}, u32[]{:S(2)}) collective-permute-start(f32[4]{0:T(128)S(1)} %get-tuple-element.64), channel_id=1, source_target_pairs={{0,64},{16,80},{32,96},{48,112},{64,128},{80,144},{96,160},{112,17... | collective-permute-start | bytes 56 | tf_op jit(solution)/shard_map/ppermute | solution.py:27
  196.4 143.4 %reduce-scatter.7.cloned.1.call-start = ((), (), s32[]{:S(2)}) async-start(), calls=%async_computation.5 | async-start | bytes 655360
  200.9 9.8 %collective-permute-start.20 = (f32[4]{0:T(128)S(1)}, f32[4]{0:T(128)S(1)}, u32[]{:S(2)}, u32[]{:S(2)}) collective-permute-start(f32[4]{0:T(128)S(1)} %get-tuple-element.43), channel_id=1, source_target_pairs={{128,0},{144,16},{160,32},{176,48},{192,64},{208,80},{224,96},{240... | collective-permute-start | bytes 56 | tf_op jit(solution)/shard_map/ppermute | solution.py:27
  204.2 9.4 %collective-permute-start.18 = (f32[4]{0:T(128)S(1)}, f32[4]{0:T(128)S(1)}, u32[]{:S(2)}, u32[]{:S(2)}) collective-permute-start(f32[4]{0:T(128)S(1)} %get-tuple-element.43), channel_id=1, source_target_pairs={{64,0},{80,16},{96,32},{112,48},{128,64},{144,80},{160,96},{176,11... | collective-permute-start | bytes 56 | tf_op jit(solution)/shard_map/ppermute | solution.py:27
  214.0 30.3 %collective-permute-start.15 = (f32[4,128,128]{2,1,0:T(8,128)S(1)}, f32[4,128,128]{2,1,0:T(8,128)S(1)}, u32[]{:S(2)}, u32[]{:S(2)}) collective-permute-start(f32[4,128,128]{2,1,0:T(8,128)S(1)} %fusion.27), channel_id=1, source_target_pairs={{48,0},{64,16},{80,32},{96,48},{112,64},{128,80},{144,96},{160,112... | collective-permute-start | bytes 786440 | tf_op jit(solution)/shard_map/ppermute | solution.py:27
  220.7 39.5 %collective-permute-start.13 = (f32[4,128,128]{2,1,0:T(8,128)S(1)}, f32[4,128,128]{2,1,0:T(8,128)S(1)}, u32[]{:S(2)}, u32[]{:S(2)}) collective-permute-start(f32[4,128,128]{2,1,0:T(8,128)S(1)} %fusion.27), channel_id=1, source_target_pairs={{32,0},{48,16},{64,32},{80,48},{96,64},{112,80},{128,96},{144,112}... | collective-permute-start | bytes 786440 | tf_op jit(solution)/shard_map/ppermute | solution.py:27
  223.0 48.4 %collective-permute-start.11 = (f32[4,128,128]{2,1,0:T(8,128)S(1)}, f32[4,128,128]{2,1,0:T(8,128)S(1)}, u32[]{:S(2)}, u32[]{:S(2)}) collective-permute-start(f32[4,128,128]{2,1,0:T(8,128)S(1)} %fusion.27), channel_id=1, source_target_pairs={{16,0},{32,16},{48,32},{64,48},{80,64},{96,80},{112,96},{128,112},... | collective-permute-start | bytes 786440 | tf_op jit(solution)/shard_map/ppermute | solution.py:27
  272.4 39.5 %collective-permute-start.21 = (f32[4,128,128]{2,1,0:T(8,128)}, f32[4,128,128]{2,1,0:T(8,128)}, u32[]{:S(2)}, u32[]{:S(2)}) collective-permute-start(f32[4,128,128]{2,1,0:T(8,128)} %get-tuple-element.47), channel_id=1, source_target_pairs={{192,0},{208,16},{224,32},{240,48},{193,1},{209,17},{225,33},{241,... | collective-permute-start | bytes 786440 | tf_op jit(solution)/shard_map/ppermute | solution.py:27
  273.7 38.1 %collective-permute-start.19 = (f32[4,128,128]{2,1,0:T(8,128)}, f32[4,128,128]{2,1,0:T(8,128)}, u32[]{:S(2)}, u32[]{:S(2)}) collective-permute-start(f32[4,128,128]{2,1,0:T(8,128)} %get-tuple-element.47), channel_id=1, source_target_pairs={{128,0},{144,16},{160,32},{176,48},{192,64},{208,80},{224,96},{240... | collective-permute-start | bytes 786440 | tf_op jit(solution)/shard_map/ppermute | solution.py:27
  275.8 36.1 %collective-permute-start.17 = (f32[4,128,128]{2,1,0:T(8,128)}, f32[4,128,128]{2,1,0:T(8,128)}, u32[]{:S(2)}, u32[]{:S(2)}) collective-permute-start(f32[4,128,128]{2,1,0:T(8,128)} %get-tuple-element.47), channel_id=1, source_target_pairs={{64,0},{80,16},{96,32},{112,48},{128,64},{144,80},{160,96},{176,11... | collective-permute-start | bytes 786440 | tf_op jit(solution)/shard_map/ppermute | solution.py:27
  (23 other events, 366.5 us)
Sparse Core Ops, SparseCore 0:
  21.9 111.7 all-gather.4
  135.5 45.3 all-gather.2
  196.5 113.2 reduce-scatter.4
  312.2 27.4 reduce-scatter.6

commit v3 on v2

--- a/solution.py
+++ b/solution.py
@@ -23,8 +23,14 @@
         return (near[0] * far[0], near[1] + near[0][:, None, None] * far[1])
 
     def fetch(value, step):
+        high = value[0].astype(jnp.bfloat16)
+        low = (value[0] - high.astype(jnp.float32)).astype(jnp.bfloat16)
+        extra = jnp.broadcast_to(jnp.stack([high, low], axis=1)[:, :, None], (value[1].shape[0], 2, value[1].shape[2]))
+        packed = jnp.concatenate([value[1].astype(jnp.bfloat16), extra], axis=1)
         pairs = [(i, i + sign * step) for i in range(count) if 0 <= i + sign * step < count]
-        got = lax.ppermute(value, axis, pairs)
+        got = lax.ppermute(packed, axis, pairs).astype(jnp.float32)
+        rows = value[1].shape[1]
+        got = (got[:, rows, 0] + got[:, rows + 1, 0], got[:, :rows])
         source = place - sign * step
         present = (source >= 0) & (source < count)
         return jax.tree.map(lambda g, e: jnp.where(present, g, e), got, identity)

time: 351 us -> 307 us (0.87)
  waiting for transfers between devices: 184 us -> 148 us
  starting transfers between devices: 71.3 us -> 45.7 us
  other arithmetic: 11.8 us -> 23.7 us
  local copies, waits for them, and re-layouts: 29.4 us -> 34.4 us
    ppermute x22 -> x12, waiting for transfers between devices: 91 us -> 33 us  [fetch(): got = lax.ppermute(packed, axis, pairs).astype(jnp.float32)]
    ppermute x22 -> x12, starting transfers between devices: 71.2 us -> 45.6 us  [fetch(): got = lax.ppermute(packed, axis, pairs).astype(jnp.float32)]
    all_gather x1, waiting for transfers between devices: 0.97 us -> 24.8 us  [per_device(): lax.all_gather(lax.all_gather(weight_b, 'fsdp', axis=0, tiled=True), 'ctx...]
    reduce_scatter x1, waiting for transfers between devices: 29.1 us -> 44.8 us  [per_device(): lax.psum_scatter(jnp.einsum('td,th->dh', columns, mixed, preferred_elemen...]
    convert_element_type x0 -> x18, other arithmetic: none -> 10.2 us  [the longest x10 6.55 us: fetch(): got = lax.ppermute(packed, axis, pairs).astype(jnp.float32)]
    unnamed x5, waiting for transfers between devices: 22.6 us -> 12.8 us
    all_gather x1, waiting for transfers between devices: 40.7 us -> 32.9 us  [per_device(): features = lax.all_gather(out_grad, 'head', axis=2, tiled=True)[0]]
    unnamed x50 -> x102, local copies, waits for them, and re-layouts: 10.3 us -> 11.9 us
  transfers between devices with their start and end apart: 26 -> 16, of which waited for: 12 -> 11; matrix products, arithmetic and copies ran while one was open for 12% -> 19% of each run, Pallas kernels for 0% -> 0%
where the time goes in v3:
time: 307 us; the launch traced here: 306 us
  waiting for transfers between devices  148 us (48%)
  starting transfers between devices  45.7 us (15%)
  local copies, waits for them, and re-layouts  34.4 us (11%)
  matrix products  25.4 us (8%)
  other arithmetic  23.7 us (8%)
  between operations  15.3 us (5%)
  blocking collectives  13.5 us (4%)
    ppermute x12, starting transfers between devices, fetch(): got = lax.ppermute(packed, axis, pairs).astype(jnp.float32)  45.6 us
    reduce_scatter x1, waiting for transfers between devices, per_device(): lax.psum_scatter(jnp.einsum('td,th->dh', columns, mixed, preferred_elemen...  44.8 us
    ppermute x12, waiting for transfers between devices, fetch(): got = lax.ppermute(packed, axis, pairs).astype(jnp.float32)  33 us
    all_gather x1, waiting for transfers between devices, per_device(): features = lax.all_gather(out_grad, 'head', axis=2, tiled=True)[0]  32.9 us
    all_gather x1, waiting for transfers between devices, per_device(): lax.all_gather(lax.all_gather(weight_b, 'fsdp', axis=0, tiled=True), 'ctx...  24.8 us
    all_gather x1, blocking collectives, per_device(): lax.all_gather(weight_b, 'fsdp', axis=0, tiled=True)  13.5 us
    unnamed x5, waiting for transfers between devices  12.8 us
    unnamed x102, local copies, waits for them, and re-layouts  11.9 us
  transfers between devices with their start and end apart: 16, of which 11 were waited for; matrix products, arithmetic and copies ran while one was open for 19% of the time, Pallas kernels for 0%

profile of v3, /device:TPU:2, one launch (start us, length us, event | category | flops | bytes accessed | tf_op | source)
XLA Modules:
  0.0 306.2 jit_solution(14032674474977776079)
XLA Ops:
  8.2 13.5 %all_gather.10 = bf16[256,512]{1,0:T(8,128)(2,1)} all-gather(bf16[64,512]{1,0:T(8,128)(2,1)S(1)} %convert_element_type.260), channel_id=1, replica_groups=mesh['ctx'=16,'fsdp'=4,'head'=4] {'fsdp'}, dimensions={0}, use_global_device_ids=true | all-gather | bytes 327680 | tf_op jit(solution)/shard_map/all_gather | solution.py:117
  29.5 6.5 %collective-permute-start.2 = (bf16[4,130,128]{2,1,0:T(8,128)(2,1)}, bf16[4,130,128]{2,1,0:T(8,128)(2,1)}, u32[]{:S(2)}, u32[]{:S(2)}) collective-permute-start(bf16[4,130,128]{2,1,0:T(8,128)(2,1)} %pad_maximum_fusion.1), channel_id=1, source_target_pairs={{0,48},{16,64},{32,80},{48,96},{64,112},{80,128},{96,144},{112,160... | collective-permute-start | bytes 399368 | tf_op jit(solution)/shard_map/ppermute | solution.py:31
  36.0 5.5 %collective-permute-start.1 = (bf16[4,130,128]{2,1,0:T(8,128)(2,1)}, bf16[4,130,128]{2,1,0:T(8,128)(2,1)}, u32[]{:S(2)}, u32[]{:S(2)}) collective-permute-start(bf16[4,130,128]{2,1,0:T(8,128)(2,1)} %pad_maximum_fusion.1), channel_id=1, source_target_pairs={{0,32},{16,48},{32,64},{48,80},{64,96},{80,112},{96,128},{112,144}... | collective-permute-start | bytes 399368 | tf_op jit(solution)/shard_map/ppermute | solution.py:31
  41.5 2.9 collective-permute-start
  47.9 3.0 collective-permute-done.2
  51.8 6.2 %collective-permute-done.1 = bf16[4,130,128]{2,1,0:T(8,128)(2,1)} collective-permute-done((bf16[4,130,128]{2,1,0:T(8,128)(2,1)}, bf16[4,130,128]{2,1,0:T(8,128)(2,1)}, u32[]{:S(2)}, u32[]{:S(2)}) %collective-permute-start.1) | collective-permute-done | bytes 133152 | tf_op jit(solution)/shard_map/ppermute | solution.py:31
  59.0 4.4 %collective-permute-done = bf16[4,130,128]{2,1,0:T(8,128)(2,1)} collective-permute-done((bf16[4,130,128]{2,1,0:T(8,128)(2,1)}, bf16[4,130,128]{2,1,0:T(8,128)(2,1)}, u32[]{:S(2)}, u32[]{:S(2)}) %collective-permute-start) | collective-permute-done | bytes 133152 | tf_op jit(solution)/shard_map/ppermute | solution.py:31
  69.0 7.1 %collective-permute-start.3 = (bf16[4,130,128]{2,1,0:T(8,128)(2,1)S(1)}, bf16[4,130,128]{2,1,0:T(8,128)(2,1)}, u32[]{:S(2)}, u32[]{:S(2)}) collective-permute-start(bf16[4,130,128]{2,1,0:T(8,128)(2,1)S(1)} %pad_maximum_fusion.2), channel_id=1, source_target_pairs={{0,64},{16,80},{32,96},{48,112},{64,128},{80,144},{96,160},{112,17... | collective-permute-start | bytes 399368 | tf_op jit(solution)/shard_map/ppermute | solution.py:31
  78.8 2.5 reshape.485
  81.2 2.6 copy.206
  84.7 3.4 %collective-permute-done.3 = bf16[4,130,128]{2,1,0:T(8,128)(2,1)} collective-permute-done((bf16[4,130,128]{2,1,0:T(8,128)(2,1)S(1)}, bf16[4,130,128]{2,1,0:T(8,128)(2,1)}, u32[]{:S(2)}, u32[]{:S(2)}) %collective-permute-start.3) | collective-permute-done | bytes 133152 | tf_op jit(solution)/shard_map/ppermute | solution.py:31
  93.0 24.8 %all-gather.5.cloned.1.call-done = bf16[4096,512]{1,0:T(8,128)(2,1)} async-done(((bf16[256,512]{1,0:T(8,128)(2,1)}), bf16[4096,512]{1,0:T(8,128)(2,1)}) %all-gather.5.cloned.1.call-update) | async-done | bytes 4194320 | tf_op jit(solution)/shard_map/all_gather | solution.py:116
  117.8 6.4 %copy.204 = bf16[512,4096]{1,0:T(8,128)(2,1)} copy(bf16[512,4096]{0,1:T(8,128)(2,1)} %bitcast.150) | data formatting | bytes 8388608 | tf_op jit(solution)/shard_map/dot_general | solution.py:114
  124.2 32.9 %all-gather.3.cloned.1.call-done = bf16[1,512,4096]{2,1,0:T(8,128)(2,1)} async-done(((bf16[1,512,1024]{2,1,0:T(8,128)(2,1)}), bf16[1,512,4096]{2,1,0:T(8,128)(2,1)}) %all-gather.3.cloned.1.call-update) | async-done | bytes 4194320 | tf_op jit(solution)/shard_map/all_gather | solution.py:111
  157.1 6.3 %multiply_reduce_fusion = (f32[2,256,4]{1,2,0:T(4,128)S(1)}, f32[2,256,4,128]{1,3,2,0:T(8,128)S(1)}) fusion(f32[2,256,4,128]{1,3,2,0:T(8,128)} %get-tuple-element.73, f32[2,256,4]{1,2,0:T(4,128)S(1)} %add_rsqrt_fusion, f32[2,256,4,128]{1,3,2,0:T(8,128)S(1)} %copy-done.4, bf16[2,256,4096,1]{2,1,3,0:T(8,128)(2,1)} %bitcast.149, ...), kind=kOutput, calls=%fused_computation.29 | convolution fusion | flops 2149578752 | bytes 11550720 | tf_op jit(solution)/shard_map/dot_general | solution.py:114
  166.0 6.6 %fusion = bf16[4096,512]{0,1:T(8,128)(2,1)} fusion(bf16[1,512,4096]{2,1,0:T(8,128)(2,1)} %all-gather.3.cloned.1.call-done, bf16[64,8,4,128]{3,2,1,0:T(4,128)(2,1)S(1)} %bitcast.152), kind=kOutput, calls=%fused_computation.1 | convolution fusion | flops 2149580800 | bytes 8912896 | tf_op jit(solution)/shard_map/td,th->dh/dot_general | solution.py:124
  180.6 7.7 %collective-permute-start.8 = (bf16[4,130,128]{2,1,0:T(8,128)(2,1)S(1)}, bf16[4,130,128]{2,1,0:T(8,128)(2,1)S(1)}, u32[]{:S(2)}, u32[]{:S(2)}) collective-permute-start(bf16[4,130,128]{2,1,0:T(8,128)(2,1)S(1)} %pad_maximum_fusion), channel_id=1, source_target_pairs={{48,0},{64,16},{80,32},{96,48},{112,64},{128,80},{144,96},{160,112... | collective-permute-start | bytes 399368 | tf_op jit(solution)/shard_map/ppermute | solution.py:31
  188.3 3.2 %collective-permute-start.7 = (bf16[4,130,128]{2,1,0:T(8,128)(2,1)S(1)}, bf16[4,130,128]{2,1,0:T(8,128)(2,1)S(1)}, u32[]{:S(2)}, u32[]{:S(2)}) collective-permute-start(bf16[4,130,128]{2,1,0:T(8,128)(2,1)S(1)} %pad_maximum_fusion), channel_id=1, source_target_pairs={{32,0},{48,16},{64,32},{80,48},{96,64},{112,80},{128,96},{144,112}... | collective-permute-start | bytes 399368 | tf_op jit(solution)/shard_map/ppermute | solution.py:31
  191.5 2.6 collective-permute-start.6
  201.3 8.0 %collective-permute-done.7 = bf16[4,130,128]{2,1,0:T(8,128)(2,1)S(1)} collective-permute-done((bf16[4,130,128]{2,1,0:T(8,128)(2,1)S(1)}, bf16[4,130,128]{2,1,0:T(8,128)(2,1)S(1)}, u32[]{:S(2)}, u32[]{:S(2)}) %collective-permute-start.7) | collective-permute-done | bytes 133152 | tf_op jit(solution)/shard_map/ppermute | solution.py:31
  209.3 6.1 %collective-permute-done.6 = bf16[4,130,128]{2,1,0:T(8,128)(2,1)S(1)} collective-permute-done((bf16[4,130,128]{2,1,0:T(8,128)(2,1)S(1)}, bf16[4,130,128]{2,1,0:T(8,128)(2,1)S(1)}, u32[]{:S(2)}, u32[]{:S(2)}) %collective-permute-start.6) | collective-permute-done | bytes 133152 | tf_op jit(solution)/shard_map/ppermute | solution.py:31
  221.1 4.8 %collective-permute-start.9 = (bf16[4,130,128]{2,1,0:T(8,128)(2,1)S(1)}, bf16[4,130,128]{2,1,0:T(8,128)(2,1)}, u32[]{:S(2)}, u32[]{:S(2)}) collective-permute-start(bf16[4,130,128]{2,1,0:T(8,128)(2,1)S(1)} %pad_maximum_fusion.3), channel_id=1, source_target_pairs={{64,0},{80,16},{96,32},{112,48},{128,64},{144,80},{160,96},{176,11... | collective-permute-start | bytes 399368 | tf_op jit(solution)/shard_map/ppermute | solution.py:31
  226.0 44.8 %reduce-scatter.5.cloned.1.call-done = bf16[256,512]{0,1:T(8,128)(2,1)} async-done(((bf16[4096,512]{0,1:T(8,128)(2,1)}), bf16[256,512]{0,1:T(8,128)(2,1)}) %reduce-scatter.5.cloned.1.call-update) | async-done | bytes 262160 | tf_op jit(solution)/shard_map/reduce_scatter | solution.py:123
  284.0 12.0 %reduce-scatter.7.cloned.1.call-done = f32[64,512]{1,0:T(8,128)} async-done(((f32[256,512]{1,0:T(8,128)}), f32[64,512]{1,0:T(8,128)}) %reduce-scatter.7.cloned.1.call-update) | async-done | bytes 131088
  (216 shorter events, 67.1 us)
Async XLA Ops:
  7.2 110.6 %all-gather.5.cloned.1.call-start = ((), (), s32[]{:S(2)}) async-start(), calls=%async_computation.3 | async-start | bytes 4456448 | tf_op jit(solution)/shard_map/all_gather | solution.py:116
  21.8 135.3 %all-gather.3.cloned.1.call-start = ((), (), s32[]{:S(2)}) async-start(), calls=%async_computation.2 | async-start | bytes 5242880 | tf_op jit(solution)/shard_map/all_gather | solution.py:111
  22.5 248.2 %reduce-scatter.5.cloned.1.call-start = ((), (), s32[]{:S(2)}) async-start(), calls=%async_computation.4 | async-start | bytes 4456448 | tf_op jit(solution)/shard_map/reduce_scatter | solution.py:123
  26.9 38.8 %copy-start.30 = (f32[4]{0:T(128)}, f32[4]{0:T(128)S(1)}, u32[]{:S(2)}) copy-start(f32[4]{0:T(128)S(1)} %get-tuple-element.40) | copy-start | bytes 52
  26.9 38.8 %copy-start.37 = (f32[4]{0:T(128)}, f32[4]{0:T(128)S(1)}, u32[]{:S(2)}) copy-start(f32[4]{0:T(128)S(1)} %get-tuple-element.37) | copy-start | bytes 52
  27.5 38.2 %copy-start.33 = (f32[4]{0:T(128)}, f32[4]{0:T(128)S(1)}, u32[]{:S(2)}) copy-start(f32[4]{0:T(128)S(1)} %broadcast_multiply_fusion.2) | copy-start | bytes 52
  29.5 21.4 %collective-permute-start.2 = (bf16[4,130,128]{2,1,0:T(8,128)(2,1)}, bf16[4,130,128]{2,1,0:T(8,128)(2,1)}, u32[]{:S(2)}, u32[]{:S(2)}) collective-permute-start(bf16[4,130,128]{2,1,0:T(8,128)(2,1)} %pad_maximum_fusion.1), channel_id=1, source_target_pairs={{0,48},{16,64},{32,80},{48,96},{64,112},{80,128},{96,144},{112,160... | collective-permute-start | bytes 399368 | tf_op jit(solution)/shard_map/ppermute | solution.py:31
  36.0 22.1 %collective-permute-start.1 = (bf16[4,130,128]{2,1,0:T(8,128)(2,1)}, bf16[4,130,128]{2,1,0:T(8,128)(2,1)}, u32[]{:S(2)}, u32[]{:S(2)}) collective-permute-start(bf16[4,130,128]{2,1,0:T(8,128)(2,1)} %pad_maximum_fusion.1), channel_id=1, source_target_pairs={{0,32},{16,48},{32,64},{48,80},{64,96},{80,112},{96,128},{112,144}... | collective-permute-start | bytes 399368 | tf_op jit(solution)/shard_map/ppermute | solution.py:31
  41.5 21.9 %collective-permute-start = (bf16[4,130,128]{2,1,0:T(8,128)(2,1)}, bf16[4,130,128]{2,1,0:T(8,128)(2,1)}, u32[]{:S(2)}, u32[]{:S(2)}) collective-permute-start(bf16[4,130,128]{2,1,0:T(8,128)(2,1)} %pad_maximum_fusion.1), channel_id=1, source_target_pairs={{0,16},{16,32},{32,48},{48,64},{64,80},{80,96},{96,112},{112,128},... | collective-permute-start | bytes 399368 | tf_op jit(solution)/shard_map/ppermute | solution.py:31
  67.7 16.1 %collective-permute-start.4 = (bf16[4,130,128]{2,1,0:T(8,128)(2,1)S(1)}, bf16[4,130,128]{2,1,0:T(8,128)(2,1)}, u32[]{:S(2)}, u32[]{:S(2)}) collective-permute-start(bf16[4,130,128]{2,1,0:T(8,128)(2,1)S(1)} %pad_maximum_fusion.2), channel_id=1, source_target_pairs={{0,128},{16,144},{32,160},{48,176},{64,192},{80,208},{96,224},{112... | collective-permute-start | bytes 399368 | tf_op jit(solution)/shard_map/ppermute | solution.py:31
  69.0 19.1 %collective-permute-start.3 = (bf16[4,130,128]{2,1,0:T(8,128)(2,1)S(1)}, bf16[4,130,128]{2,1,0:T(8,128)(2,1)}, u32[]{:S(2)}, u32[]{:S(2)}) collective-permute-start(bf16[4,130,128]{2,1,0:T(8,128)(2,1)S(1)} %pad_maximum_fusion.2), channel_id=1, source_target_pairs={{0,64},{16,80},{32,96},{48,112},{64,128},{80,144},{96,160},{112,17... | collective-permute-start | bytes 399368 | tf_op jit(solution)/shard_map/ppermute | solution.py:31
  76.9 12.3 %collective-permute-start.5 = (bf16[4,130,128]{2,1,0:T(8,128)(2,1)S(1)}, bf16[4,130,128]{2,1,0:T(8,128)(2,1)S(1)}, u32[]{:S(2)}, u32[]{:S(2)}) collective-permute-start(bf16[4,130,128]{2,1,0:T(8,128)(2,1)S(1)} %pad_maximum_fusion.2), channel_id=1, source_target_pairs={{0,192},{16,208},{32,224},{48,240},{1,193},{17,209},{33,225},{49,2... | collective-permute-start | bytes 399368 | tf_op jit(solution)/shard_map/ppermute | solution.py:31
  90.9 26.9 %copy-start.6 = (f32[4,128,128]{2,1,0:T(8,128)}, f32[4,128,128]{2,1,0:T(8,128)S(1)}, u32[]{:S(2)}) copy-start(f32[4,128,128]{2,1,0:T(8,128)S(1)} %fusion.39) | copy-start | bytes 786436
  117.8 39.3 %copy-start.4 = (f32[2,256,4,128]{1,3,2,0:T(8,128)S(1)}, f32[2,256,4,128]{1,3,2,0:T(8,128)}, u32[]{:S(2)}) copy-start(f32[2,256,4,128]{1,3,2,0:T(8,128)} %copy.206) | copy-start | bytes 3145732
  172.6 21.5 %copy-start.21 = (f32[256,256]{1,0:T(8,128)S(1)}, f32[256,256]{1,0:T(8,128)}, u32[]{:S(2)}) copy-start(f32[256,256]{1,0:T(8,128)} %copy-done.20) | copy-start | bytes 786436
  172.6 123.4 %reduce-scatter.7.cloned.1.call-start = ((), (), s32[]{:S(2)}) async-start(), calls=%async_computation.5 | async-start | bytes 655360
  178.8 38.1 %copy-start.34 = (f32[4]{0:T(128)}, f32[4]{0:T(128)S(1)}, u32[]{:S(2)}) copy-start(f32[4]{0:T(128)S(1)} %broadcast_multiply_fusion.1) | copy-start | bytes 52
  180.6 20.7 %collective-permute-start.8 = (bf16[4,130,128]{2,1,0:T(8,128)(2,1)S(1)}, bf16[4,130,128]{2,1,0:T(8,128)(2,1)S(1)}, u32[]{:S(2)}, u32[]{:S(2)}) collective-permute-start(bf16[4,130,128]{2,1,0:T(8,128)(2,1)S(1)} %pad_maximum_fusion), channel_id=1, source_target_pairs={{48,0},{64,16},{80,32},{96,48},{112,64},{128,80},{144,96},{160,112... | collective-permute-start | bytes 399368 | tf_op jit(solution)/shard_map/ppermute | solution.py:31
  188.3 21.0 %collective-permute-start.7 = (bf16[4,130,128]{2,1,0:T(8,128)(2,1)S(1)}, bf16[4,130,128]{2,1,0:T(8,128)(2,1)S(1)}, u32[]{:S(2)}, u32[]{:S(2)}) collective-permute-start(bf16[4,130,128]{2,1,0:T(8,128)(2,1)S(1)} %pad_maximum_fusion), channel_id=1, source_target_pairs={{32,0},{48,16},{64,32},{80,48},{96,64},{112,80},{128,96},{144,112}... | collective-permute-start | bytes 399368 | tf_op jit(solution)/shard_map/ppermute | solution.py:31
  191.5 24.0 %collective-permute-start.6 = (bf16[4,130,128]{2,1,0:T(8,128)(2,1)S(1)}, bf16[4,130,128]{2,1,0:T(8,128)(2,1)S(1)}, u32[]{:S(2)}, u32[]{:S(2)}) collective-permute-start(bf16[4,130,128]{2,1,0:T(8,128)(2,1)S(1)} %pad_maximum_fusion), channel_id=1, source_target_pairs={{16,0},{32,16},{48,32},{64,48},{80,64},{96,80},{112,96},{128,112},... | collective-permute-start | bytes 399368 | tf_op jit(solution)/shard_map/ppermute | solution.py:31
  209.3 64.1 %copy-start.9 = (bf16[2,256,4,128]{1,3,2,0:T(8,128)(2,1)S(1)}, bf16[2,256,4,128]{1,3,2,0:T(8,128)(2,1)}, u32[]{:S(2)}) copy-start(bf16[2,256,4,128]{1,3,2,0:T(8,128)(2,1)} %fusion.10) | copy-start | bytes 1572868
  217.9 59.5 %collective-permute-start.11 = (bf16[4,130,128]{2,1,0:T(8,128)(2,1)S(1)}, bf16[4,130,128]{2,1,0:T(8,128)(2,1)}, u32[]{:S(2)}, u32[]{:S(2)}) collective-permute-start(bf16[4,130,128]{2,1,0:T(8,128)(2,1)S(1)} %pad_maximum_fusion.3), channel_id=1, source_target_pairs={{192,0},{208,16},{224,32},{240,48},{193,1},{209,17},{225,33},{241,... | collective-permute-start | bytes 399368 | tf_op jit(solution)/shard_map/ppermute | solution.py:31
  219.2 55.5 %collective-permute-start.10 = (bf16[4,130,128]{2,1,0:T(8,128)(2,1)S(1)}, bf16[4,130,128]{2,1,0:T(8,128)(2,1)}, u32[]{:S(2)}, u32[]{:S(2)}) collective-permute-start(bf16[4,130,128]{2,1,0:T(8,128)(2,1)S(1)} %pad_maximum_fusion.3), channel_id=1, source_target_pairs={{128,0},{144,16},{160,32},{176,48},{192,64},{208,80},{224,96},{240... | collective-permute-start | bytes 399368 | tf_op jit(solution)/shard_map/ppermute | solution.py:31
  221.1 54.5 %collective-permute-start.9 = (bf16[4,130,128]{2,1,0:T(8,128)(2,1)S(1)}, bf16[4,130,128]{2,1,0:T(8,128)(2,1)}, u32[]{:S(2)}, u32[]{:S(2)}) collective-permute-start(bf16[4,130,128]{2,1,0:T(8,128)(2,1)S(1)} %pad_maximum_fusion.3), channel_id=1, source_target_pairs={{64,0},{80,16},{96,32},{112,48},{128,64},{144,80},{160,96},{176,11... | collective-permute-start | bytes 399368 | tf_op jit(solution)/shard_map/ppermute | solution.py:31
  (39 other events, 349.1 us)
Sparse Core Ops, SparseCore 0:
  21.9 95.8 all-gather.4
  119.6 37.4 all-gather.2
  172.7 97.9 reduce-scatter.4
  273.1 22.9 reduce-scatter.6

commit v4 on v3

--- a/solution.py
+++ b/solution.py
@@ -71,6 +71,8 @@
     head_local = log_decay.shape[2]
     width_local = queries.shape[2]
     blocks = tok_local // SPAN
+    features = lax.all_gather(out_grad, "head", axis=2, tiled=True)[0]
+    features, weight_b = lax.optimization_barrier((features, out_weight.astype(jnp.bfloat16)))
     shaped = (blocks, SPAN, head_local, HEAD_DIM)
     query_c = queries.reshape(shaped)
     key_c = keys.reshape(shaped)
@@ -108,8 +110,6 @@
     normed = attn * inverse
     silu_gate = jax.nn.silu(gate_pre.reshape(shaped).astype(jnp.float32))
     mixed = (normed * silu_gate).astype(jnp.bfloat16).reshape(tok_local, width_local)
-    features = lax.all_gather(out_grad, "head", axis=2, tiled=True)[0]
-    weight_b = out_weight.astype(jnp.bfloat16)
     columns = features
     mixed_grad = jnp.dot(
         columns,
@@ -127,11 +127,11 @@
             "ctx",
             scatter_dimension=0,
             tiled=True,
-        ).astype(jnp.float32),
+        ),
         "fsdp",
         scatter_dimension=0,
         tiled=True,
-    )
+    ).astype(jnp.float32)
     normed_grad = mixed_grad.reshape(shaped) * silu_gate
     inner = jnp.mean(normed_grad * normed, axis=-1, keepdims=True)
     attn_grad = (inverse * (normed_grad - normed * inner)).astype(jnp.bfloat16)

time: 307 us -> 297 us (0.967)
  waiting for transfers between devices: 148 us -> 169 us
  local copies, waits for them, and re-layouts: 34.4 us -> 15.4 us
  starting transfers between devices: 45.7 us -> 39.6 us
  other arithmetic: 23.7 us -> 18.3 us
    reduce_scatter x0 -> x1, waiting for transfers between devices: none -> 15.5 us  [per_device(): lax.psum_scatter(lax.psum_scatter(jnp.einsum('td,th->dh', columns, mixed,...]
    unnamed x5 -> x4, waiting for transfers between devices: 12.8 us -> 0.73 us
    all_gather x1, waiting for transfers between devices: 32.9 us -> 44 us  [per_device(): features = lax.all_gather(out_grad, 'head', axis=2, tiled=True)[0]]
    unnamed x102 -> x82, local copies, waits for them, and re-layouts: 11.9 us -> 0.82 us
    ppermute x12, waiting for transfers between devices: 33 us -> 42.3 us  [fetch(): got = lax.ppermute(packed, axis, pairs).astype(jnp.float32)]
    reduce_scatter x1, waiting for transfers between devices: 44.8 us -> 38 us  [per_device(): lax.psum_scatter(jnp.einsum('td,th->dh', columns, mixed, preferred_elemen...]
    dot_general x1 -> x0, local copies, waits for them, and re-layouts: 6.43 us -> none  [per_device(): jnp.dot(columns, lax.all_gather(lax.all_gather(weight_b, 'fsdp', axis=0,...]
    ppermute x12, starting transfers between devices: 45.6 us -> 39.5 us  [fetch(): got = lax.ppermute(packed, axis, pairs).astype(jnp.float32)]
  transfers between devices with their start and end apart: 16 -> 16, of which waited for: 11 -> 12; matrix products, arithmetic and copies ran while one was open for 19% -> 12% of each run, Pallas kernels for 0% -> 0%
where the time goes in v4:
time: 297 us; the launch traced here: 296 us
  waiting for transfers between devices  169 us (57%)
  starting transfers between devices  39.6 us (13%)
  matrix products  25.2 us (8%)
  other arithmetic  18.3 us (6%)
  local copies, waits for them, and re-layouts  15.4 us (5%)
  between operations  15.4 us (5%)
  blocking collectives  13.3 us (4%)
    all_gather x1, waiting for transfers between devices, per_device(): features = lax.all_gather(out_grad, 'head', axis=2, tiled=True)[0]  44 us
    ppermute x12, waiting for transfers between devices, fetch(): got = lax.ppermute(packed, axis, pairs).astype(jnp.float32)  42.3 us
    ppermute x12, starting transfers between devices, fetch(): got = lax.ppermute(packed, axis, pairs).astype(jnp.float32)  39.5 us
    reduce_scatter x1, waiting for transfers between devices, per_device(): lax.psum_scatter(jnp.einsum('td,th->dh', columns, mixed, preferred_elemen...  38 us
    all_gather x1, waiting for transfers between devices, per_device(): lax.all_gather(lax.all_gather(weight_b, 'fsdp', axis=0, tiled=True), 'ctx...  28.1 us
    reduce_scatter x1, waiting for transfers between devices, per_device(): lax.psum_scatter(lax.psum_scatter(jnp.einsum('td,th->dh', columns, mixed,...  15.5 us
    all_gather x1, blocking collectives, per_device(): lax.all_gather(weight_b, 'fsdp', axis=0, tiled=True)  13.3 us
    dot_general x1, matrix products, per_device(): jnp.dot(columns, lax.all_gather(lax.all_gather(weight_b, 'fsdp', axis=0,...  6.77 us
  transfers between devices with their start and end apart: 16, of which 12 were waited for; matrix products, arithmetic and copies ran while one was open for 12% of the time, Pallas kernels for 0%

profile of v4, /device:TPU:2, one launch (start us, length us, event | category | flops | bytes accessed | tf_op | source)
XLA Modules:
  0.0 296.0 jit_solution(11684175723808837289)
XLA Ops:
  8.9 44.0 %all-gather.3.cloned.1.call-done = bf16[1,512,4096]{2,1,0:T(8,128)(2,1)} async-done(((bf16[1,512,1024]{2,1,0:T(8,128)(2,1)}), bf16[1,512,4096]{2,1,0:T(8,128)(2,1)}) %all-gather.3.cloned.1.call-update) | async-done | bytes 4194320 | tf_op jit(solution)/shard_map/all_gather | solution.py:74
  52.9 13.3 %all_gather.10 = bf16[256,512]{1,0:T(8,128)(2,1)} all-gather(bf16[64,512]{1,0:T(8,128)(2,1)S(1)} %convert_element_type.257), channel_id=1, replica_groups=mesh['ctx'=16,'fsdp'=4,'head'=4] {'fsdp'}, dimensions={0}, use_global_device_ids=true | all-gather | bytes 327680 | tf_op jit(solution)/shard_map/all_gather | solution.py:117
  67.1 2.4 reduce-window.6
  72.7 5.4 %collective-permute-start.2 = (bf16[4,130,128]{2,1,0:T(8,128)(2,1)S(1)}, bf16[4,130,128]{2,1,0:T(8,128)(2,1)}, u32[]{:S(2)}, u32[]{:S(2)}) collective-permute-start(bf16[4,130,128]{2,1,0:T(8,128)(2,1)S(1)} %pad_maximum_fusion.1), channel_id=1, source_target_pairs={{0,48},{16,64},{32,80},{48,96},{64,112},{80,128},{96,144},{112,160... | collective-permute-start | bytes 399368 | tf_op jit(solution)/shard_map/ppermute | solution.py:31
  78.1 4.8 %collective-permute-start.1 = (bf16[4,130,128]{2,1,0:T(8,128)(2,1)S(1)}, bf16[4,130,128]{2,1,0:T(8,128)(2,1)}, u32[]{:S(2)}, u32[]{:S(2)}) collective-permute-start(bf16[4,130,128]{2,1,0:T(8,128)(2,1)S(1)} %pad_maximum_fusion.1), channel_id=1, source_target_pairs={{0,32},{16,48},{32,64},{48,80},{64,96},{80,112},{96,128},{112,144}... | collective-permute-start | bytes 399368 | tf_op jit(solution)/shard_map/ppermute | solution.py:31
  82.9 2.6 collective-permute-start
  88.2 4.8 %collective-permute-done.2 = bf16[4,130,128]{2,1,0:T(8,128)(2,1)} collective-permute-done((bf16[4,130,128]{2,1,0:T(8,128)(2,1)S(1)}, bf16[4,130,128]{2,1,0:T(8,128)(2,1)}, u32[]{:S(2)}, u32[]{:S(2)}) %collective-permute-start.2) | collective-permute-done | bytes 133152 | tf_op jit(solution)/shard_map/ppermute | solution.py:31
  94.0 5.6 %collective-permute-done.1 = bf16[4,130,128]{2,1,0:T(8,128)(2,1)} collective-permute-done((bf16[4,130,128]{2,1,0:T(8,128)(2,1)S(1)}, bf16[4,130,128]{2,1,0:T(8,128)(2,1)}, u32[]{:S(2)}, u32[]{:S(2)}) %collective-permute-start.1) | collective-permute-done | bytes 133152 | tf_op jit(solution)/shard_map/ppermute | solution.py:31
  100.5 5.3 %collective-permute-done = bf16[4,130,128]{2,1,0:T(8,128)(2,1)S(1)} collective-permute-done((bf16[4,130,128]{2,1,0:T(8,128)(2,1)S(1)}, bf16[4,130,128]{2,1,0:T(8,128)(2,1)S(1)}, u32[]{:S(2)}, u32[]{:S(2)}) %collective-permute-start) | collective-permute-done | bytes 133152 | tf_op jit(solution)/shard_map/ppermute | solution.py:31
  109.0 5.3 %collective-permute-start.3 = (bf16[4,130,128]{2,1,0:T(8,128)(2,1)S(1)}, bf16[4,130,128]{2,1,0:T(8,128)(2,1)}, u32[]{:S(2)}, u32[]{:S(2)}) collective-permute-start(bf16[4,130,128]{2,1,0:T(8,128)(2,1)S(1)} %pad_maximum_fusion.2), channel_id=1, source_target_pairs={{0,64},{16,80},{32,96},{48,112},{64,128},{80,144},{96,160},{112,17... | collective-permute-start | bytes 399368 | tf_op jit(solution)/shard_map/ppermute | solution.py:31
  119.1 8.1 %collective-permute-done.3 = bf16[4,130,128]{2,1,0:T(8,128)(2,1)} collective-permute-done((bf16[4,130,128]{2,1,0:T(8,128)(2,1)S(1)}, bf16[4,130,128]{2,1,0:T(8,128)(2,1)}, u32[]{:S(2)}, u32[]{:S(2)}) %collective-permute-start.3) | collective-permute-done | bytes 133152 | tf_op jit(solution)/shard_map/ppermute | solution.py:31
  131.7 28.1 %all-gather.5.cloned.1.call-done = bf16[4096,512]{1,0:T(8,128)(2,1)} async-done(((bf16[256,512]{1,0:T(8,128)(2,1)}), bf16[4096,512]{1,0:T(8,128)(2,1)}) %all-gather.5.cloned.1.call-update) | async-done | bytes 4194320 | tf_op jit(solution)/shard_map/all_gather | solution.py:116
  159.9 6.8 %fusion.87 = f32[512,512]{1,0:T(8,128)} fusion(bf16[512,4096]{1,0:T(8,128)(2,1)} %bitcast.143, bf16[4096,512]{1,0:T(8,128)(2,1)} %all-gather.5.cloned.1.call-done), kind=kOutput, calls=%fused_computation.175 | convolution fusion | flops 2147483648 | bytes 9437184 | tf_op jit(solution)/shard_map/dot_general | solution.py:114
  166.6 2.5 reshape.480
  173.9 6.6 %convolution_convert_fusion = bf16[4096,512]{1,0:T(8,128)(2,1)} fusion(bf16[512,4096]{1,0:T(8,128)(2,1)} %bitcast.144, bf16[64,8,4,128]{3,2,1,0:T(4,128)(2,1)S(1)} %bitcast.136), kind=kOutput, calls=%fused_computation | convolution fusion | flops 2149580800 | bytes 8912896 | tf_op jit(solution)/shard_map/td,th->dh/dot_general | solution.py:124
  182.3 5.3 %collective-permute-start.8 = (bf16[4,130,128]{2,1,0:T(8,128)(2,1)S(1)}, bf16[4,130,128]{2,1,0:T(8,128)(2,1)S(1)}, u32[]{:S(2)}, u32[]{:S(2)}) collective-permute-start(bf16[4,130,128]{2,1,0:T(8,128)(2,1)S(1)} %pad_maximum_fusion), channel_id=1, source_target_pairs={{48,0},{64,16},{80,32},{96,48},{112,64},{128,80},{144,96},{160,112... | collective-permute-start | bytes 399368 | tf_op jit(solution)/shard_map/ppermute | solution.py:31
  187.6 2.9 collective-permute-start.7
  190.6 3.1 %collective-permute-start.6 = (bf16[4,130,128]{2,1,0:T(8,128)(2,1)S(1)}, bf16[4,130,128]{2,1,0:T(8,128)(2,1)S(1)}, u32[]{:S(2)}, u32[]{:S(2)}) collective-permute-start(bf16[4,130,128]{2,1,0:T(8,128)(2,1)S(1)} %pad_maximum_fusion), channel_id=1, source_target_pairs={{16,0},{32,16},{48,32},{64,48},{80,64},{96,80},{112,96},{128,112},... | collective-permute-start | bytes 399368 | tf_op jit(solution)/shard_map/ppermute | solution.py:31
  199.6 7.1 %collective-permute-done.7 = bf16[4,130,128]{2,1,0:T(8,128)(2,1)S(1)} collective-permute-done((bf16[4,130,128]{2,1,0:T(8,128)(2,1)S(1)}, bf16[4,130,128]{2,1,0:T(8,128)(2,1)S(1)}, u32[]{:S(2)}, u32[]{:S(2)}) %collective-permute-start.7) | collective-permute-done | bytes 133152 | tf_op jit(solution)/shard_map/ppermute | solution.py:31
  206.8 2.7 collective-permute-done.6
  213.5 4.9 %collective-permute-start.9 = (bf16[4,130,128]{2,1,0:T(8,128)(2,1)S(1)}, bf16[4,130,128]{2,1,0:T(8,128)(2,1)S(1)}, u32[]{:S(2)}, u32[]{:S(2)}) collective-permute-start(bf16[4,130,128]{2,1,0:T(8,128)(2,1)S(1)} %pad_maximum_fusion.3), channel_id=1, source_target_pairs={{64,0},{80,16},{96,32},{112,48},{128,64},{144,80},{160,96},{176,11... | collective-permute-start | bytes 399368 | tf_op jit(solution)/shard_map/ppermute | solution.py:31
  220.7 7.3 %collective-permute-done.9 = bf16[4,130,128]{2,1,0:T(8,128)(2,1)S(1)} collective-permute-done((bf16[4,130,128]{2,1,0:T(8,128)(2,1)S(1)}, bf16[4,130,128]{2,1,0:T(8,128)(2,1)S(1)}, u32[]{:S(2)}, u32[]{:S(2)}) %collective-permute-start.9) | collective-permute-done | bytes 133152 | tf_op jit(solution)/shard_map/ppermute | solution.py:31
  229.3 38.0 %reduce-scatter.3.cloned.1.call-done = bf16[256,512]{1,0:T(8,128)(2,1)} async-done(((bf16[4096,512]{1,0:T(8,128)(2,1)}), bf16[256,512]{1,0:T(8,128)(2,1)}) %reduce-scatter.3.cloned.1.call-update) | async-done | bytes 262160 | tf_op jit(solution)/shard_map/reduce_scatter | solution.py:123
  272.3 15.5 %reduce-scatter.5.cloned.1.call-done = bf16[64,512]{1,0:T(8,128)(2,1)} async-done(((bf16[256,512]{1,0:T(8,128)(2,1)}), bf16[64,512]{1,0:T(8,128)(2,1)}) %reduce-scatter.5.cloned.1.call-update) | async-done | bytes 65552 | tf_op jit(solution)/shard_map/reduce_scatter | solution.py:122
  (198 shorter events, 48.0 us)
Async XLA Ops:
  7.2 63.7 %copy-start.13 = (bf16[1,512,512]{2,1,0:T(8,128)(2,1)S(1)}, bf16[1,512,512]{2,1,0:T(8,128)(2,1)}, u32[]{:S(2)}) copy-start(bf16[1,512,512]{2,1,0:T(8,128)(2,1)} %param.12) | copy-start | bytes 1572868
  7.2 63.8 %copy-start.14 = (bf16[1,512,512]{2,1,0:T(8,128)(2,1)S(1)}, bf16[1,512,512]{2,1,0:T(8,128)(2,1)}, u32[]{:S(2)}) copy-start(bf16[1,512,512]{2,1,0:T(8,128)(2,1)} %param.13) | copy-start | bytes 1572868
  7.2 45.7 %all-gather.3.cloned.1.call-start = ((), (), s32[]{:S(2)}) async-start(), calls=%async_computation.2 | async-start | bytes 5242880 | tf_op jit(solution)/shard_map/all_gather | solution.py:74
  7.9 151.9 %all-gather.5.cloned.1.call-start = ((), (), s32[]{:S(2)}) async-start(), calls=%async_computation.3 | async-start | bytes 4456448 | tf_op jit(solution)/shard_map/all_gather | solution.py:116
  66.3 201.0 %reduce-scatter.3.cloned.1.call-start = ((), (), s32[]{:S(2)}) async-start(), calls=%async_computation.4 | async-start | bytes 4456448 | tf_op jit(solution)/shard_map/reduce_scatter | solution.py:123
  70.7 36.0 %copy-start.28 = (f32[4]{0:T(128)}, f32[4]{0:T(128)S(1)}, u32[]{:S(2)}) copy-start(f32[4]{0:T(128)S(1)} %get-tuple-element.14) | copy-start | bytes 52
  70.7 36.0 %copy-start.34 = (f32[4]{0:T(128)}, f32[4]{0:T(128)S(1)}, u32[]{:S(2)}) copy-start(f32[4]{0:T(128)S(1)} %get-tuple-element.11) | copy-start | bytes 52
  71.3 35.4 %copy-start.31 = (f32[4]{0:T(128)}, f32[4]{0:T(128)S(1)}, u32[]{:S(2)}) copy-start(f32[4]{0:T(128)S(1)} %broadcast_multiply_fusion.2) | copy-start | bytes 52
  72.7 20.3 %collective-permute-start.2 = (bf16[4,130,128]{2,1,0:T(8,128)(2,1)S(1)}, bf16[4,130,128]{2,1,0:T(8,128)(2,1)}, u32[]{:S(2)}, u32[]{:S(2)}) collective-permute-start(bf16[4,130,128]{2,1,0:T(8,128)(2,1)S(1)} %pad_maximum_fusion.1), channel_id=1, source_target_pairs={{0,48},{16,64},{32,80},{48,96},{64,112},{80,128},{96,144},{112,160... | collective-permute-start | bytes 399368 | tf_op jit(solution)/shard_map/ppermute | solution.py:31
  78.1 21.4 %collective-permute-start.1 = (bf16[4,130,128]{2,1,0:T(8,128)(2,1)S(1)}, bf16[4,130,128]{2,1,0:T(8,128)(2,1)}, u32[]{:S(2)}, u32[]{:S(2)}) collective-permute-start(bf16[4,130,128]{2,1,0:T(8,128)(2,1)S(1)} %pad_maximum_fusion.1), channel_id=1, source_target_pairs={{0,32},{16,48},{32,64},{48,80},{64,96},{80,112},{96,128},{112,144}... | collective-permute-start | bytes 399368 | tf_op jit(solution)/shard_map/ppermute | solution.py:31
  82.9 22.9 %collective-permute-start = (bf16[4,130,128]{2,1,0:T(8,128)(2,1)S(1)}, bf16[4,130,128]{2,1,0:T(8,128)(2,1)S(1)}, u32[]{:S(2)}, u32[]{:S(2)}) collective-permute-start(bf16[4,130,128]{2,1,0:T(8,128)(2,1)S(1)} %pad_maximum_fusion.1), channel_id=1, source_target_pairs={{0,16},{16,32},{32,48},{48,64},{64,80},{80,96},{96,112},{112,128},... | collective-permute-start | bytes 399368 | tf_op jit(solution)/shard_map/ppermute | solution.py:31
  85.9 44.0 %copy-start = (bf16[2,256,4,128]{1,3,2,0:T(8,128)(2,1)}, bf16[2,256,4,128]{1,3,2,0:T(8,128)(2,1)S(1)}, u32[]{:S(2)}) copy-start(bf16[2,256,4,128]{1,3,2,0:T(8,128)(2,1)S(1)} %copy.143) | copy-start | bytes 1572868
  107.7 10.4 %collective-permute-start.4 = (bf16[4,130,128]{2,1,0:T(8,128)(2,1)S(1)}, bf16[4,130,128]{2,1,0:T(8,128)(2,1)}, u32[]{:S(2)}, u32[]{:S(2)}) collective-permute-start(bf16[4,130,128]{2,1,0:T(8,128)(2,1)S(1)} %pad_maximum_fusion.2), channel_id=1, source_target_pairs={{0,128},{16,144},{32,160},{48,176},{64,192},{80,208},{96,224},{112... | collective-permute-start | bytes 399368 | tf_op jit(solution)/shard_map/ppermute | solution.py:31
  109.0 18.1 %collective-permute-start.3 = (bf16[4,130,128]{2,1,0:T(8,128)(2,1)S(1)}, bf16[4,130,128]{2,1,0:T(8,128)(2,1)}, u32[]{:S(2)}, u32[]{:S(2)}) collective-permute-start(bf16[4,130,128]{2,1,0:T(8,128)(2,1)S(1)} %pad_maximum_fusion.2), channel_id=1, source_target_pairs={{0,64},{16,80},{32,96},{48,112},{64,128},{80,144},{96,160},{112,17... | collective-permute-start | bytes 399368 | tf_op jit(solution)/shard_map/ppermute | solution.py:31
  115.1 13.1 %collective-permute-start.5 = (bf16[4,130,128]{2,1,0:T(8,128)(2,1)S(1)}, bf16[4,130,128]{2,1,0:T(8,128)(2,1)S(1)}, u32[]{:S(2)}, u32[]{:S(2)}) collective-permute-start(bf16[4,130,128]{2,1,0:T(8,128)(2,1)S(1)} %pad_maximum_fusion.2), channel_id=1, source_target_pairs={{0,192},{16,208},{32,224},{48,240},{1,193},{17,209},{33,225},{49,2... | collective-permute-start | bytes 399368 | tf_op jit(solution)/shard_map/ppermute | solution.py:31
  129.9 36.7 %copy-start.10 = (f32[4,128,128]{2,1,0:T(8,128)}, f32[4,128,128]{2,1,0:T(8,128)S(1)}, u32[]{:S(2)}) copy-start(f32[4,128,128]{2,1,0:T(8,128)S(1)} %fusion.37) | copy-start | bytes 786436
  180.5 107.2 %reduce-scatter.5.cloned.1.call-start = ((), (), s32[]{:S(2)}) async-start(), calls=%async_computation.5 | async-start | bytes 327680 | tf_op jit(solution)/shard_map/reduce_scatter | solution.py:122
  182.3 17.3 %collective-permute-start.8 = (bf16[4,130,128]{2,1,0:T(8,128)(2,1)S(1)}, bf16[4,130,128]{2,1,0:T(8,128)(2,1)S(1)}, u32[]{:S(2)}, u32[]{:S(2)}) collective-permute-start(bf16[4,130,128]{2,1,0:T(8,128)(2,1)S(1)} %pad_maximum_fusion), channel_id=1, source_target_pairs={{48,0},{64,16},{80,32},{96,48},{112,64},{128,80},{144,96},{160,112... | collective-permute-start | bytes 399368 | tf_op jit(solution)/shard_map/ppermute | solution.py:31
  187.6 19.1 %collective-permute-start.7 = (bf16[4,130,128]{2,1,0:T(8,128)(2,1)S(1)}, bf16[4,130,128]{2,1,0:T(8,128)(2,1)S(1)}, u32[]{:S(2)}, u32[]{:S(2)}) collective-permute-start(bf16[4,130,128]{2,1,0:T(8,128)(2,1)S(1)} %pad_maximum_fusion), channel_id=1, source_target_pairs={{32,0},{48,16},{64,32},{80,48},{96,64},{112,80},{128,96},{144,112}... | collective-permute-start | bytes 399368 | tf_op jit(solution)/shard_map/ppermute | solution.py:31
  190.6 18.9 %collective-permute-start.6 = (bf16[4,130,128]{2,1,0:T(8,128)(2,1)S(1)}, bf16[4,130,128]{2,1,0:T(8,128)(2,1)S(1)}, u32[]{:S(2)}, u32[]{:S(2)}) collective-permute-start(bf16[4,130,128]{2,1,0:T(8,128)(2,1)S(1)} %pad_maximum_fusion), channel_id=1, source_target_pairs={{16,0},{32,16},{48,32},{64,48},{80,64},{96,80},{112,96},{128,112},... | collective-permute-start | bytes 399368 | tf_op jit(solution)/shard_map/ppermute | solution.py:31
  210.3 17.9 %collective-permute-start.11 = (bf16[4,130,128]{2,1,0:T(8,128)(2,1)S(1)}, bf16[4,130,128]{2,1,0:T(8,128)(2,1)}, u32[]{:S(2)}, u32[]{:S(2)}) collective-permute-start(bf16[4,130,128]{2,1,0:T(8,128)(2,1)S(1)} %pad_maximum_fusion.3), channel_id=1, source_target_pairs={{192,0},{208,16},{224,32},{240,48},{193,1},{209,17},{225,33},{241,... | collective-permute-start | bytes 399368 | tf_op jit(solution)/shard_map/ppermute | solution.py:31
  211.6 8.2 %collective-permute-start.10 = (bf16[4,130,128]{2,1,0:T(8,128)(2,1)S(1)}, bf16[4,130,128]{2,1,0:T(8,128)(2,1)}, u32[]{:S(2)}, u32[]{:S(2)}) collective-permute-start(bf16[4,130,128]{2,1,0:T(8,128)(2,1)S(1)} %pad_maximum_fusion.3), channel_id=1, source_target_pairs={{128,0},{144,16},{160,32},{176,48},{192,64},{208,80},{224,96},{240... | collective-permute-start | bytes 399368 | tf_op jit(solution)/shard_map/ppermute | solution.py:31
  213.5 14.5 %collective-permute-start.9 = (bf16[4,130,128]{2,1,0:T(8,128)(2,1)S(1)}, bf16[4,130,128]{2,1,0:T(8,128)(2,1)S(1)}, u32[]{:S(2)}, u32[]{:S(2)}) collective-permute-start(bf16[4,130,128]{2,1,0:T(8,128)(2,1)S(1)} %pad_maximum_fusion.3), channel_id=1, source_target_pairs={{64,0},{80,16},{96,32},{112,48},{128,64},{144,80},{160,96},{176,11... | collective-permute-start | bytes 399368 | tf_op jit(solution)/shard_map/ppermute | solution.py:31
  218.5 48.8 %copy-start.23 = (f32[2,256,4]{1,2,0:T(4,128)S(1)}, f32[2,256,4]{1,2,0:T(4,128)}, u32[]{:S(2)}) copy-start(f32[2,256,4]{1,2,0:T(4,128)} %copy-done.22) | copy-start | bytes 24580
  (33 other events, 290.2 us)
Sparse Core Ops, SparseCore 0:
  9.8 43.0 all-gather.2
  66.4 93.4 all-gather.4
  180.6 86.6 reduce-scatter.2
  269.7 18.0 reduce-scatter.4

commit v5 on v4

--- a/solution.py
+++ b/solution.py
@@ -72,7 +72,8 @@
     width_local = queries.shape[2]
     blocks = tok_local // SPAN
     features = lax.all_gather(out_grad, "head", axis=2, tiled=True)[0]
-    features, weight_b = lax.optimization_barrier((features, out_weight.astype(jnp.bfloat16)))
+    weight_part = lax.all_gather(out_weight.astype(jnp.bfloat16), "fsdp", axis=0, tiled=True)
+    features, weight_part = lax.optimization_barrier((features, weight_part))
     shaped = (blocks, SPAN, head_local, HEAD_DIM)
     query_c = queries.reshape(shaped)
     key_c = keys.reshape(shaped)
@@ -113,9 +114,7 @@
     columns = features
     mixed_grad = jnp.dot(
         columns,
-        lax.all_gather(
-            lax.all_gather(weight_b, "fsdp", axis=0, tiled=True), "ctx", axis=0, tiled=True
-        ),
+        lax.all_gather(weight_part, "ctx", axis=0, tiled=True),
         preferred_element_type=jnp.float32,
     )
     columns = features

time: 297 us -> 287 us (0.966)
  waiting for transfers between devices: 169 us -> 159 us
    all_gather x1, waiting for transfers between devices: 44 us -> 30.5 us  [per_device(): features = lax.all_gather(out_grad, 'head', axis=2, tiled=True)[0]]
    ppermute x12, waiting for transfers between devices: 42.3 us -> 46.6 us  [fetch(): got = lax.ppermute(packed, axis, pairs).astype(jnp.float32)]
  transfers between devices with their start and end apart: 16 -> 16, of which waited for: 12 -> 12; matrix products, arithmetic and copies ran while one was open for 12% -> 13% of each run, Pallas kernels for 0% -> 0%
where the time goes in v5:
time: 287 us; the launch traced here: 286 us
  waiting for transfers between devices  159 us (55%)
  starting transfers between devices  38.8 us (14%)
  matrix products  25.2 us (9%)
  other arithmetic  18.3 us (6%)
  local copies, waits for them, and re-layouts  15.4 us (5%)
  between operations  15.4 us (5%)
  blocking collectives  13.5 us (5%)
    ppermute x12, waiting for transfers between devices, fetch(): got = lax.ppermute(packed, axis, pairs).astype(jnp.float32)  46.6 us
    ppermute x12, starting transfers between devices, fetch(): got = lax.ppermute(packed, axis, pairs).astype(jnp.float32)  38.6 us
    reduce_scatter x1, waiting for transfers between devices, per_device(): lax.psum_scatter(jnp.einsum('td,th->dh', columns, mixed, preferred_elemen...  37.6 us
    all_gather x1, waiting for transfers between devices, per_device(): features = lax.all_gather(out_grad, 'head', axis=2, tiled=True)[0]  30.5 us
    all_gather x1, waiting for transfers between devices, per_device(): lax.all_gather(weight_part, 'ctx', axis=0, tiled=True)  26.8 us
    reduce_scatter x1, waiting for transfers between devices, per_device(): lax.psum_scatter(lax.psum_scatter(jnp.einsum('td,th->dh', columns, mixed,...  16.8 us
    all_gather x1, blocking collectives, per_device(): lax.all_gather(out_weight.astype(jnp.bfloat16), 'fsdp', axis=0, tiled=True)  13.5 us
    dot_general x1, matrix products, per_device(): jnp.dot(columns, lax.all_gather(weight_part, 'ctx', axis=0, tiled=True),...  6.77 us
  transfers between devices with their start and end apart: 16, of which 12 were waited for; matrix products, arithmetic and copies ran while one was open for 13% of the time, Pallas kernels for 0%

profile of v5, /device:TPU:2, one launch (start us, length us, event | category | flops | bytes accessed | tf_op | source)
XLA Modules:
  0.0 285.6 jit_solution(5815177229138645195)
XLA Ops:
  8.9 13.5 %all_gather.10 = bf16[256,512]{1,0:T(8,128)(2,1)} all-gather(bf16[64,512]{1,0:T(8,128)(2,1)S(1)} %convert_element_type.257), channel_id=1, replica_groups=mesh['ctx'=16,'fsdp'=4,'head'=4] {'fsdp'}, dimensions={0}, use_global_device_ids=true | all-gather | bytes 327680 | tf_op jit(solution)/shard_map/all_gather | solution.py:75
  22.4 30.5 %all-gather.3.cloned.1.call-done = bf16[1,512,4096]{2,1,0:T(8,128)(2,1)} async-done(((bf16[1,512,1024]{2,1,0:T(8,128)(2,1)}), bf16[1,512,4096]{2,1,0:T(8,128)(2,1)}) %all-gather.3.cloned.1.call-update) | async-done | bytes 4194320 | tf_op jit(solution)/shard_map/all_gather | solution.py:74
  53.7 2.4 reduce-window.6
  59.3 5.4 %collective-permute-start.2 = (bf16[4,130,128]{2,1,0:T(8,128)(2,1)S(1)}, bf16[4,130,128]{2,1,0:T(8,128)(2,1)}, u32[]{:S(2)}, u32[]{:S(2)}) collective-permute-start(bf16[4,130,128]{2,1,0:T(8,128)(2,1)S(1)} %pad_maximum_fusion.1), channel_id=1, source_target_pairs={{0,48},{16,64},{32,80},{48,96},{64,112},{80,128},{96,144},{112,160... | collective-permute-start | bytes 399368 | tf_op jit(solution)/shard_map/ppermute | solution.py:31
  64.8 4.8 %collective-permute-start.1 = (bf16[4,130,128]{2,1,0:T(8,128)(2,1)S(1)}, bf16[4,130,128]{2,1,0:T(8,128)(2,1)}, u32[]{:S(2)}, u32[]{:S(2)}) collective-permute-start(bf16[4,130,128]{2,1,0:T(8,128)(2,1)S(1)} %pad_maximum_fusion.1), channel_id=1, source_target_pairs={{0,32},{16,48},{32,64},{48,80},{64,96},{80,112},{96,128},{112,144}... | collective-permute-start | bytes 399368 | tf_op jit(solution)/shard_map/ppermute | solution.py:31
  69.6 2.6 collective-permute-start
  74.9 5.7 %collective-permute-done.2 = bf16[4,130,128]{2,1,0:T(8,128)(2,1)} collective-permute-done((bf16[4,130,128]{2,1,0:T(8,128)(2,1)S(1)}, bf16[4,130,128]{2,1,0:T(8,128)(2,1)}, u32[]{:S(2)}, u32[]{:S(2)}) %collective-permute-start.2) | collective-permute-done | bytes 133152 | tf_op jit(solution)/shard_map/ppermute | solution.py:31
  81.4 7.8 %collective-permute-done.1 = bf16[4,130,128]{2,1,0:T(8,128)(2,1)} collective-permute-done((bf16[4,130,128]{2,1,0:T(8,128)(2,1)S(1)}, bf16[4,130,128]{2,1,0:T(8,128)(2,1)}, u32[]{:S(2)}, u32[]{:S(2)}) %collective-permute-start.1) | collective-permute-done | bytes 133152 | tf_op jit(solution)/shard_map/ppermute | solution.py:31
  90.2 4.5 %collective-permute-done = bf16[4,130,128]{2,1,0:T(8,128)(2,1)S(1)} collective-permute-done((bf16[4,130,128]{2,1,0:T(8,128)(2,1)S(1)}, bf16[4,130,128]{2,1,0:T(8,128)(2,1)S(1)}, u32[]{:S(2)}, u32[]{:S(2)}) %collective-permute-start) | collective-permute-done | bytes 133152 | tf_op jit(solution)/shard_map/ppermute | solution.py:31
  97.9 4.5 %collective-permute-start.3 = (bf16[4,130,128]{2,1,0:T(8,128)(2,1)S(1)}, bf16[4,130,128]{2,1,0:T(8,128)(2,1)}, u32[]{:S(2)}, u32[]{:S(2)}) collective-permute-start(bf16[4,130,128]{2,1,0:T(8,128)(2,1)S(1)} %pad_maximum_fusion.2), channel_id=1, source_target_pairs={{0,64},{16,80},{32,96},{48,112},{64,128},{80,144},{96,160},{112,17... | collective-permute-start | bytes 399368 | tf_op jit(solution)/shard_map/ppermute | solution.py:31
  109.2 8.6 %collective-permute-done.3 = bf16[4,130,128]{2,1,0:T(8,128)(2,1)} collective-permute-done((bf16[4,130,128]{2,1,0:T(8,128)(2,1)S(1)}, bf16[4,130,128]{2,1,0:T(8,128)(2,1)}, u32[]{:S(2)}, u32[]{:S(2)}) %collective-permute-start.3) | collective-permute-done | bytes 133152 | tf_op jit(solution)/shard_map/ppermute | solution.py:31
  122.4 26.8 %all-gather.5.cloned.1.call-done = bf16[4096,512]{1,0:T(8,128)(2,1)} async-done(((bf16[256,512]{1,0:T(8,128)(2,1)}), bf16[4096,512]{1,0:T(8,128)(2,1)}) %all-gather.5.cloned.1.call-update) | async-done | bytes 4194320 | tf_op jit(solution)/shard_map/all_gather | solution.py:117
  149.2 6.8 %fusion.87 = f32[512,512]{1,0:T(8,128)} fusion(bf16[512,4096]{1,0:T(8,128)(2,1)} %bitcast.143, bf16[4096,512]{1,0:T(8,128)(2,1)} %all-gather.5.cloned.1.call-done), kind=kOutput, calls=%fused_computation.175 | convolution fusion | flops 2147483648 | bytes 9437184 | tf_op jit(solution)/shard_map/dot_general | solution.py:115
  156.0 2.5 reshape.480
  163.2 6.6 %convolution_convert_fusion = bf16[4096,512]{1,0:T(8,128)(2,1)} fusion(bf16[512,4096]{1,0:T(8,128)(2,1)} %bitcast.144, bf16[64,8,4,128]{3,2,1,0:T(4,128)(2,1)S(1)} %bitcast.136), kind=kOutput, calls=%fused_computation | convolution fusion | flops 2149580800 | bytes 8912896 | tf_op jit(solution)/shard_map/td,th->dh/dot_general | solution.py:123
  171.7 5.5 %collective-permute-start.8 = (bf16[4,130,128]{2,1,0:T(8,128)(2,1)S(1)}, bf16[4,130,128]{2,1,0:T(8,128)(2,1)S(1)}, u32[]{:S(2)}, u32[]{:S(2)}) collective-permute-start(bf16[4,130,128]{2,1,0:T(8,128)(2,1)S(1)} %pad_maximum_fusion), channel_id=1, source_target_pairs={{48,0},{64,16},{80,32},{96,48},{112,64},{128,80},{144,96},{160,112... | collective-permute-start | bytes 399368 | tf_op jit(solution)/shard_map/ppermute | solution.py:31
  177.1 3.6 %collective-permute-start.7 = (bf16[4,130,128]{2,1,0:T(8,128)(2,1)S(1)}, bf16[4,130,128]{2,1,0:T(8,128)(2,1)S(1)}, u32[]{:S(2)}, u32[]{:S(2)}) collective-permute-start(bf16[4,130,128]{2,1,0:T(8,128)(2,1)S(1)} %pad_maximum_fusion), channel_id=1, source_target_pairs={{32,0},{48,16},{64,32},{80,48},{96,64},{112,80},{128,96},{144,112}... | collective-permute-start | bytes 399368 | tf_op jit(solution)/shard_map/ppermute | solution.py:31
  180.8 2.5 collective-permute-start.6
  187.9 6.9 %collective-permute-done.7 = bf16[4,130,128]{2,1,0:T(8,128)(2,1)S(1)} collective-permute-done((bf16[4,130,128]{2,1,0:T(8,128)(2,1)S(1)}, bf16[4,130,128]{2,1,0:T(8,128)(2,1)S(1)}, u32[]{:S(2)}, u32[]{:S(2)}) %collective-permute-start.7) | collective-permute-done | bytes 133152 | tf_op jit(solution)/shard_map/ppermute | solution.py:31
  194.9 2.9 %collective-permute-done.6 = bf16[4,130,128]{2,1,0:T(8,128)(2,1)S(1)} collective-permute-done((bf16[4,130,128]{2,1,0:T(8,128)(2,1)S(1)}, bf16[4,130,128]{2,1,0:T(8,128)(2,1)S(1)}, u32[]{:S(2)}, u32[]{:S(2)}) %collective-permute-start.6) | collective-permute-done | bytes 133152 | tf_op jit(solution)/shard_map/ppermute | solution.py:31
  201.8 4.5 %collective-permute-start.9 = (bf16[4,130,128]{2,1,0:T(8,128)(2,1)S(1)}, bf16[4,130,128]{2,1,0:T(8,128)(2,1)S(1)}, u32[]{:S(2)}, u32[]{:S(2)}) collective-permute-start(bf16[4,130,128]{2,1,0:T(8,128)(2,1)S(1)} %pad_maximum_fusion.3), channel_id=1, source_target_pairs={{64,0},{80,16},{96,32},{112,48},{128,64},{144,80},{160,96},{176,11... | collective-permute-start | bytes 399368 | tf_op jit(solution)/shard_map/ppermute | solution.py:31
  208.7 8.2 %collective-permute-done.9 = bf16[4,130,128]{2,1,0:T(8,128)(2,1)S(1)} collective-permute-done((bf16[4,130,128]{2,1,0:T(8,128)(2,1)S(1)}, bf16[4,130,128]{2,1,0:T(8,128)(2,1)S(1)}, u32[]{:S(2)}, u32[]{:S(2)}) %collective-permute-start.9) | collective-permute-done | bytes 133152 | tf_op jit(solution)/shard_map/ppermute | solution.py:31
  218.0 37.6 %reduce-scatter.3.cloned.1.call-done = bf16[256,512]{1,0:T(8,128)(2,1)} async-done(((bf16[4096,512]{1,0:T(8,128)(2,1)}), bf16[256,512]{1,0:T(8,128)(2,1)}) %reduce-scatter.3.cloned.1.call-update) | async-done | bytes 262160 | tf_op jit(solution)/shard_map/reduce_scatter | solution.py:122
  260.6 16.8 %reduce-scatter.5.cloned.1.call-done = bf16[64,512]{1,0:T(8,128)(2,1)} async-done(((bf16[256,512]{1,0:T(8,128)(2,1)}), bf16[64,512]{1,0:T(8,128)(2,1)}) %reduce-scatter.5.cloned.1.call-update) | async-done | bytes 65552 | tf_op jit(solution)/shard_map/reduce_scatter | solution.py:121
  (198 shorter events, 48.8 us)
Async XLA Ops:
  7.2 50.4 %copy-start.13 = (bf16[1,512,512]{2,1,0:T(8,128)(2,1)S(1)}, bf16[1,512,512]{2,1,0:T(8,128)(2,1)}, u32[]{:S(2)}) copy-start(bf16[1,512,512]{2,1,0:T(8,128)(2,1)} %param.12) | copy-start | bytes 1572868
  7.2 50.5 %copy-start.14 = (bf16[1,512,512]{2,1,0:T(8,128)(2,1)S(1)}, bf16[1,512,512]{2,1,0:T(8,128)(2,1)}, u32[]{:S(2)}) copy-start(bf16[1,512,512]{2,1,0:T(8,128)(2,1)} %param.13) | copy-start | bytes 1572868
  7.2 45.7 %all-gather.3.cloned.1.call-start = ((), (), s32[]{:S(2)}) async-start(), calls=%async_computation.2 | async-start | bytes 5242880 | tf_op jit(solution)/shard_map/all_gather | solution.py:74
  7.9 141.3 %all-gather.5.cloned.1.call-start = ((), (), s32[]{:S(2)}) async-start(), calls=%async_computation.3 | async-start | bytes 4456448 | tf_op jit(solution)/shard_map/all_gather | solution.py:117
  53.0 202.7 %reduce-scatter.3.cloned.1.call-start = ((), (), s32[]{:S(2)}) async-start(), calls=%async_computation.4 | async-start | bytes 4456448 | tf_op jit(solution)/shard_map/reduce_scatter | solution.py:122
  57.4 38.3 %copy-start.28 = (f32[4]{0:T(128)}, f32[4]{0:T(128)S(1)}, u32[]{:S(2)}) copy-start(f32[4]{0:T(128)S(1)} %get-tuple-element.14) | copy-start | bytes 52
  57.4 38.3 %copy-start.34 = (f32[4]{0:T(128)}, f32[4]{0:T(128)S(1)}, u32[]{:S(2)}) copy-start(f32[4]{0:T(128)S(1)} %get-tuple-element.11) | copy-start | bytes 52
  58.0 37.7 %copy-start.31 = (f32[4]{0:T(128)}, f32[4]{0:T(128)S(1)}, u32[]{:S(2)}) copy-start(f32[4]{0:T(128)S(1)} %broadcast_multiply_fusion.2) | copy-start | bytes 52
  59.3 21.2 %collective-permute-start.2 = (bf16[4,130,128]{2,1,0:T(8,128)(2,1)S(1)}, bf16[4,130,128]{2,1,0:T(8,128)(2,1)}, u32[]{:S(2)}, u32[]{:S(2)}) collective-permute-start(bf16[4,130,128]{2,1,0:T(8,128)(2,1)S(1)} %pad_maximum_fusion.1), channel_id=1, source_target_pairs={{0,48},{16,64},{32,80},{48,96},{64,112},{80,128},{96,144},{112,160... | collective-permute-start | bytes 399368 | tf_op jit(solution)/shard_map/ppermute | solution.py:31
  64.8 24.4 %collective-permute-start.1 = (bf16[4,130,128]{2,1,0:T(8,128)(2,1)S(1)}, bf16[4,130,128]{2,1,0:T(8,128)(2,1)}, u32[]{:S(2)}, u32[]{:S(2)}) collective-permute-start(bf16[4,130,128]{2,1,0:T(8,128)(2,1)S(1)} %pad_maximum_fusion.1), channel_id=1, source_target_pairs={{0,32},{16,48},{32,64},{48,80},{64,96},{80,112},{96,128},{112,144}... | collective-permute-start | bytes 399368 | tf_op jit(solution)/shard_map/ppermute | solution.py:31
  69.6 25.1 %collective-permute-start = (bf16[4,130,128]{2,1,0:T(8,128)(2,1)S(1)}, bf16[4,130,128]{2,1,0:T(8,128)(2,1)S(1)}, u32[]{:S(2)}, u32[]{:S(2)}) collective-permute-start(bf16[4,130,128]{2,1,0:T(8,128)(2,1)S(1)} %pad_maximum_fusion.1), channel_id=1, source_target_pairs={{0,16},{16,32},{32,48},{48,64},{64,80},{80,96},{96,112},{112,128},... | collective-permute-start | bytes 399368 | tf_op jit(solution)/shard_map/ppermute | solution.py:31
  72.6 48.0 %copy-start = (bf16[2,256,4,128]{1,3,2,0:T(8,128)(2,1)}, bf16[2,256,4,128]{1,3,2,0:T(8,128)(2,1)S(1)}, u32[]{:S(2)}) copy-start(bf16[2,256,4,128]{1,3,2,0:T(8,128)(2,1)S(1)} %copy.143) | copy-start | bytes 1572868
  96.6 11.7 %collective-permute-start.4 = (bf16[4,130,128]{2,1,0:T(8,128)(2,1)S(1)}, bf16[4,130,128]{2,1,0:T(8,128)(2,1)}, u32[]{:S(2)}, u32[]{:S(2)}) collective-permute-start(bf16[4,130,128]{2,1,0:T(8,128)(2,1)S(1)} %pad_maximum_fusion.2), channel_id=1, source_target_pairs={{0,128},{16,144},{32,160},{48,176},{64,192},{80,208},{96,224},{112... | collective-permute-start | bytes 399368 | tf_op jit(solution)/shard_map/ppermute | solution.py:31
  97.9 19.9 %collective-permute-start.3 = (bf16[4,130,128]{2,1,0:T(8,128)(2,1)S(1)}, bf16[4,130,128]{2,1,0:T(8,128)(2,1)}, u32[]{:S(2)}, u32[]{:S(2)}) collective-permute-start(bf16[4,130,128]{2,1,0:T(8,128)(2,1)S(1)} %pad_maximum_fusion.2), channel_id=1, source_target_pairs={{0,64},{16,80},{32,96},{48,112},{64,128},{80,144},{96,160},{112,17... | collective-permute-start | bytes 399368 | tf_op jit(solution)/shard_map/ppermute | solution.py:31
  103.2 15.7 %collective-permute-start.5 = (bf16[4,130,128]{2,1,0:T(8,128)(2,1)S(1)}, bf16[4,130,128]{2,1,0:T(8,128)(2,1)S(1)}, u32[]{:S(2)}, u32[]{:S(2)}) collective-permute-start(bf16[4,130,128]{2,1,0:T(8,128)(2,1)S(1)} %pad_maximum_fusion.2), channel_id=1, source_target_pairs={{0,192},{16,208},{32,224},{48,240},{1,193},{17,209},{33,225},{49,2... | collective-permute-start | bytes 399368 | tf_op jit(solution)/shard_map/ppermute | solution.py:31
  120.6 35.4 %copy-start.10 = (f32[4,128,128]{2,1,0:T(8,128)}, f32[4,128,128]{2,1,0:T(8,128)S(1)}, u32[]{:S(2)}) copy-start(f32[4,128,128]{2,1,0:T(8,128)S(1)} %fusion.37) | copy-start | bytes 786436
  169.9 107.5 %reduce-scatter.5.cloned.1.call-start = ((), (), s32[]{:S(2)}) async-start(), calls=%async_computation.5 | async-start | bytes 327680 | tf_op jit(solution)/shard_map/reduce_scatter | solution.py:121
  171.7 16.3 %collective-permute-start.8 = (bf16[4,130,128]{2,1,0:T(8,128)(2,1)S(1)}, bf16[4,130,128]{2,1,0:T(8,128)(2,1)S(1)}, u32[]{:S(2)}, u32[]{:S(2)}) collective-permute-start(bf16[4,130,128]{2,1,0:T(8,128)(2,1)S(1)} %pad_maximum_fusion), channel_id=1, source_target_pairs={{48,0},{64,16},{80,32},{96,48},{112,64},{128,80},{144,96},{160,112... | collective-permute-start | bytes 399368 | tf_op jit(solution)/shard_map/ppermute | solution.py:31
  177.1 17.7 %collective-permute-start.7 = (bf16[4,130,128]{2,1,0:T(8,128)(2,1)S(1)}, bf16[4,130,128]{2,1,0:T(8,128)(2,1)S(1)}, u32[]{:S(2)}, u32[]{:S(2)}) collective-permute-start(bf16[4,130,128]{2,1,0:T(8,128)(2,1)S(1)} %pad_maximum_fusion), channel_id=1, source_target_pairs={{32,0},{48,16},{64,32},{80,48},{96,64},{112,80},{128,96},{144,112}... | collective-permute-start | bytes 399368 | tf_op jit(solution)/shard_map/ppermute | solution.py:31
  180.8 16.9 %collective-permute-start.6 = (bf16[4,130,128]{2,1,0:T(8,128)(2,1)S(1)}, bf16[4,130,128]{2,1,0:T(8,128)(2,1)S(1)}, u32[]{:S(2)}, u32[]{:S(2)}) collective-permute-start(bf16[4,130,128]{2,1,0:T(8,128)(2,1)S(1)} %pad_maximum_fusion), channel_id=1, source_target_pairs={{16,0},{32,16},{48,32},{64,48},{80,64},{96,80},{112,96},{128,112},... | collective-permute-start | bytes 399368 | tf_op jit(solution)/shard_map/ppermute | solution.py:31
  198.5 18.5 %collective-permute-start.11 = (bf16[4,130,128]{2,1,0:T(8,128)(2,1)S(1)}, bf16[4,130,128]{2,1,0:T(8,128)(2,1)}, u32[]{:S(2)}, u32[]{:S(2)}) collective-permute-start(bf16[4,130,128]{2,1,0:T(8,128)(2,1)S(1)} %pad_maximum_fusion.3), channel_id=1, source_target_pairs={{192,0},{208,16},{224,32},{240,48},{193,1},{209,17},{225,33},{241,... | collective-permute-start | bytes 399368 | tf_op jit(solution)/shard_map/ppermute | solution.py:31
  199.8 7.9 %collective-permute-start.10 = (bf16[4,130,128]{2,1,0:T(8,128)(2,1)S(1)}, bf16[4,130,128]{2,1,0:T(8,128)(2,1)}, u32[]{:S(2)}, u32[]{:S(2)}) collective-permute-start(bf16[4,130,128]{2,1,0:T(8,128)(2,1)S(1)} %pad_maximum_fusion.3), channel_id=1, source_target_pairs={{128,0},{144,16},{160,32},{176,48},{192,64},{208,80},{224,96},{240... | collective-permute-start | bytes 399368 | tf_op jit(solution)/shard_map/ppermute | solution.py:31
  201.8 15.0 %collective-permute-start.9 = (bf16[4,130,128]{2,1,0:T(8,128)(2,1)S(1)}, bf16[4,130,128]{2,1,0:T(8,128)(2,1)S(1)}, u32[]{:S(2)}, u32[]{:S(2)}) collective-permute-start(bf16[4,130,128]{2,1,0:T(8,128)(2,1)S(1)} %pad_maximum_fusion.3), channel_id=1, source_target_pairs={{64,0},{80,16},{96,32},{112,48},{128,64},{144,80},{160,96},{176,11... | collective-permute-start | bytes 399368 | tf_op jit(solution)/shard_map/ppermute | solution.py:31
  206.4 49.2 %copy-start.23 = (f32[2,256,4]{1,2,0:T(4,128)S(1)}, f32[2,256,4]{1,2,0:T(4,128)}, u32[]{:S(2)}) copy-start(f32[2,256,4]{1,2,0:T(4,128)} %copy-done.22) | copy-start | bytes 24580
  (33 other events, 302.7 us)
Sparse Core Ops, SparseCore 0:
  9.8 43.0 all-gather.2
  54.7 94.4 all-gather.4
  170.0 85.6 reduce-scatter.2
  258.0 19.3 reduce-scatter.4

commit v6 on v5

--- a/solution.py
+++ b/solution.py
@@ -112,21 +112,15 @@
     silu_gate = jax.nn.silu(gate_pre.reshape(shaped).astype(jnp.float32))
     mixed = (normed * silu_gate).astype(jnp.bfloat16).reshape(tok_local, width_local)
     columns = features
-    mixed_grad = jnp.dot(
-        columns,
-        lax.all_gather(weight_part, "ctx", axis=0, tiled=True),
-        preferred_element_type=jnp.float32,
-    )
-    columns = features
+    partial = jnp.einsum("td,th->dh", columns, mixed, preferred_element_type=jnp.float32).astype(
+        jnp.bfloat16
+    )
+    weight_full, partial = lax.optimization_barrier(
+        (lax.all_gather(weight_part, "ctx", axis=0, tiled=True), partial)
+    )
+    mixed_grad = jnp.dot(columns, weight_full, preferred_element_type=jnp.float32)
     grad_rows = lax.psum_scatter(
-        lax.psum_scatter(
-            jnp.einsum("td,th->dh", columns, mixed, preferred_element_type=jnp.float32).astype(
-                jnp.bfloat16
-            ),
-            "ctx",
-            scatter_dimension=0,
-            tiled=True,
-        ),
+        lax.psum_scatter(partial, "ctx", scatter_dimension=0, tiled=True),
         "fsdp",
         scatter_dimension=0,
         tiled=True,

time: 287 us -> 277 us (0.965)
  waiting for transfers between devices: 159 us -> 146 us
  other arithmetic: 18.3 us -> 22.3 us
    ppermute x12, waiting for transfers between devices: 46.6 us -> 41.2 us  [fetch(): got = lax.ppermute(packed, axis, pairs).astype(jnp.float32)]
    all_gather x1, waiting for transfers between devices: 26.8 us -> 22.2 us  [per_device(): lax.all_gather(weight_part, 'ctx', axis=0, tiled=True)]
    reduce_scatter x2, waiting for transfers between devices: 54.4 us -> 51 us  [the longest x1 33.1 us: per_device(): lax.psum_scatter(partial, 'ctx', scatter_dimension=0, tiled=True)]
  transfers between devices with their start and end apart: 16 -> 16, of which waited for: 12 -> 11; matrix products, arithmetic and copies ran while one was open for 13% -> 22% of each run, Pallas kernels for 0% -> 0%
where the time goes in v6:
time: 277 us; the launch traced here: 276 us
  waiting for transfers between devices  146 us (53%)
  starting transfers between devices  37.9 us (14%)
  matrix products  24.2 us (9%)
  other arithmetic  22.3 us (8%)
  local copies, waits for them, and re-layouts  17.1 us (6%)
  between operations  15.4 us (6%)
  blocking collectives  13.5 us (5%)
    ppermute x12, waiting for transfers between devices, fetch(): got = lax.ppermute(packed, axis, pairs).astype(jnp.float32)  41.2 us
    ppermute x12, starting transfers between devices, fetch(): got = lax.ppermute(packed, axis, pairs).astype(jnp.float32)  37.7 us
    reduce_scatter x1, waiting for transfers between devices, per_device(): lax.psum_scatter(partial, 'ctx', scatter_dimension=0, tiled=True)  33.1 us
    all_gather x1, waiting for transfers between devices, per_device(): features = lax.all_gather(out_grad, 'head', axis=2, tiled=True)[0]  30.5 us
    all_gather x1, waiting for transfers between devices, per_device(): lax.all_gather(weight_part, 'ctx', axis=0, tiled=True)  22.2 us
    reduce_scatter x1, waiting for transfers between devices, per_device(): lax.psum_scatter(lax.psum_scatter(partial, 'ctx', scatter_dimension=0, ti...  17.9 us
    all_gather x1, blocking collectives, per_device(): lax.all_gather(out_weight.astype(jnp.bfloat16), 'fsdp', axis=0, tiled=True)  13.5 us
    dot_general x1, matrix products, per_device(): jnp.einsum('td,th->dh', columns, mixed, preferred_element_type=jnp.float32)  6.72 us
  transfers between devices with their start and end apart: 16, of which 11 were waited for; matrix products, arithmetic and copies ran while one was open for 22% of the time, Pallas kernels for 0%

profile of v6, /device:TPU:2, one launch (start us, length us, event | category | flops | bytes accessed | tf_op | source)
XLA Modules:
  0.0 276.0 jit_solution(7824612844181266330)
XLA Ops:
  8.9 13.5 %all_gather.10 = bf16[256,512]{1,0:T(8,128)(2,1)} all-gather(bf16[64,512]{1,0:T(8,128)(2,1)S(1)} %convert_element_type.257), channel_id=1, replica_groups=mesh['ctx'=16,'fsdp'=4,'head'=4] {'fsdp'}, dimensions={0}, use_global_device_ids=true | all-gather | bytes 327680 | tf_op jit(solution)/shard_map/all_gather | solution.py:75
  22.4 30.5 %all-gather.3.cloned.1.call-done = bf16[1,512,4096]{2,1,0:T(8,128)(2,1)} async-done(((bf16[1,512,1024]{2,1,0:T(8,128)(2,1)}), bf16[1,512,4096]{2,1,0:T(8,128)(2,1)}) %all-gather.3.cloned.1.call-update) | async-done | bytes 4194320 | tf_op jit(solution)/shard_map/all_gather | solution.py:74
  53.7 2.4 reduce-window.6
  59.4 3.5 %collective-permute-start = (bf16[4,130,128]{2,1,0:T(8,128)(2,1)S(1)}, bf16[4,130,128]{2,1,0:T(8,128)(2,1)}, u32[]{:S(2)}, u32[]{:S(2)}) collective-permute-start(bf16[4,130,128]{2,1,0:T(8,128)(2,1)S(1)} %pad_maximum_fusion.1), channel_id=1, source_target_pairs={{0,16},{16,32},{32,48},{48,64},{64,80},{80,96},{96,112},{112,128},... | collective-permute-start | bytes 399368 | tf_op jit(solution)/shard_map/ppermute | solution.py:31
  62.9 4.5 %collective-permute-start.1 = (bf16[4,130,128]{2,1,0:T(8,128)(2,1)S(1)}, bf16[4,130,128]{2,1,0:T(8,128)(2,1)}, u32[]{:S(2)}, u32[]{:S(2)}) collective-permute-start(bf16[4,130,128]{2,1,0:T(8,128)(2,1)S(1)} %pad_maximum_fusion.1), channel_id=1, source_target_pairs={{0,32},{16,48},{32,64},{48,80},{64,96},{80,112},{96,128},{112,144}... | collective-permute-start | bytes 399368 | tf_op jit(solution)/shard_map/ppermute | solution.py:31
  67.3 4.9 %collective-permute-start.2 = (bf16[4,130,128]{2,1,0:T(8,128)(2,1)S(1)}, bf16[4,130,128]{2,1,0:T(8,128)(2,1)S(1)}, u32[]{:S(2)}, u32[]{:S(2)}) collective-permute-start(bf16[4,130,128]{2,1,0:T(8,128)(2,1)S(1)} %pad_maximum_fusion.1), channel_id=1, source_target_pairs={{0,48},{16,64},{32,80},{48,96},{64,112},{80,128},{96,144},{112,160... | collective-permute-start | bytes 399368 | tf_op jit(solution)/shard_map/ppermute | solution.py:31
  75.9 5.7 %collective-permute-done.1 = bf16[4,130,128]{2,1,0:T(8,128)(2,1)} collective-permute-done((bf16[4,130,128]{2,1,0:T(8,128)(2,1)S(1)}, bf16[4,130,128]{2,1,0:T(8,128)(2,1)}, u32[]{:S(2)}, u32[]{:S(2)}) %collective-permute-start.1) | collective-permute-done | bytes 133152 | tf_op jit(solution)/shard_map/ppermute | solution.py:31
  82.5 9.1 %collective-permute-done.2 = bf16[4,130,128]{2,1,0:T(8,128)(2,1)S(1)} collective-permute-done((bf16[4,130,128]{2,1,0:T(8,128)(2,1)S(1)}, bf16[4,130,128]{2,1,0:T(8,128)(2,1)S(1)}, u32[]{:S(2)}, u32[]{:S(2)}) %collective-permute-start.2) | collective-permute-done | bytes 133152 | tf_op jit(solution)/shard_map/ppermute | solution.py:31
  93.6 3.1 %collective-permute-start.3 = (bf16[4,130,128]{2,1,0:T(8,128)(2,1)S(1)}, bf16[4,130,128]{2,1,0:T(8,128)(2,1)}, u32[]{:S(2)}, u32[]{:S(2)}) collective-permute-start(bf16[4,130,128]{2,1,0:T(8,128)(2,1)S(1)} %pad_maximum_fusion.2), channel_id=1, source_target_pairs={{0,64},{16,80},{32,96},{48,112},{64,128},{80,144},{96,160},{112,17... | collective-permute-start | bytes 399368 | tf_op jit(solution)/shard_map/ppermute | solution.py:31
  101.8 9.6 %collective-permute-done.3 = bf16[4,130,128]{2,1,0:T(8,128)(2,1)} collective-permute-done((bf16[4,130,128]{2,1,0:T(8,128)(2,1)S(1)}, bf16[4,130,128]{2,1,0:T(8,128)(2,1)}, u32[]{:S(2)}, u32[]{:S(2)}) %collective-permute-start.3) | collective-permute-done | bytes 133152 | tf_op jit(solution)/shard_map/ppermute | solution.py:31
  112.3 4.2 %collective-permute-done.4 = bf16[4,130,128]{2,1,0:T(8,128)(2,1)} collective-permute-done((bf16[4,130,128]{2,1,0:T(8,128)(2,1)S(1)}, bf16[4,130,128]{2,1,0:T(8,128)(2,1)}, u32[]{:S(2)}, u32[]{:S(2)}) %collective-permute-start.4) | collective-permute-done | bytes 133152 | tf_op jit(solution)/shard_map/ppermute | solution.py:31
  122.4 6.7 %convolution_convert_fusion = bf16[4096,512]{1,0:T(8,128)(2,1)} fusion(bf16[512,4096]{1,0:T(8,128)(2,1)} %bitcast.143, bf16[64,8,4,128]{3,2,1,0:T(4,128)(2,1)} %bitcast.136), kind=kOutput, calls=%fused_computation | convolution fusion | flops 2149580800 | bytes 8912896 | tf_op jit(solution)/shard_map/td,th->dh/dot_general | solution.py:115
  129.2 22.2 %all-gather.5.cloned.1.call-done = bf16[4096,512]{1,0:T(8,128)(2,1)} async-done(((bf16[256,512]{1,0:T(8,128)(2,1)}), bf16[4096,512]{1,0:T(8,128)(2,1)}) %all-gather.5.cloned.1.call-update) | async-done | bytes 4194320 | tf_op jit(solution)/shard_map/all_gather | solution.py:119
  154.2 5.8 %fusion.87 = f32[512,512]{1,0:T(8,128)S(1)} fusion(bf16[512,4096]{1,0:T(8,128)(2,1)} %bitcast.144, bf16[4096,512]{1,0:T(8,128)(2,1)} %all-gather.5.cloned.1.call-done), kind=kOutput, calls=%fused_computation.175 | convolution fusion | flops 2147483648 | bytes 9437184 | tf_op jit(solution)/shard_map/dot_general | solution.py:121
  164.9 4.7 %collective-permute-start.6 = (bf16[4,130,128]{2,1,0:T(8,128)(2,1)S(1)}, bf16[4,130,128]{2,1,0:T(8,128)(2,1)S(1)}, u32[]{:S(2)}, u32[]{:S(2)}) collective-permute-start(bf16[4,130,128]{2,1,0:T(8,128)(2,1)S(1)} %pad_maximum_fusion), channel_id=1, source_target_pairs={{16,0},{32,16},{48,32},{64,48},{80,64},{96,80},{112,96},{128,112},... | collective-permute-start | bytes 399368 | tf_op jit(solution)/shard_map/ppermute | solution.py:31
  169.6 2.1 collective-permute-start.7
  171.7 4.2 %collective-permute-start.8 = (bf16[4,130,128]{2,1,0:T(8,128)(2,1)S(1)}, bf16[4,130,128]{2,1,0:T(8,128)(2,1)S(1)}, u32[]{:S(2)}, u32[]{:S(2)}) collective-permute-start(bf16[4,130,128]{2,1,0:T(8,128)(2,1)S(1)} %pad_maximum_fusion), channel_id=1, source_target_pairs={{48,0},{64,16},{80,32},{96,48},{112,64},{128,80},{144,96},{160,112... | collective-permute-start | bytes 399368 | tf_op jit(solution)/shard_map/ppermute | solution.py:31
  180.4 7.6 %collective-permute-done.7 = bf16[4,130,128]{2,1,0:T(8,128)(2,1)S(1)} collective-permute-done((bf16[4,130,128]{2,1,0:T(8,128)(2,1)S(1)}, bf16[4,130,128]{2,1,0:T(8,128)(2,1)S(1)}, u32[]{:S(2)}, u32[]{:S(2)}) %collective-permute-start.7) | collective-permute-done | bytes 133152 | tf_op jit(solution)/shard_map/ppermute | solution.py:31
  188.0 3.1 %collective-permute-done.8 = bf16[4,130,128]{2,1,0:T(8,128)(2,1)S(1)} collective-permute-done((bf16[4,130,128]{2,1,0:T(8,128)(2,1)S(1)}, bf16[4,130,128]{2,1,0:T(8,128)(2,1)S(1)}, u32[]{:S(2)}, u32[]{:S(2)}) %collective-permute-start.8) | collective-permute-done | bytes 133152 | tf_op jit(solution)/shard_map/ppermute | solution.py:31
  193.0 2.0 add_convert_fusion.2
  195.1 5.6 %collective-permute-start.9 = (bf16[4,130,128]{2,1,0:T(8,128)(2,1)S(1)}, bf16[4,130,128]{2,1,0:T(8,128)(2,1)}, u32[]{:S(2)}, u32[]{:S(2)}) collective-permute-start(bf16[4,130,128]{2,1,0:T(8,128)(2,1)S(1)} %pad_maximum_fusion.3), channel_id=1, source_target_pairs={{64,0},{80,16},{96,32},{112,48},{128,64},{144,80},{160,96},{176,11... | collective-permute-start | bytes 399368 | tf_op jit(solution)/shard_map/ppermute | solution.py:31
  200.7 2.0 collective-permute-start.10
  211.8 33.1 %reduce-scatter.3.cloned.1.call-done = bf16[256,512]{1,0:T(8,128)(2,1)} async-done(((bf16[4096,512]{1,0:T(8,128)(2,1)}), bf16[256,512]{1,0:T(8,128)(2,1)}) %reduce-scatter.3.cloned.1.call-update) | async-done | bytes 262160 | tf_op jit(solution)/shard_map/reduce_scatter | solution.py:123
  249.8 17.9 %reduce-scatter.5.cloned.1.call-done = bf16[64,512]{1,0:T(8,128)(2,1)} async-done(((bf16[256,512]{1,0:T(8,128)(2,1)}), bf16[64,512]{1,0:T(8,128)(2,1)}) %reduce-scatter.5.cloned.1.call-update) | async-done | bytes 65552 | tf_op jit(solution)/shard_map/reduce_scatter | solution.py:122
  (213 shorter events, 52.8 us)
Async XLA Ops:
  7.2 49.5 %copy-start.15 = (bf16[1,512,512]{2,1,0:T(8,128)(2,1)S(1)}, bf16[1,512,512]{2,1,0:T(8,128)(2,1)}, u32[]{:S(2)}) copy-start(bf16[1,512,512]{2,1,0:T(8,128)(2,1)} %param.12) | copy-start | bytes 1572868
  7.2 49.6 %copy-start.16 = (bf16[1,512,512]{2,1,0:T(8,128)(2,1)S(1)}, bf16[1,512,512]{2,1,0:T(8,128)(2,1)}, u32[]{:S(2)}) copy-start(bf16[1,512,512]{2,1,0:T(8,128)(2,1)} %param.13) | copy-start | bytes 1572868
  7.2 45.7 %all-gather.3.cloned.1.call-start = ((), (), s32[]{:S(2)}) async-start(), calls=%async_computation.2 | async-start | bytes 5242880 | tf_op jit(solution)/shard_map/all_gather | solution.py:74
  7.9 143.4 %all-gather.5.cloned.1.call-start = ((), (), s32[]{:S(2)}) async-start(), calls=%async_computation.3 | async-start | bytes 4456448 | tf_op jit(solution)/shard_map/all_gather | solution.py:119
  53.0 192.0 %reduce-scatter.3.cloned.1.call-start = ((), (), s32[]{:S(2)}) async-start(), calls=%async_computation.4 | async-start | bytes 4456448 | tf_op jit(solution)/shard_map/reduce_scatter | solution.py:123
  57.7 34.9 %copy-start.30 = (f32[4]{0:T(128)}, f32[4]{0:T(128)S(1)}, u32[]{:S(2)}) copy-start(f32[4]{0:T(128)S(1)} %get-tuple-element.18) | copy-start | bytes 52
  57.7 34.9 %copy-start.37 = (f32[4]{0:T(128)}, f32[4]{0:T(128)S(1)}, u32[]{:S(2)}) copy-start(f32[4]{0:T(128)S(1)} %get-tuple-element.15) | copy-start | bytes 52
  59.4 15.6 %collective-permute-start = (bf16[4,130,128]{2,1,0:T(8,128)(2,1)S(1)}, bf16[4,130,128]{2,1,0:T(8,128)(2,1)}, u32[]{:S(2)}, u32[]{:S(2)}) collective-permute-start(bf16[4,130,128]{2,1,0:T(8,128)(2,1)S(1)} %pad_maximum_fusion.1), channel_id=1, source_target_pairs={{0,16},{16,32},{32,48},{48,64},{64,80},{80,96},{96,112},{112,128},... | collective-permute-start | bytes 399368 | tf_op jit(solution)/shard_map/ppermute | solution.py:31
  62.9 18.7 %collective-permute-start.1 = (bf16[4,130,128]{2,1,0:T(8,128)(2,1)S(1)}, bf16[4,130,128]{2,1,0:T(8,128)(2,1)}, u32[]{:S(2)}, u32[]{:S(2)}) collective-permute-start(bf16[4,130,128]{2,1,0:T(8,128)(2,1)S(1)} %pad_maximum_fusion.1), channel_id=1, source_target_pairs={{0,32},{16,48},{32,64},{48,80},{64,96},{80,112},{96,128},{112,144}... | collective-permute-start | bytes 399368 | tf_op jit(solution)/shard_map/ppermute | solution.py:31
  67.3 24.3 %collective-permute-start.2 = (bf16[4,130,128]{2,1,0:T(8,128)(2,1)S(1)}, bf16[4,130,128]{2,1,0:T(8,128)(2,1)S(1)}, u32[]{:S(2)}, u32[]{:S(2)}) collective-permute-start(bf16[4,130,128]{2,1,0:T(8,128)(2,1)S(1)} %pad_maximum_fusion.1), channel_id=1, source_target_pairs={{0,48},{16,64},{32,80},{48,96},{64,112},{80,128},{96,144},{112,160... | collective-permute-start | bytes 399368 | tf_op jit(solution)/shard_map/ppermute | solution.py:31
  72.6 46.7 %copy-start = (bf16[2,256,4,128]{1,3,2,0:T(8,128)(2,1)}, bf16[2,256,4,128]{1,3,2,0:T(8,128)(2,1)S(1)}, u32[]{:S(2)}) copy-start(bf16[2,256,4,128]{1,3,2,0:T(8,128)(2,1)S(1)} %copy.144) | copy-start | bytes 1572868
  93.6 17.8 %collective-permute-start.3 = (bf16[4,130,128]{2,1,0:T(8,128)(2,1)S(1)}, bf16[4,130,128]{2,1,0:T(8,128)(2,1)}, u32[]{:S(2)}, u32[]{:S(2)}) collective-permute-start(bf16[4,130,128]{2,1,0:T(8,128)(2,1)S(1)} %pad_maximum_fusion.2), channel_id=1, source_target_pairs={{0,64},{16,80},{32,96},{48,112},{64,128},{80,144},{96,160},{112,17... | collective-permute-start | bytes 399368 | tf_op jit(solution)/shard_map/ppermute | solution.py:31
  96.7 19.7 %collective-permute-start.4 = (bf16[4,130,128]{2,1,0:T(8,128)(2,1)S(1)}, bf16[4,130,128]{2,1,0:T(8,128)(2,1)}, u32[]{:S(2)}, u32[]{:S(2)}) collective-permute-start(bf16[4,130,128]{2,1,0:T(8,128)(2,1)S(1)} %pad_maximum_fusion.2), channel_id=1, source_target_pairs={{0,128},{16,144},{32,160},{48,176},{64,192},{80,208},{96,224},{112... | collective-permute-start | bytes 399368 | tf_op jit(solution)/shard_map/ppermute | solution.py:31
  98.8 18.8 %collective-permute-start.5 = (bf16[4,130,128]{2,1,0:T(8,128)(2,1)S(1)}, bf16[4,130,128]{2,1,0:T(8,128)(2,1)S(1)}, u32[]{:S(2)}, u32[]{:S(2)}) collective-permute-start(bf16[4,130,128]{2,1,0:T(8,128)(2,1)S(1)} %pad_maximum_fusion.2), channel_id=1, source_target_pairs={{0,192},{16,208},{32,224},{48,240},{1,193},{17,209},{33,225},{49,2... | collective-permute-start | bytes 399368 | tf_op jit(solution)/shard_map/ppermute | solution.py:31
  151.4 116.4 %reduce-scatter.5.cloned.1.call-start = ((), (), s32[]{:S(2)}) async-start(), calls=%async_computation.5 | async-start | bytes 327680 | tf_op jit(solution)/shard_map/reduce_scatter | solution.py:122
  154.2 38.8 %copy-start.34 = (f32[4]{0:T(128)}, f32[4]{0:T(128)S(1)}, u32[]{:S(2)}) copy-start(f32[4]{0:T(128)S(1)} %broadcast_multiply_fusion.1) | copy-start | bytes 52
  164.9 15.4 %collective-permute-start.6 = (bf16[4,130,128]{2,1,0:T(8,128)(2,1)S(1)}, bf16[4,130,128]{2,1,0:T(8,128)(2,1)S(1)}, u32[]{:S(2)}, u32[]{:S(2)}) collective-permute-start(bf16[4,130,128]{2,1,0:T(8,128)(2,1)S(1)} %pad_maximum_fusion), channel_id=1, source_target_pairs={{16,0},{32,16},{48,32},{64,48},{80,64},{96,80},{112,96},{128,112},... | collective-permute-start | bytes 399368 | tf_op jit(solution)/shard_map/ppermute | solution.py:31
  169.6 18.4 %collective-permute-start.7 = (bf16[4,130,128]{2,1,0:T(8,128)(2,1)S(1)}, bf16[4,130,128]{2,1,0:T(8,128)(2,1)S(1)}, u32[]{:S(2)}, u32[]{:S(2)}) collective-permute-start(bf16[4,130,128]{2,1,0:T(8,128)(2,1)S(1)} %pad_maximum_fusion), channel_id=1, source_target_pairs={{32,0},{48,16},{64,32},{80,48},{96,64},{112,80},{128,96},{144,112}... | collective-permute-start | bytes 399368 | tf_op jit(solution)/shard_map/ppermute | solution.py:31
  171.7 19.4 %collective-permute-start.8 = (bf16[4,130,128]{2,1,0:T(8,128)(2,1)S(1)}, bf16[4,130,128]{2,1,0:T(8,128)(2,1)S(1)}, u32[]{:S(2)}, u32[]{:S(2)}) collective-permute-start(bf16[4,130,128]{2,1,0:T(8,128)(2,1)S(1)} %pad_maximum_fusion), channel_id=1, source_target_pairs={{48,0},{64,16},{80,32},{96,48},{112,64},{128,80},{144,96},{160,112... | collective-permute-start | bytes 399368 | tf_op jit(solution)/shard_map/ppermute | solution.py:31
  195.1 12.9 %collective-permute-start.9 = (bf16[4,130,128]{2,1,0:T(8,128)(2,1)S(1)}, bf16[4,130,128]{2,1,0:T(8,128)(2,1)}, u32[]{:S(2)}, u32[]{:S(2)}) collective-permute-start(bf16[4,130,128]{2,1,0:T(8,128)(2,1)S(1)} %pad_maximum_fusion.3), channel_id=1, source_target_pairs={{64,0},{80,16},{96,32},{112,48},{128,64},{144,80},{160,96},{176,11... | collective-permute-start | bytes 399368 | tf_op jit(solution)/shard_map/ppermute | solution.py:31
  200.7 8.2 %collective-permute-start.10 = (bf16[4,130,128]{2,1,0:T(8,128)(2,1)S(1)}, bf16[4,130,128]{2,1,0:T(8,128)(2,1)}, u32[]{:S(2)}, u32[]{:S(2)}) collective-permute-start(bf16[4,130,128]{2,1,0:T(8,128)(2,1)S(1)} %pad_maximum_fusion.3), channel_id=1, source_target_pairs={{128,0},{144,16},{160,32},{176,48},{192,64},{208,80},{224,96},{240... | collective-permute-start | bytes 399368 | tf_op jit(solution)/shard_map/ppermute | solution.py:31
  202.7 8.0 %collective-permute-start.11 = (bf16[4,130,128]{2,1,0:T(8,128)(2,1)S(1)}, bf16[4,130,128]{2,1,0:T(8,128)(2,1)}, u32[]{:S(2)}, u32[]{:S(2)}) collective-permute-start(bf16[4,130,128]{2,1,0:T(8,128)(2,1)S(1)} %pad_maximum_fusion.3), channel_id=1, source_target_pairs={{192,0},{208,16},{224,32},{240,48},{193,1},{209,17},{225,33},{241,... | collective-permute-start | bytes 399368 | tf_op jit(solution)/shard_map/ppermute | solution.py:31
  204.8 40.2 %copy-start.25 = (f32[2,256,4]{1,2,0:T(4,128)S(1)}, f32[2,256,4]{1,2,0:T(4,128)}, u32[]{:S(2)}) copy-start(f32[2,256,4]{1,2,0:T(4,128)} %copy-done.24) | copy-start | bytes 24580
  205.1 39.9 %copy-start.42 = (f32[2,4]{1,0:T(2,128)S(1)}, f32[2,4]{1,0:T(2,128)}, u32[]{:S(2)}) copy-start(f32[2,4]{1,0:T(2,128)} %pad_exponential_fusion) | copy-start | bytes 100
  (40 other events, 479.4 us)
Sparse Core Ops, SparseCore 0:
  9.8 43.0 all-gather.2
  54.7 96.5 all-gather.4
  153.9 91.0 reduce-scatter.2
  247.3 20.3 reduce-scatter.4

commit v7 on v6

--- a/solution.py
+++ b/solution.py
@@ -44,6 +44,19 @@
     for step in (4, 8, 12):
         total = join(total, fetch(window, step))
     return total[1]
+
+
+def gather_features(part, axis):
+    count = lax.axis_size(axis)
+    if count != 4:
+        whole = lax.all_gather(part, axis)
+        return whole
+    place = lax.axis_index(axis)
+    far = lax.ppermute(part, axis, [(i, i ^ 2) for i in range(count)])
+    pair = jnp.stack([part, far])
+    near = lax.ppermute(pair, axis, [(i, i ^ 1) for i in range(count)])
+    stacked = jnp.concatenate([pair[:1], near[:1], pair[1:], near[1:]])
+    return stacked[jnp.arange(count) ^ place]
 
 
 def decay_mask(cumul):
@@ -71,9 +84,8 @@
     head_local = log_decay.shape[2]
     width_local = queries.shape[2]
     blocks = tok_local // SPAN
-    features = lax.all_gather(out_grad, "head", axis=2, tiled=True)[0]
+    features = gather_features(out_grad[0], "head")
     weight_part = lax.all_gather(out_weight.astype(jnp.bfloat16), "fsdp", axis=0, tiled=True)
-    features, weight_part = lax.optimization_barrier((features, weight_part))
     shaped = (blocks, SPAN, head_local, HEAD_DIM)
     query_c = queries.reshape(shaped)
     key_c = keys.reshape(shaped)
@@ -112,13 +124,17 @@
     silu_gate = jax.nn.silu(gate_pre.reshape(shaped).astype(jnp.float32))
     mixed = (normed * silu_gate).astype(jnp.bfloat16).reshape(tok_local, width_local)
     columns = features
-    partial = jnp.einsum("td,th->dh", columns, mixed, preferred_element_type=jnp.float32).astype(
-        jnp.bfloat16
-    )
+    partial = jnp.einsum("ktd,th->kdh", columns, mixed, preferred_element_type=jnp.float32)
+    partial = partial.reshape(-1, partial.shape[2]).astype(jnp.bfloat16)
     weight_full, partial = lax.optimization_barrier(
         (lax.all_gather(weight_part, "ctx", axis=0, tiled=True), partial)
     )
-    mixed_grad = jnp.dot(columns, weight_full, preferred_element_type=jnp.float32)
+    mixed_grad = jnp.einsum(
+        "ktd,kdh->th",
+        columns,
+        weight_full.reshape(columns.shape[0], columns.shape[2], -1),
+        preferred_element_type=jnp.float32,
+    )
     grad_rows = lax.psum_scatter(
         lax.psum_scatter(partial, "ctx", scatter_dimension=0, tiled=True),
         "fsdp",

time: 277 us -> 292 us (1.054)
  waiting for transfers between devices: 146 us -> 121 us
  local copies, waits for them, and re-layouts: 17.1 us -> 41.6 us
  other arithmetic: 22.3 us -> 32.7 us
  starting transfers between devices: 37.9 us -> 42.4 us
    all_gather x1 -> x0, waiting for transfers between devices: 30.5 us -> none  [per_device(): features = lax.all_gather(out_grad, 'head', axis=2, tiled=True)[0]]
    ppermute x0 -> x2, waiting for transfers between devices: none -> 29 us  [the longest x1 29 us: gather_features(): far = lax.ppermute(part, axis, [(i, i ^ 2) for i in range(count)])]
    all_gather x1, waiting for transfers between devices: 22.2 us -> 0.01 us  [per_device(): lax.all_gather(weight_part, 'ctx', axis=0, tiled=True)]
    dot_general x0 -> x2, local copies, waits for them, and re-layouts: none -> 12.6 us  [the longest x1 6.33 us: per_device(): jnp.einsum('ktd,kdh->th', columns, weight_full.reshape(columns.shape[0],...]
    gather x0 -> x1, local copies, waits for them, and re-layouts: none -> 5.1 us  [gather_features(): return stacked[jnp.arange(count) ^ place]]
    concatenate x0 -> x1, other arithmetic: none -> 3.29 us  [gather_features(): stacked = jnp.concatenate([pair[:1], near[:1], pair[1:], near[1:]])]
    reshape x4 -> x2, local copies, waits for them, and re-layouts: 3.03 us -> 0.03 us  [the longest x2 3.01 us: per_device(): normed_grad = mixed_grad.reshape(shaped) * silu_gate]
  transfers between devices with their start and end apart: 16 -> 17, of which waited for: 11 -> 10; matrix products, arithmetic and copies ran while one was open for 22% -> 32% of each run, Pallas kernels for 0% -> 0%
where the time goes in v7:
time: 292 us; the launch traced here: 291 us
  waiting for transfers between devices  121 us (41%)
  starting transfers between devices  42.4 us (15%)
  local copies, waits for them, and re-layouts  41.6 us (14%)
  other arithmetic  32.7 us (11%)
  matrix products  24.3 us (8%)
  between operations  15.3 us (5%)
  blocking collectives  13.5 us (5%)
    ppermute x12, waiting for transfers between devices, fetch(): got = lax.ppermute(packed, axis, pairs).astype(jnp.float32)  40.6 us
    ppermute x12, starting transfers between devices, fetch(): got = lax.ppermute(packed, axis, pairs).astype(jnp.float32)  39.9 us
    reduce_scatter x1, waiting for transfers between devices, per_device(): lax.psum_scatter(partial, 'ctx', scatter_dimension=0, tiled=True)  31.8 us
    ppermute x1, waiting for transfers between devices, gather_features(): far = lax.ppermute(part, axis, [(i, i ^ 2) for i in range(count)])  29 us
    reduce_scatter x1, waiting for transfers between devices, per_device(): lax.psum_scatter(lax.psum_scatter(partial, 'ctx', scatter_dimension=0, ti...  19.2 us
    all_gather x1, blocking collectives, per_device(): lax.all_gather(out_weight.astype(jnp.bfloat16), 'fsdp', axis=0, tiled=True)  13.5 us
    dot_general x1, matrix products, per_device(): jnp.einsum('ktd,th->kdh', columns, mixed, preferred_element_type=jnp.floa...  6.54 us
    dot_general x1, local copies, waits for them, and re-layouts, per_device(): jnp.einsum('ktd,kdh->th', columns, weight_full.reshape(columns.shape[0],...  6.33 us
  transfers between devices with their start and end apart: 17, of which 10 were waited for; matrix products, arithmetic and copies ran while one was open for 32% of the time, Pallas kernels for 0%

profile of v7, /device:TPU:2, one launch (start us, length us, event | category | flops | bytes accessed | tf_op | source)
XLA Modules:
  0.0 290.7 jit_solution(11928070343039282301)
XLA Ops:
  8.3 13.5 %all_gather.6 = bf16[256,512]{1,0:T(8,128)(2,1)} all-gather(bf16[64,512]{1,0:T(8,128)(2,1)S(1)} %convert_element_type.257), channel_id=1, replica_groups=mesh['ctx'=16,'fsdp'=4,'head'=4] {'fsdp'}, dimensions={0}, use_global_device_ids=true | all-gather | bytes 327680 | tf_op jit(solution)/shard_map/all_gather | solution.py:88
  22.6 2.4 reduce-window.6
  30.4 3.8 %collective-permute-start = (bf16[4,130,128]{2,1,0:T(8,128)(2,1)S(1)}, bf16[4,130,128]{2,1,0:T(8,128)(2,1)}, u32[]{:S(2)}, u32[]{:S(2)}) collective-permute-start(bf16[4,130,128]{2,1,0:T(8,128)(2,1)S(1)} %pad_maximum_fusion.3), channel_id=1, source_target_pairs={{0,16},{16,32},{32,48},{48,64},{64,80},{80,96},{96,112},{112,128},... | collective-permute-start | bytes 399368 | tf_op jit(solution)/shard_map/ppermute | solution.py:31
  34.2 5.2 %collective-permute-start.1 = (bf16[4,130,128]{2,1,0:T(8,128)(2,1)S(1)}, bf16[4,130,128]{2,1,0:T(8,128)(2,1)}, u32[]{:S(2)}, u32[]{:S(2)}) collective-permute-start(bf16[4,130,128]{2,1,0:T(8,128)(2,1)S(1)} %pad_maximum_fusion.3), channel_id=1, source_target_pairs={{0,32},{16,48},{32,64},{48,80},{64,96},{80,112},{96,128},{112,144}... | collective-permute-start | bytes 399368 | tf_op jit(solution)/shard_map/ppermute | solution.py:31
  39.4 5.9 %collective-permute-start.2 = (bf16[4,130,128]{2,1,0:T(8,128)(2,1)S(1)}, bf16[4,130,128]{2,1,0:T(8,128)(2,1)}, u32[]{:S(2)}, u32[]{:S(2)}) collective-permute-start(bf16[4,130,128]{2,1,0:T(8,128)(2,1)S(1)} %pad_maximum_fusion.3), channel_id=1, source_target_pairs={{0,48},{16,64},{32,80},{48,96},{64,112},{80,128},{96,144},{112,160... | collective-permute-start | bytes 399368 | tf_op jit(solution)/shard_map/ppermute | solution.py:31
  45.4 2.2 collective-permute-start.6
  58.4 6.4 %collective-permute-done.2 = bf16[4,130,128]{2,1,0:T(8,128)(2,1)} collective-permute-done((bf16[4,130,128]{2,1,0:T(8,128)(2,1)S(1)}, bf16[4,130,128]{2,1,0:T(8,128)(2,1)}, u32[]{:S(2)}, u32[]{:S(2)}) %collective-permute-start.2) | collective-permute-done | bytes 133152 | tf_op jit(solution)/shard_map/ppermute | solution.py:31
  66.7 29.0 %collective-permute-done.6 = bf16[512,1024]{1,0:T(8,128)(2,1)} collective-permute-done((bf16[512,1024]{1,0:T(8,128)(2,1)S(1)}, bf16[512,1024]{1,0:T(8,128)(2,1)}, u32[]{:S(2)}, u32[]{:S(2)}) %collective-permute-start.6) | collective-permute-done | bytes 1048608 | tf_op jit(solution)/shard_map/ppermute | solution.py:55
  95.7 2.8 pad_maximum_fusion.1
  110.4 4.5 %collective-permute-done.3 = bf16[4,130,128]{2,1,0:T(8,128)(2,1)} collective-permute-done((bf16[4,130,128]{2,1,0:T(8,128)(2,1)S(1)}, bf16[4,130,128]{2,1,0:T(8,128)(2,1)}, u32[]{:S(2)}, u32[]{:S(2)}) %collective-permute-start.3) | collective-permute-done | bytes 133152 | tf_op jit(solution)/shard_map/ppermute | solution.py:31
  115.8 11.8 %collective-permute-done.4 = bf16[4,130,128]{2,1,0:T(8,128)(2,1)S(1)} collective-permute-done((bf16[4,130,128]{2,1,0:T(8,128)(2,1)S(1)}, bf16[4,130,128]{2,1,0:T(8,128)(2,1)S(1)}, u32[]{:S(2)}, u32[]{:S(2)}) %collective-permute-start.4) | collective-permute-done | bytes 133152 | tf_op jit(solution)/shard_map/ppermute | solution.py:31
  136.4 3.3 %pad_maximum_fusion = bf16[4,512,1024]{2,1,0:T(8,128)(2,1)} fusion(bf16[1,512,1024]{2,1,0:T(8,128)(2,1)S(1)} %get-tuple-element.36, bf16[1,512,1024]{2,1,0:T(8,128)(2,1)} %bitcast.8, bf16[1,512,1024]{2,1,0:T(8,128)(2,1)S(1)} %get-tuple-element.35, bf16[1,512,1024]{2,1,0:T(8,128)(2,1)S(1)} %copy-done.5), kind=kLoop, calls=%fused_computation.2 | loop fusion | flops 6291456 | bytes 8388608 | tf_op jit(solution)/shard_map/concatenate | solution.py:58
  139.6 5.1 %gather_fusion = bf16[4,512,1024]{2,1,0:T(8,128)(2,1)} fusion(bf16[4,512,1024]{2,1,0:T(8,128)(2,1)} %pad_maximum_fusion, s32[1024]{0:T(1024)} %pad_clamp_fusion), kind=kCustom, calls=%fused_computation | custom fusion | bytes 8388624 | tf_op jit(solution)/shard_map/gather | solution.py:59
  144.7 6.3 %copy.179 = bf16[4,1024,512]{2,1,0:T(8,128)(2,1)} copy(bf16[4,1024,512]{1,2,0:T(8,128)(2,1)} %bitcast.162) | data formatting | bytes 8388608 | tf_op jit(solution)/shard_map/ktd,th->kdh/dot_general | solution.py:127
  151.0 6.5 %convolution_convert_fusion = bf16[4096,512]{1,0:T(8,128)(2,1)} fusion(bf16[4096,512]{1,0:T(8,128)(2,1)} %bitcast.166, bf16[64,8,4,128]{3,2,1,0:T(4,128)(2,1)S(1)} %bitcast.168), kind=kOutput, calls=%fused_computation.1 | convolution fusion | flops 2149580800 | bytes 8912896 | tf_op jit(solution)/shard_map/ktd,th->kdh/dot_general | solution.py:127
  160.6 6.3 %copy.183 = bf16[512,1024,4]{1,0,2:T(8,128)(2,1)} copy(bf16[512,1024,4]{0,1,2:T(8,128)(2,1)} %bitcast.164) | data formatting | bytes 8388608 | tf_op jit(solution)/shard_map/ktd,kdh->th/dot_general | solution.py:132
  166.9 6.2 %multiply_reduce_fusion = (f32[2,256,4]{1,2,0:T(4,128)S(1)}, f32[2,256,4,128]{1,3,2,0:T(8,128)S(1)}) fusion(f32[2,256,4,128]{1,3,2,0:T(8,128)S(1)} %get-tuple-element.47, f32[2,256,4]{1,2,0:T(4,128)S(1)} %add_rsqrt_fusion, f32[2,256,4,128]{1,3,2,0:T(8,128)} %copy.181, bf16[4,128,1024,4]{2,1,0,3:T(8,128)(2,1)} %bitcast.165, ...), kind=kOutput, calls=%fused_computation.34 | convolution fusion | flops 2149578752 | bytes 11550720 | tf_op jit(solution)/shard_map/ktd,kdh->th/dot_general | solution.py:132
  177.8 7.0 %collective-permute-start.10 = (bf16[4,130,128]{2,1,0:T(8,128)(2,1)S(1)}, bf16[4,130,128]{2,1,0:T(8,128)(2,1)S(1)}, u32[]{:S(2)}, u32[]{:S(2)}) collective-permute-start(bf16[4,130,128]{2,1,0:T(8,128)(2,1)S(1)} %pad_maximum_fusion.2), channel_id=1, source_target_pairs={{48,0},{64,16},{80,32},{96,48},{112,64},{128,80},{144,96},{160,112... | collective-permute-start | bytes 399368 | tf_op jit(solution)/shard_map/ppermute | solution.py:31
  188.5 3.0 %collective-permute-done.9 = bf16[4,130,128]{2,1,0:T(8,128)(2,1)S(1)} collective-permute-done((bf16[4,130,128]{2,1,0:T(8,128)(2,1)S(1)}, bf16[4,130,128]{2,1,0:T(8,128)(2,1)S(1)}, u32[]{:S(2)}, u32[]{:S(2)}) %collective-permute-start.9) | collective-permute-done | bytes 133152 | tf_op jit(solution)/shard_map/ppermute | solution.py:31
  191.5 8.6 %collective-permute-done.10 = bf16[4,130,128]{2,1,0:T(8,128)(2,1)S(1)} collective-permute-done((bf16[4,130,128]{2,1,0:T(8,128)(2,1)S(1)}, bf16[4,130,128]{2,1,0:T(8,128)(2,1)S(1)}, u32[]{:S(2)}, u32[]{:S(2)}) %collective-permute-start.10) | collective-permute-done | bytes 133152 | tf_op jit(solution)/shard_map/ppermute | solution.py:31
  203.5 6.3 %collective-permute-start.11 = (bf16[4,130,128]{2,1,0:T(8,128)(2,1)S(1)}, bf16[4,130,128]{2,1,0:T(8,128)(2,1)}, u32[]{:S(2)}, u32[]{:S(2)}) collective-permute-start(bf16[4,130,128]{2,1,0:T(8,128)(2,1)S(1)} %pad_maximum_fusion.5), channel_id=1, source_target_pairs={{64,0},{80,16},{96,32},{112,48},{128,64},{144,80},{160,96},{176,11... | collective-permute-start | bytes 399368 | tf_op jit(solution)/shard_map/ppermute | solution.py:31
  217.1 4.2 %collective-permute-done.11 = bf16[4,130,128]{2,1,0:T(8,128)(2,1)} collective-permute-done((bf16[4,130,128]{2,1,0:T(8,128)(2,1)S(1)}, bf16[4,130,128]{2,1,0:T(8,128)(2,1)}, u32[]{:S(2)}, u32[]{:S(2)}) %collective-permute-start.11) | collective-permute-done | bytes 133152 | tf_op jit(solution)/shard_map/ppermute | solution.py:31
  225.7 31.8 %reduce-scatter.3.cloned.1.call-done = bf16[256,512]{1,0:T(8,128)(2,1)} async-done(((bf16[4096,512]{1,0:T(8,128)(2,1)}), bf16[256,512]{1,0:T(8,128)(2,1)}) %reduce-scatter.3.cloned.1.call-update) | async-done | bytes 262160 | tf_op jit(solution)/shard_map/reduce_scatter | solution.py:139
  263.2 19.2 %reduce-scatter.5.cloned.1.call-done = bf16[64,512]{1,0:T(8,128)(2,1)} async-done(((bf16[256,512]{1,0:T(8,128)(2,1)}), bf16[64,512]{1,0:T(8,128)(2,1)}) %reduce-scatter.5.cloned.1.call-update) | async-done | bytes 65552 | tf_op jit(solution)/shard_map/reduce_scatter | solution.py:138
  (217 shorter events, 74.0 us)
Async XLA Ops:
  7.2 38.2 %copy-start.4 = (bf16[1,512,1024]{2,1,0:T(8,128)(2,1)S(1)}, bf16[1,512,1024]{2,1,0:T(8,128)(2,1)}, u32[]{:S(2)}) copy-start(bf16[1,512,1024]{2,1,0:T(8,128)(2,1)} %param.16) | copy-start | bytes 3145732
  7.2 40.4 %copy-start.14 = (bf16[1,512,512]{2,1,0:T(8,128)(2,1)S(1)}, bf16[1,512,512]{2,1,0:T(8,128)(2,1)}, u32[]{:S(2)}) copy-start(bf16[1,512,512]{2,1,0:T(8,128)(2,1)} %param.11) | copy-start | bytes 1572868
  7.2 150.4 %all-gather.2.cloned.1.call-start = ((), (), s32[]{:S(2)}) async-start(), calls=%async_computation.2 | async-start | bytes 4456448 | tf_op jit(solution)/shard_map/all_gather | solution.py:130
  21.8 235.8 %reduce-scatter.3.cloned.1.call-start = ((), (), s32[]{:S(2)}) async-start(), calls=%async_computation.3 | async-start | bytes 4456448 | tf_op jit(solution)/shard_map/reduce_scatter | solution.py:139
  30.4 24.0 %collective-permute-start = (bf16[4,130,128]{2,1,0:T(8,128)(2,1)S(1)}, bf16[4,130,128]{2,1,0:T(8,128)(2,1)}, u32[]{:S(2)}, u32[]{:S(2)}) collective-permute-start(bf16[4,130,128]{2,1,0:T(8,128)(2,1)S(1)} %pad_maximum_fusion.3), channel_id=1, source_target_pairs={{0,16},{16,32},{32,48},{48,64},{64,80},{80,96},{96,112},{112,128},... | collective-permute-start | bytes 399368 | tf_op jit(solution)/shard_map/ppermute | solution.py:31
  34.2 23.3 %collective-permute-start.1 = (bf16[4,130,128]{2,1,0:T(8,128)(2,1)S(1)}, bf16[4,130,128]{2,1,0:T(8,128)(2,1)}, u32[]{:S(2)}, u32[]{:S(2)}) collective-permute-start(bf16[4,130,128]{2,1,0:T(8,128)(2,1)S(1)} %pad_maximum_fusion.3), channel_id=1, source_target_pairs={{0,32},{16,48},{32,64},{48,80},{64,96},{80,112},{96,128},{112,144}... | collective-permute-start | bytes 399368 | tf_op jit(solution)/shard_map/ppermute | solution.py:31
  39.4 25.5 %collective-permute-start.2 = (bf16[4,130,128]{2,1,0:T(8,128)(2,1)S(1)}, bf16[4,130,128]{2,1,0:T(8,128)(2,1)}, u32[]{:S(2)}, u32[]{:S(2)}) collective-permute-start(bf16[4,130,128]{2,1,0:T(8,128)(2,1)S(1)} %pad_maximum_fusion.3), channel_id=1, source_target_pairs={{0,48},{16,64},{32,80},{48,96},{64,112},{80,128},{96,144},{112,160... | collective-permute-start | bytes 399368 | tf_op jit(solution)/shard_map/ppermute | solution.py:31
  45.4 50.3 %collective-permute-start.6 = (bf16[512,1024]{1,0:T(8,128)(2,1)S(1)}, bf16[512,1024]{1,0:T(8,128)(2,1)}, u32[]{:S(2)}, u32[]{:S(2)}) collective-permute-start(bf16[512,1024]{1,0:T(8,128)(2,1)S(1)} %bitcast.167), channel_id=1, source_target_pairs={{0,2},{1,3},{2,0},{3,1},{4,6},{5,7},{6,4},{7,5},{8,10},{9,11},{10,... | collective-permute-start | bytes 3145736 | tf_op jit(solution)/shard_map/ppermute | solution.py:55
  53.8 44.7 %copy-start.28 = (f32[4]{0:T(128)S(1)}, f32[4]{0:T(128)}, u32[]{:S(2)}) copy-start(f32[4]{0:T(128)} %copy-done.27) | copy-start | bytes 52
  55.3 40.4 %copy-start.8 = (f32[4,130,128]{2,1,0:T(8,128)}, f32[4,130,128]{2,1,0:T(8,128)S(1)}, u32[]{:S(2)}) copy-start(f32[4,130,128]{2,1,0:T(8,128)S(1)} %convert_element_type.247) | copy-start | bytes 798724
  98.5 36.0 %collective-permute-start.7 = (bf16[2,512,1024]{2,1,0:T(8,128)(2,1)}, bf16[2,512,1024]{2,1,0:T(8,128)(2,1)}, u32[]{:S(2)}, u32[]{:S(2)}) collective-permute-start(bf16[2,512,1024]{2,1,0:T(8,128)(2,1)} %pad_maximum_fusion.1), channel_id=1, source_target_pairs={{0,1},{1,0},{2,3},{3,2},{4,5},{5,4},{6,7},{7,6},{8,9},{9,8},{10,11... | collective-permute-start | bytes 6291464 | tf_op jit(solution)/shard_map/ppermute | solution.py:57
  100.7 14.1 %collective-permute-start.3 = (bf16[4,130,128]{2,1,0:T(8,128)(2,1)S(1)}, bf16[4,130,128]{2,1,0:T(8,128)(2,1)}, u32[]{:S(2)}, u32[]{:S(2)}) collective-permute-start(bf16[4,130,128]{2,1,0:T(8,128)(2,1)S(1)} %pad_maximum_fusion.4), channel_id=1, source_target_pairs={{0,64},{16,80},{32,96},{48,112},{64,128},{80,144},{96,160},{112,17... | collective-permute-start | bytes 399368 | tf_op jit(solution)/shard_map/ppermute | solution.py:31
  102.7 24.9 %collective-permute-start.4 = (bf16[4,130,128]{2,1,0:T(8,128)(2,1)S(1)}, bf16[4,130,128]{2,1,0:T(8,128)(2,1)S(1)}, u32[]{:S(2)}, u32[]{:S(2)}) collective-permute-start(bf16[4,130,128]{2,1,0:T(8,128)(2,1)S(1)} %pad_maximum_fusion.4), channel_id=1, source_target_pairs={{0,128},{16,144},{32,160},{48,176},{64,192},{80,208},{96,224},{112... | collective-permute-start | bytes 399368 | tf_op jit(solution)/shard_map/ppermute | solution.py:31
  105.2 23.2 %collective-permute-start.5 = (bf16[4,130,128]{2,1,0:T(8,128)(2,1)S(1)}, bf16[4,130,128]{2,1,0:T(8,128)(2,1)}, u32[]{:S(2)}, u32[]{:S(2)}) collective-permute-start(bf16[4,130,128]{2,1,0:T(8,128)(2,1)S(1)} %pad_maximum_fusion.4), channel_id=1, source_target_pairs={{0,192},{16,208},{32,224},{48,240},{1,193},{17,209},{33,225},{49,2... | collective-permute-start | bytes 399368 | tf_op jit(solution)/shard_map/ppermute | solution.py:31
  157.6 124.8 %reduce-scatter.5.cloned.1.call-start = ((), (), s32[]{:S(2)}) async-start(), calls=%async_computation.4 | async-start | bytes 327680 | tf_op jit(solution)/shard_map/reduce_scatter | solution.py:138
  160.6 41.0 %copy-start.33 = (f32[4]{0:T(128)}, f32[4]{0:T(128)S(1)}, u32[]{:S(2)}) copy-start(f32[4]{0:T(128)S(1)} %broadcast_multiply_fusion.1) | copy-start | bytes 52
  174.0 14.5 %collective-permute-start.8 = (bf16[4,130,128]{2,1,0:T(8,128)(2,1)S(1)}, bf16[4,130,128]{2,1,0:T(8,128)(2,1)S(1)}, u32[]{:S(2)}, u32[]{:S(2)}) collective-permute-start(bf16[4,130,128]{2,1,0:T(8,128)(2,1)S(1)} %pad_maximum_fusion.2), channel_id=1, source_target_pairs={{16,0},{32,16},{48,32},{64,48},{80,64},{96,80},{112,96},{128,112},... | collective-permute-start | bytes 399368 | tf_op jit(solution)/shard_map/ppermute | solution.py:31
  175.9 15.6 %collective-permute-start.9 = (bf16[4,130,128]{2,1,0:T(8,128)(2,1)S(1)}, bf16[4,130,128]{2,1,0:T(8,128)(2,1)S(1)}, u32[]{:S(2)}, u32[]{:S(2)}) collective-permute-start(bf16[4,130,128]{2,1,0:T(8,128)(2,1)S(1)} %pad_maximum_fusion.2), channel_id=1, source_target_pairs={{32,0},{48,16},{64,32},{80,48},{96,64},{112,80},{128,96},{144,112}... | collective-permute-start | bytes 399368 | tf_op jit(solution)/shard_map/ppermute | solution.py:31
  177.8 22.3 %collective-permute-start.10 = (bf16[4,130,128]{2,1,0:T(8,128)(2,1)S(1)}, bf16[4,130,128]{2,1,0:T(8,128)(2,1)S(1)}, u32[]{:S(2)}, u32[]{:S(2)}) collective-permute-start(bf16[4,130,128]{2,1,0:T(8,128)(2,1)S(1)} %pad_maximum_fusion.2), channel_id=1, source_target_pairs={{48,0},{64,16},{80,32},{96,48},{112,64},{128,80},{144,96},{160,112... | collective-permute-start | bytes 399368 | tf_op jit(solution)/shard_map/ppermute | solution.py:31
  188.4 69.2 %copy-start.22 = (f32[2,256,4]{1,2,0:T(4,128)S(1)}, f32[2,256,4]{1,2,0:T(4,128)}, u32[]{:S(2)}) copy-start(f32[2,256,4]{1,2,0:T(4,128)} %copy-done.21) | copy-start | bytes 24580
  203.5 17.7 %collective-permute-start.11 = (bf16[4,130,128]{2,1,0:T(8,128)(2,1)S(1)}, bf16[4,130,128]{2,1,0:T(8,128)(2,1)}, u32[]{:S(2)}, u32[]{:S(2)}) collective-permute-start(bf16[4,130,128]{2,1,0:T(8,128)(2,1)S(1)} %pad_maximum_fusion.5), channel_id=1, source_target_pairs={{64,0},{80,16},{96,32},{112,48},{128,64},{144,80},{160,96},{176,11... | collective-permute-start | bytes 399368 | tf_op jit(solution)/shard_map/ppermute | solution.py:31
  209.9 12.3 %collective-permute-start.12 = (bf16[4,130,128]{2,1,0:T(8,128)(2,1)S(1)}, bf16[4,130,128]{2,1,0:T(8,128)(2,1)}, u32[]{:S(2)}, u32[]{:S(2)}) collective-permute-start(bf16[4,130,128]{2,1,0:T(8,128)(2,1)S(1)} %pad_maximum_fusion.5), channel_id=1, source_target_pairs={{128,0},{144,16},{160,32},{176,48},{192,64},{208,80},{224,96},{240... | collective-permute-start | bytes 399368 | tf_op jit(solution)/shard_map/ppermute | solution.py:31
  211.9 12.0 %collective-permute-start.13 = (bf16[4,130,128]{2,1,0:T(8,128)(2,1)S(1)}, bf16[4,130,128]{2,1,0:T(8,128)(2,1)}, u32[]{:S(2)}, u32[]{:S(2)}) collective-permute-start(bf16[4,130,128]{2,1,0:T(8,128)(2,1)S(1)} %pad_maximum_fusion.5), channel_id=1, source_target_pairs={{192,0},{208,16},{224,32},{240,48},{193,1},{209,17},{225,33},{241,... | collective-permute-start | bytes 399368 | tf_op jit(solution)/shard_map/ppermute | solution.py:31
  214.9 45.5 %copy-start = (f32[2,256,4,128]{3,1,2,0:T(8,128)S(1)}, f32[2,256,4,128]{3,1,2,0:T(8,128)}, u32[]{:S(2)}) copy-start(f32[2,256,4,128]{3,1,2,0:T(8,128)} %convolution_bitcast_fusion.5) | copy-start | bytes 3145732
  (40 other events, 593.5 us)
Sparse Core Ops, SparseCore 0:
  21.9 94.9 all-gather.1
  157.7 99.7 reduce-scatter.2
  260.1 22.2 reduce-scatter.4

commit v8 on v6

--- a/solution.py
+++ b/solution.py
@@ -119,12 +119,11 @@
         (lax.all_gather(weight_part, "ctx", axis=0, tiled=True), partial)
     )
     mixed_grad = jnp.dot(columns, weight_full, preferred_element_type=jnp.float32)
-    grad_rows = lax.psum_scatter(
-        lax.psum_scatter(partial, "ctx", scatter_dimension=0, tiled=True),
-        "fsdp",
-        scatter_dimension=0,
-        tiled=True,
-    ).astype(jnp.float32)
+    by_ctx = lax.psum_scatter(partial, "ctx", scatter_dimension=0, tiled=True)
+    spread = lax.axis_size("fsdp")
+    grad_rows = lax.all_to_all(
+        by_ctx.reshape(spread, -1, by_ctx.shape[1]), "fsdp", 0, 0, tiled=False
+    ).astype(jnp.float32).sum(0)
     normed_grad = mixed_grad.reshape(shaped) * silu_gate
     inner = jnp.mean(normed_grad * normed, axis=-1, keepdims=True)
     attn_grad = (inverse * (normed_grad - normed * inner)).astype(jnp.bfloat16)

time: 277 us -> 264 us (0.953)
  waiting for transfers between devices: 146 us -> 129 us
  starting transfers between devices: 37.9 us -> 42 us
    reduce_scatter x2 -> x1, waiting for transfers between devices: 51 us -> 29.8 us  [per_device(): by_ctx = lax.psum_scatter(partial, 'ctx', scatter_dimension=0, tiled=True)]
    all_to_all x0 -> x1, waiting for transfers between devices: none -> 4.83 us  [per_device(): lax.all_to_all(by_ctx.reshape(spread, -1, by_ctx.shape[1]), 'fsdp', 0, 0,...]
    all_to_all x0 -> x1, starting transfers between devices: none -> 4.18 us  [per_device(): lax.all_to_all(by_ctx.reshape(spread, -1, by_ctx.shape[1]), 'fsdp', 0, 0,...]
  transfers between devices with their start and end apart: 16 -> 16, of which waited for: 11 -> 11; matrix products, arithmetic and copies ran while one was open for 22% -> 23% of each run, Pallas kernels for 0% -> 0%
where the time goes in v8:
time: 264 us; the launch traced here: 263 us
  waiting for transfers between devices  129 us (49%)
  starting transfers between devices  42 us (16%)
  matrix products  24.2 us (9%)
  other arithmetic  21.4 us (8%)
  local copies, waits for them, and re-layouts  17.1 us (6%)
  between operations  15.4 us (6%)
  blocking collectives  13.5 us (5%)
    ppermute x12, waiting for transfers between devices, fetch(): got = lax.ppermute(packed, axis, pairs).astype(jnp.float32)  41.5 us
    ppermute x12, starting transfers between devices, fetch(): got = lax.ppermute(packed, axis, pairs).astype(jnp.float32)  37.7 us
    all_gather x1, waiting for transfers between devices, per_device(): features = lax.all_gather(out_grad, 'head', axis=2, tiled=True)[0]  30.5 us
    reduce_scatter x1, waiting for transfers between devices, per_device(): by_ctx = lax.psum_scatter(partial, 'ctx', scatter_dimension=0, tiled=True)  29.8 us
    all_gather x1, waiting for transfers between devices, per_device(): lax.all_gather(weight_part, 'ctx', axis=0, tiled=True)  22.2 us
    all_gather x1, blocking collectives, per_device(): lax.all_gather(out_weight.astype(jnp.bfloat16), 'fsdp', axis=0, tiled=True)  13.5 us
    dot_general x1, matrix products, per_device(): jnp.einsum('td,th->dh', columns, mixed, preferred_element_type=jnp.float32)  6.72 us
    dot_general x1, matrix products, per_device(): jnp.dot(columns, weight_full, preferred_element_type=jnp.float32)  5.79 us
  transfers between devices with their start and end apart: 16, of which 11 were waited for; matrix products, arithmetic and copies ran while one was open for 23% of the time, Pallas kernels for 0%

profile of v8, /device:TPU:2, one launch (start us, length us, event | category | flops | bytes accessed | tf_op | source)
XLA Modules:
  0.0 263.2 jit_solution(6281591934825513890)
XLA Ops:
  8.9 13.5 %all_gather.10 = bf16[256,512]{1,0:T(8,128)(2,1)} all-gather(bf16[64,512]{1,0:T(8,128)(2,1)S(1)} %convert_element_type.257), channel_id=1, replica_groups=mesh['ctx'=16,'fsdp'=4,'head'=4] {'fsdp'}, dimensions={0}, use_global_device_ids=true | all-gather | bytes 327680 | tf_op jit(solution)/shard_map/all_gather | solution.py:75
  22.4 30.5 %all-gather.3.cloned.1.call-done = bf16[1,512,4096]{2,1,0:T(8,128)(2,1)} async-done(((bf16[1,512,1024]{2,1,0:T(8,128)(2,1)}), bf16[1,512,4096]{2,1,0:T(8,128)(2,1)}) %all-gather.3.cloned.1.call-update) | async-done | bytes 4194320 | tf_op jit(solution)/shard_map/all_gather | solution.py:74
  53.7 2.4 reduce-window.6
  59.4 3.5 %collective-permute-start = (bf16[4,130,128]{2,1,0:T(8,128)(2,1)S(1)}, bf16[4,130,128]{2,1,0:T(8,128)(2,1)}, u32[]{:S(2)}, u32[]{:S(2)}) collective-permute-start(bf16[4,130,128]{2,1,0:T(8,128)(2,1)S(1)} %pad_maximum_fusion.1), channel_id=1, source_target_pairs={{0,16},{16,32},{32,48},{48,64},{64,80},{80,96},{96,112},{112,128},... | collective-permute-start | bytes 399368 | tf_op jit(solution)/shard_map/ppermute | solution.py:31
  62.9 4.5 %collective-permute-start.1 = (bf16[4,130,128]{2,1,0:T(8,128)(2,1)S(1)}, bf16[4,130,128]{2,1,0:T(8,128)(2,1)}, u32[]{:S(2)}, u32[]{:S(2)}) collective-permute-start(bf16[4,130,128]{2,1,0:T(8,128)(2,1)S(1)} %pad_maximum_fusion.1), channel_id=1, source_target_pairs={{0,32},{16,48},{32,64},{48,80},{64,96},{80,112},{96,128},{112,144}... | collective-permute-start | bytes 399368 | tf_op jit(solution)/shard_map/ppermute | solution.py:31
  67.3 4.9 %collective-permute-start.2 = (bf16[4,130,128]{2,1,0:T(8,128)(2,1)S(1)}, bf16[4,130,128]{2,1,0:T(8,128)(2,1)S(1)}, u32[]{:S(2)}, u32[]{:S(2)}) collective-permute-start(bf16[4,130,128]{2,1,0:T(8,128)(2,1)S(1)} %pad_maximum_fusion.1), channel_id=1, source_target_pairs={{0,48},{16,64},{32,80},{48,96},{64,112},{80,128},{96,144},{112,160... | collective-permute-start | bytes 399368 | tf_op jit(solution)/shard_map/ppermute | solution.py:31
  75.9 5.7 %collective-permute-done.1 = bf16[4,130,128]{2,1,0:T(8,128)(2,1)} collective-permute-done((bf16[4,130,128]{2,1,0:T(8,128)(2,1)S(1)}, bf16[4,130,128]{2,1,0:T(8,128)(2,1)}, u32[]{:S(2)}, u32[]{:S(2)}) %collective-permute-start.1) | collective-permute-done | bytes 133152 | tf_op jit(solution)/shard_map/ppermute | solution.py:31
  82.5 9.1 %collective-permute-done.2 = bf16[4,130,128]{2,1,0:T(8,128)(2,1)S(1)} collective-permute-done((bf16[4,130,128]{2,1,0:T(8,128)(2,1)S(1)}, bf16[4,130,128]{2,1,0:T(8,128)(2,1)S(1)}, u32[]{:S(2)}, u32[]{:S(2)}) %collective-permute-start.2) | collective-permute-done | bytes 133152 | tf_op jit(solution)/shard_map/ppermute | solution.py:31
  93.6 3.1 %collective-permute-start.3 = (bf16[4,130,128]{2,1,0:T(8,128)(2,1)S(1)}, bf16[4,130,128]{2,1,0:T(8,128)(2,1)}, u32[]{:S(2)}, u32[]{:S(2)}) collective-permute-start(bf16[4,130,128]{2,1,0:T(8,128)(2,1)S(1)} %pad_maximum_fusion.2), channel_id=1, source_target_pairs={{0,64},{16,80},{32,96},{48,112},{64,128},{80,144},{96,160},{112,17... | collective-permute-start | bytes 399368 | tf_op jit(solution)/shard_map/ppermute | solution.py:31
  101.8 9.6 %collective-permute-done.3 = bf16[4,130,128]{2,1,0:T(8,128)(2,1)} collective-permute-done((bf16[4,130,128]{2,1,0:T(8,128)(2,1)S(1)}, bf16[4,130,128]{2,1,0:T(8,128)(2,1)}, u32[]{:S(2)}, u32[]{:S(2)}) %collective-permute-start.3) | collective-permute-done | bytes 133152 | tf_op jit(solution)/shard_map/ppermute | solution.py:31
  112.3 4.2 %collective-permute-done.4 = bf16[4,130,128]{2,1,0:T(8,128)(2,1)} collective-permute-done((bf16[4,130,128]{2,1,0:T(8,128)(2,1)S(1)}, bf16[4,130,128]{2,1,0:T(8,128)(2,1)}, u32[]{:S(2)}, u32[]{:S(2)}) %collective-permute-start.4) | collective-permute-done | bytes 133152 | tf_op jit(solution)/shard_map/ppermute | solution.py:31
  122.4 6.7 %convolution_convert_fusion = bf16[4096,512]{1,0:T(8,128)(2,1)} fusion(bf16[512,4096]{1,0:T(8,128)(2,1)} %bitcast.145, bf16[64,8,4,128]{3,2,1,0:T(4,128)(2,1)} %bitcast.137), kind=kOutput, calls=%fused_computation | convolution fusion | flops 2149580800 | bytes 8912896 | tf_op jit(solution)/shard_map/td,th->dh/dot_general | solution.py:115
  129.2 22.2 %all-gather.5.cloned.1.call-done = bf16[4096,512]{1,0:T(8,128)(2,1)} async-done(((bf16[256,512]{1,0:T(8,128)(2,1)}), bf16[4096,512]{1,0:T(8,128)(2,1)}) %all-gather.5.cloned.1.call-update) | async-done | bytes 4194320 | tf_op jit(solution)/shard_map/all_gather | solution.py:119
  154.2 5.8 %fusion.84 = f32[512,512]{1,0:T(8,128)S(1)} fusion(bf16[512,4096]{1,0:T(8,128)(2,1)} %bitcast.146, bf16[4096,512]{1,0:T(8,128)(2,1)} %all-gather.5.cloned.1.call-done), kind=kOutput, calls=%fused_computation.172 | convolution fusion | flops 2147483648 | bytes 9437184 | tf_op jit(solution)/shard_map/dot_general | solution.py:121
  164.9 4.7 %collective-permute-start.6 = (bf16[4,130,128]{2,1,0:T(8,128)(2,1)S(1)}, bf16[4,130,128]{2,1,0:T(8,128)(2,1)S(1)}, u32[]{:S(2)}, u32[]{:S(2)}) collective-permute-start(bf16[4,130,128]{2,1,0:T(8,128)(2,1)S(1)} %pad_maximum_fusion), channel_id=1, source_target_pairs={{16,0},{32,16},{48,32},{64,48},{80,64},{96,80},{112,96},{128,112},... | collective-permute-start | bytes 399368 | tf_op jit(solution)/shard_map/ppermute | solution.py:31
  169.6 2.1 collective-permute-start.7
  171.7 4.2 %collective-permute-start.8 = (bf16[4,130,128]{2,1,0:T(8,128)(2,1)S(1)}, bf16[4,130,128]{2,1,0:T(8,128)(2,1)S(1)}, u32[]{:S(2)}, u32[]{:S(2)}) collective-permute-start(bf16[4,130,128]{2,1,0:T(8,128)(2,1)S(1)} %pad_maximum_fusion), channel_id=1, source_target_pairs={{48,0},{64,16},{80,32},{96,48},{112,64},{128,80},{144,96},{160,112... | collective-permute-start | bytes 399368 | tf_op jit(solution)/shard_map/ppermute | solution.py:31
  180.3 7.5 %collective-permute-done.7 = bf16[4,130,128]{2,1,0:T(8,128)(2,1)S(1)} collective-permute-done((bf16[4,130,128]{2,1,0:T(8,128)(2,1)S(1)}, bf16[4,130,128]{2,1,0:T(8,128)(2,1)S(1)}, u32[]{:S(2)}, u32[]{:S(2)}) %collective-permute-start.7) | collective-permute-done | bytes 133152 | tf_op jit(solution)/shard_map/ppermute | solution.py:31
  187.9 3.2 %collective-permute-done.8 = bf16[4,130,128]{2,1,0:T(8,128)(2,1)S(1)} collective-permute-done((bf16[4,130,128]{2,1,0:T(8,128)(2,1)S(1)}, bf16[4,130,128]{2,1,0:T(8,128)(2,1)S(1)}, u32[]{:S(2)}, u32[]{:S(2)}) %collective-permute-start.8) | collective-permute-done | bytes 133152 | tf_op jit(solution)/shard_map/ppermute | solution.py:31
  195.1 5.6 %collective-permute-start.9 = (bf16[4,130,128]{2,1,0:T(8,128)(2,1)S(1)}, bf16[4,130,128]{2,1,0:T(8,128)(2,1)}, u32[]{:S(2)}, u32[]{:S(2)}) collective-permute-start(bf16[4,130,128]{2,1,0:T(8,128)(2,1)S(1)} %pad_maximum_fusion.3), channel_id=1, source_target_pairs={{64,0},{80,16},{96,32},{112,48},{128,64},{144,80},{160,96},{176,11... | collective-permute-start | bytes 399368 | tf_op jit(solution)/shard_map/ppermute | solution.py:31
  206.0 2.2 collective-permute-done.9
  215.1 29.8 %reduce-scatter.2.cloned.1.call-done = bf16[256,512]{1,0:T(8,128)(2,1)} async-done(((bf16[4096,512]{1,0:T(8,128)(2,1)}), bf16[256,512]{1,0:T(8,128)(2,1)}) %reduce-scatter.2.cloned.1.call-update) | async-done | bytes 262160 | tf_op jit(solution)/shard_map/reduce_scatter | solution.py:122
  244.9 4.2 %all-to-all-start = ((bf16[4,64,512]{2,1,0:T(8,128)(2,1)}), bf16[4,64,512]{2,1,0:T(8,128)(2,1)S(1)}, u32[]{:S(2)}, u32[]{:S(2)}) async-start(bf16[4,64,512]{2,1,0:T(8,128)(2,1)} %bitcast.138), calls=%async_computation.1 | async-start | bytes 524288 | tf_op jit(solution)/shard_map/all_to_all | solution.py:124
  250.9 4.8 %all-to-all-done = bf16[4,64,512]{2,1,0:T(8,128)(2,1)S(1)} async-done(((bf16[4,64,512]{2,1,0:T(8,128)(2,1)}), bf16[4,64,512]{2,1,0:T(8,128)(2,1)S(1)}, u32[]{:S(2)}, u32[]{:S(2)}) %all-to-all-start) | async-done | bytes 262176 | tf_op jit(solution)/shard_map/all_to_all | solution.py:124
  (215 shorter events, 54.0 us)
Async XLA Ops:
  7.2 49.5 %copy-start.16 = (bf16[1,512,512]{2,1,0:T(8,128)(2,1)S(1)}, bf16[1,512,512]{2,1,0:T(8,128)(2,1)}, u32[]{:S(2)}) copy-start(bf16[1,512,512]{2,1,0:T(8,128)(2,1)} %param.12) | copy-start | bytes 1572868
  7.2 49.6 %copy-start.17 = (bf16[1,512,512]{2,1,0:T(8,128)(2,1)S(1)}, bf16[1,512,512]{2,1,0:T(8,128)(2,1)}, u32[]{:S(2)}) copy-start(bf16[1,512,512]{2,1,0:T(8,128)(2,1)} %param.13) | copy-start | bytes 1572868
  7.2 45.7 %all-gather.3.cloned.1.call-start = ((), (), s32[]{:S(2)}) async-start(), calls=%async_computation.2 | async-start | bytes 5242880 | tf_op jit(solution)/shard_map/all_gather | solution.py:74
  7.9 143.4 %all-gather.5.cloned.1.call-start = ((), (), s32[]{:S(2)}) async-start(), calls=%async_computation.3 | async-start | bytes 4456448 | tf_op jit(solution)/shard_map/all_gather | solution.py:119
  53.0 191.9 %reduce-scatter.2.cloned.1.call-start = ((), (), s32[]{:S(2)}) async-start(), calls=%async_computation.4 | async-start | bytes 4456448 | tf_op jit(solution)/shard_map/reduce_scatter | solution.py:122
  57.7 34.9 %copy-start.30 = (f32[4]{0:T(128)}, f32[4]{0:T(128)S(1)}, u32[]{:S(2)}) copy-start(f32[4]{0:T(128)S(1)} %get-tuple-element.18) | copy-start | bytes 52
  57.7 34.9 %copy-start.37 = (f32[4]{0:T(128)}, f32[4]{0:T(128)S(1)}, u32[]{:S(2)}) copy-start(f32[4]{0:T(128)S(1)} %get-tuple-element.15) | copy-start | bytes 52
  58.0 34.6 %copy-start.33 = (f32[4]{0:T(128)}, f32[4]{0:T(128)S(1)}, u32[]{:S(2)}) copy-start(f32[4]{0:T(128)S(1)} %broadcast_multiply_fusion.2) | copy-start | bytes 52
  59.4 15.6 %collective-permute-start = (bf16[4,130,128]{2,1,0:T(8,128)(2,1)S(1)}, bf16[4,130,128]{2,1,0:T(8,128)(2,1)}, u32[]{:S(2)}, u32[]{:S(2)}) collective-permute-start(bf16[4,130,128]{2,1,0:T(8,128)(2,1)S(1)} %pad_maximum_fusion.1), channel_id=1, source_target_pairs={{0,16},{16,32},{32,48},{48,64},{64,80},{80,96},{96,112},{112,128},... | collective-permute-start | bytes 399368 | tf_op jit(solution)/shard_map/ppermute | solution.py:31
  62.9 18.7 %collective-permute-start.1 = (bf16[4,130,128]{2,1,0:T(8,128)(2,1)S(1)}, bf16[4,130,128]{2,1,0:T(8,128)(2,1)}, u32[]{:S(2)}, u32[]{:S(2)}) collective-permute-start(bf16[4,130,128]{2,1,0:T(8,128)(2,1)S(1)} %pad_maximum_fusion.1), channel_id=1, source_target_pairs={{0,32},{16,48},{32,64},{48,80},{64,96},{80,112},{96,128},{112,144}... | collective-permute-start | bytes 399368 | tf_op jit(solution)/shard_map/ppermute | solution.py:31
  67.3 24.3 %collective-permute-start.2 = (bf16[4,130,128]{2,1,0:T(8,128)(2,1)S(1)}, bf16[4,130,128]{2,1,0:T(8,128)(2,1)S(1)}, u32[]{:S(2)}, u32[]{:S(2)}) collective-permute-start(bf16[4,130,128]{2,1,0:T(8,128)(2,1)S(1)} %pad_maximum_fusion.1), channel_id=1, source_target_pairs={{0,48},{16,64},{32,80},{48,96},{64,112},{80,128},{96,144},{112,160... | collective-permute-start | bytes 399368 | tf_op jit(solution)/shard_map/ppermute | solution.py:31
  72.6 46.7 %copy-start = (bf16[2,256,4,128]{1,3,2,0:T(8,128)(2,1)}, bf16[2,256,4,128]{1,3,2,0:T(8,128)(2,1)S(1)}, u32[]{:S(2)}) copy-start(bf16[2,256,4,128]{1,3,2,0:T(8,128)(2,1)S(1)} %copy.144) | copy-start | bytes 1572868
  93.6 17.8 %collective-permute-start.3 = (bf16[4,130,128]{2,1,0:T(8,128)(2,1)S(1)}, bf16[4,130,128]{2,1,0:T(8,128)(2,1)}, u32[]{:S(2)}, u32[]{:S(2)}) collective-permute-start(bf16[4,130,128]{2,1,0:T(8,128)(2,1)S(1)} %pad_maximum_fusion.2), channel_id=1, source_target_pairs={{0,64},{16,80},{32,96},{48,112},{64,128},{80,144},{96,160},{112,17... | collective-permute-start | bytes 399368 | tf_op jit(solution)/shard_map/ppermute | solution.py:31
  96.7 19.7 %collective-permute-start.4 = (bf16[4,130,128]{2,1,0:T(8,128)(2,1)S(1)}, bf16[4,130,128]{2,1,0:T(8,128)(2,1)}, u32[]{:S(2)}, u32[]{:S(2)}) collective-permute-start(bf16[4,130,128]{2,1,0:T(8,128)(2,1)S(1)} %pad_maximum_fusion.2), channel_id=1, source_target_pairs={{0,128},{16,144},{32,160},{48,176},{64,192},{80,208},{96,224},{112... | collective-permute-start | bytes 399368 | tf_op jit(solution)/shard_map/ppermute | solution.py:31
  98.8 18.8 %collective-permute-start.5 = (bf16[4,130,128]{2,1,0:T(8,128)(2,1)S(1)}, bf16[4,130,128]{2,1,0:T(8,128)(2,1)S(1)}, u32[]{:S(2)}, u32[]{:S(2)}) collective-permute-start(bf16[4,130,128]{2,1,0:T(8,128)(2,1)S(1)} %pad_maximum_fusion.2), channel_id=1, source_target_pairs={{0,192},{16,208},{32,224},{48,240},{1,193},{17,209},{33,225},{49,2... | collective-permute-start | bytes 399368 | tf_op jit(solution)/shard_map/ppermute | solution.py:31
  154.2 38.8 %copy-start.34 = (f32[4]{0:T(128)}, f32[4]{0:T(128)S(1)}, u32[]{:S(2)}) copy-start(f32[4]{0:T(128)S(1)} %broadcast_multiply_fusion.1) | copy-start | bytes 52
  164.9 15.4 %collective-permute-start.6 = (bf16[4,130,128]{2,1,0:T(8,128)(2,1)S(1)}, bf16[4,130,128]{2,1,0:T(8,128)(2,1)S(1)}, u32[]{:S(2)}, u32[]{:S(2)}) collective-permute-start(bf16[4,130,128]{2,1,0:T(8,128)(2,1)S(1)} %pad_maximum_fusion), channel_id=1, source_target_pairs={{16,0},{32,16},{48,32},{64,48},{80,64},{96,80},{112,96},{128,112},... | collective-permute-start | bytes 399368 | tf_op jit(solution)/shard_map/ppermute | solution.py:31
  169.6 18.3 %collective-permute-start.7 = (bf16[4,130,128]{2,1,0:T(8,128)(2,1)S(1)}, bf16[4,130,128]{2,1,0:T(8,128)(2,1)S(1)}, u32[]{:S(2)}, u32[]{:S(2)}) collective-permute-start(bf16[4,130,128]{2,1,0:T(8,128)(2,1)S(1)} %pad_maximum_fusion), channel_id=1, source_target_pairs={{32,0},{48,16},{64,32},{80,48},{96,64},{112,80},{128,96},{144,112}... | collective-permute-start | bytes 399368 | tf_op jit(solution)/shard_map/ppermute | solution.py:31
  171.7 19.5 %collective-permute-start.8 = (bf16[4,130,128]{2,1,0:T(8,128)(2,1)S(1)}, bf16[4,130,128]{2,1,0:T(8,128)(2,1)S(1)}, u32[]{:S(2)}, u32[]{:S(2)}) collective-permute-start(bf16[4,130,128]{2,1,0:T(8,128)(2,1)S(1)} %pad_maximum_fusion), channel_id=1, source_target_pairs={{48,0},{64,16},{80,32},{96,48},{112,64},{128,80},{144,96},{160,112... | collective-permute-start | bytes 399368 | tf_op jit(solution)/shard_map/ppermute | solution.py:31
  195.1 13.1 %collective-permute-start.9 = (bf16[4,130,128]{2,1,0:T(8,128)(2,1)S(1)}, bf16[4,130,128]{2,1,0:T(8,128)(2,1)}, u32[]{:S(2)}, u32[]{:S(2)}) collective-permute-start(bf16[4,130,128]{2,1,0:T(8,128)(2,1)S(1)} %pad_maximum_fusion.3), channel_id=1, source_target_pairs={{64,0},{80,16},{96,32},{112,48},{128,64},{144,80},{160,96},{176,11... | collective-permute-start | bytes 399368 | tf_op jit(solution)/shard_map/ppermute | solution.py:31
  200.7 8.5 %collective-permute-start.10 = (bf16[4,130,128]{2,1,0:T(8,128)(2,1)S(1)}, bf16[4,130,128]{2,1,0:T(8,128)(2,1)}, u32[]{:S(2)}, u32[]{:S(2)}) collective-permute-start(bf16[4,130,128]{2,1,0:T(8,128)(2,1)S(1)} %pad_maximum_fusion.3), channel_id=1, source_target_pairs={{128,0},{144,16},{160,32},{176,48},{192,64},{208,80},{224,96},{240... | collective-permute-start | bytes 399368 | tf_op jit(solution)/shard_map/ppermute | solution.py:31
  202.6 8.3 %collective-permute-start.11 = (bf16[4,130,128]{2,1,0:T(8,128)(2,1)S(1)}, bf16[4,130,128]{2,1,0:T(8,128)(2,1)}, u32[]{:S(2)}, u32[]{:S(2)}) collective-permute-start(bf16[4,130,128]{2,1,0:T(8,128)(2,1)S(1)} %pad_maximum_fusion.3), channel_id=1, source_target_pairs={{192,0},{208,16},{224,32},{240,48},{193,1},{209,17},{225,33},{241,... | collective-permute-start | bytes 399368 | tf_op jit(solution)/shard_map/ppermute | solution.py:31
  212.0 37.0 %copy-start.43 = (f32[2,4]{1,0:T(2,128)S(1)}, f32[2,4]{1,0:T(2,128)}, u32[]{:S(2)}) copy-start(f32[2,4]{1,0:T(2,128)} %pad_exponential_fusion) | copy-start | bytes 100
  244.9 10.9 %all-to-all-start = ((bf16[4,64,512]{2,1,0:T(8,128)(2,1)}), bf16[4,64,512]{2,1,0:T(8,128)(2,1)S(1)}, u32[]{:S(2)}, u32[]{:S(2)}) async-start(bf16[4,64,512]{2,1,0:T(8,128)(2,1)} %bitcast.138), calls=%async_computation.1 | async-start | bytes 524288 | tf_op jit(solution)/shard_map/all_to_all | solution.py:124
  (41 other events, 393.8 us)
Sparse Core Ops, SparseCore 0:
  9.8 43.0 all-gather.2
  54.7 96.5 all-gather.4
  153.9 90.9 reduce-scatter.1

commit v9 on v8

--- a/solution.py
+++ b/solution.py
@@ -37,12 +37,11 @@
 
     own = (gain, state)
     identity = (jnp.ones_like(gain), jnp.zeros_like(state))
-    near = [fetch(own, step) for step in (1, 2, 3)]
-    inner = join(join(near[0], near[1]), near[2])
-    window = join(own, inner)
-    total = inner
-    for step in (4, 8, 12):
-        total = join(total, fetch(window, step))
+    total = fetch(own, 1)
+    step = 1
+    while step < count:
+        total = join(total, fetch(total, step))
+        step *= 2
     return total[1]
 
 

time: 264 us -> 245 us (0.928)
  waiting for transfers between devices: 129 us -> 103 us
  matrix products: 24.2 us -> 28.6 us
  local copies, waits for them, and re-layouts: 17.1 us -> 20.9 us
    ppermute x12 -> x10, waiting for transfers between devices: 41.5 us -> 64.9 us  [fetch(): got = lax.ppermute(packed, axis, pairs).astype(jnp.float32)]
    reduce_scatter x1, waiting for transfers between devices: 29.8 us -> 6.81 us  [per_device(): by_ctx = lax.psum_scatter(partial, 'ctx', scatter_dimension=0, tiled=True)]
    all_gather x1, waiting for transfers between devices: 22.2 us -> 1.96 us  [per_device(): lax.all_gather(weight_part, 'ctx', axis=0, tiled=True)]
    all_gather x1, waiting for transfers between devices: 30.5 us -> 23.7 us  [per_device(): features = lax.all_gather(out_grad, 'head', axis=2, tiled=True)[0]]
    convert_element_type x10 -> x8, other arithmetic: 5.65 us -> 1.97 us  [fetch(): got = lax.ppermute(packed, axis, pairs).astype(jnp.float32)]
    ppermute x12 -> x10, starting transfers between devices: 37.7 us -> 35.8 us  [fetch(): got = lax.ppermute(packed, axis, pairs).astype(jnp.float32)]
  transfers between devices with their start and end apart: 16 -> 14, of which waited for: 11 -> 14; matrix products, arithmetic and copies ran while one was open for 23% -> 27% of each run, Pallas kernels for 0% -> 0%
where the time goes in v9:
time: 245 us; the launch traced here: 244 us
  waiting for transfers between devices  103 us (42%)
  starting transfers between devices  41.2 us (17%)
  matrix products  28.6 us (12%)
  local copies, waits for them, and re-layouts  20.9 us (9%)
  other arithmetic  20.9 us (9%)
  between operations  15.5 us (6%)
  blocking collectives  13.6 us (6%)
    ppermute x10, waiting for transfers between devices, fetch(): got = lax.ppermute(packed, axis, pairs).astype(jnp.float32)  64.9 us
    ppermute x10, starting transfers between devices, fetch(): got = lax.ppermute(packed, axis, pairs).astype(jnp.float32)  35.8 us
    all_gather x1, waiting for transfers between devices, per_device(): features = lax.all_gather(out_grad, 'head', axis=2, tiled=True)[0]  23.7 us
    all_gather x1, blocking collectives, per_device(): lax.all_gather(out_weight.astype(jnp.bfloat16), 'fsdp', axis=0, tiled=True)  13.6 us
    reduce_scatter x1, waiting for transfers between devices, per_device(): by_ctx = lax.psum_scatter(partial, 'ctx', scatter_dimension=0, tiled=True)  6.81 us
    dot_general x1, matrix products, per_device(): jnp.einsum('td,th->dh', columns, mixed, preferred_element_type=jnp.float32)  6.67 us
    dot_general x1, matrix products, per_device(): jnp.dot(columns, weight_full, preferred_element_type=jnp.float32)  5.79 us
    all_to_all x1, starting transfers between devices, per_device(): lax.all_to_all(by_ctx.reshape(spread, -1, by_ctx.shape[1]), 'fsdp', 0, 0,...  5.28 us
  transfers between devices with their start and end apart: 14, of which 14 were waited for; matrix products, arithmetic and copies ran while one was open for 27% of the time, Pallas kernels for 0%

profile of v9, /device:TPU:2, one launch (start us, length us, event | category | flops | bytes accessed | tf_op | source)
XLA Modules:
  0.0 243.7 jit_solution(13641520011217762746)
XLA Ops:
  13.0 13.6 %all_gather.10 = bf16[256,512]{1,0:T(8,128)(2,1)} all-gather(bf16[64,512]{1,0:T(8,128)(2,1)S(1)} %convert_element_type.452), channel_id=1, replica_groups=mesh['ctx'=16,'fsdp'=4,'head'=4] {'fsdp'}, dimensions={0}, use_global_device_ids=true | all-gather | bytes 327680 | tf_op jit(solution)/shard_map/all_gather | solution.py:74
  29.2 23.7 %all-gather.3.cloned.1.call-done = bf16[1,512,4096]{2,1,0:T(8,128)(2,1)} async-done(((bf16[1,512,1024]{2,1,0:T(8,128)(2,1)}), bf16[1,512,4096]{2,1,0:T(8,128)(2,1)}) %all-gather.3.cloned.1.call-update) | async-done | bytes 4194320 | tf_op jit(solution)/shard_map/all_gather | solution.py:73
  54.0 3.5 %collective-permute-start = (bf16[4,130,128]{2,1,0:T(8,128)(2,1)}, bf16[4,130,128]{2,1,0:T(8,128)(2,1)}, u32[]{:S(2)}, u32[]{:S(2)}) collective-permute-start(bf16[4,130,128]{2,1,0:T(8,128)(2,1)} %pad_maximum_fusion.1), channel_id=1, source_target_pairs={{0,16},{16,32},{32,48},{48,64},{64,80},{80,96},{96,112},{112,128},... | collective-permute-start | bytes 399368 | tf_op jit(solution)/shard_map/ppermute | solution.py:31
  60.4 4.1 %collective-permute-done = bf16[4,130,128]{2,1,0:T(8,128)(2,1)} collective-permute-done((bf16[4,130,128]{2,1,0:T(8,128)(2,1)}, bf16[4,130,128]{2,1,0:T(8,128)(2,1)}, u32[]{:S(2)}, u32[]{:S(2)}) %collective-permute-start) | collective-permute-done | bytes 133152 | tf_op jit(solution)/shard_map/ppermute | solution.py:31
  68.2 9.9 %collective-permute-done.1 = bf16[4,130,128]{2,1,0:T(8,128)(2,1)S(1)} collective-permute-done((bf16[4,130,128]{2,1,0:T(8,128)(2,1)S(1)}, bf16[4,130,128]{2,1,0:T(8,128)(2,1)S(1)}, u32[]{:S(2)}, u32[]{:S(2)}) %collective-permute-start.1) | collective-permute-done | bytes 133152 | tf_op jit(solution)/shard_map/ppermute | solution.py:31
  81.1 12.6 %collective-permute-done.2 = bf16[4,130,128]{2,1,0:T(8,128)(2,1)S(1)} collective-permute-done((bf16[4,130,128]{2,1,0:T(8,128)(2,1)S(1)}, bf16[4,130,128]{2,1,0:T(8,128)(2,1)S(1)}, u32[]{:S(2)}, u32[]{:S(2)}) %collective-permute-start.2) | collective-permute-done | bytes 133152 | tf_op jit(solution)/shard_map/ppermute | solution.py:31
  94.2 4.2 %collective-permute-start.3 = (bf16[4,130,128]{2,1,0:T(8,128)(2,1)S(1)}, bf16[4,130,128]{2,1,0:T(8,128)(2,1)S(1)}, u32[]{:S(2)}, u32[]{:S(2)}) collective-permute-start(bf16[4,130,128]{2,1,0:T(8,128)(2,1)S(1)} %pad_maximum_fusion.4), channel_id=1, source_target_pairs={{0,64},{16,80},{32,96},{48,112},{64,128},{80,144},{96,160},{112,17... | collective-permute-start | bytes 399368 | tf_op jit(solution)/shard_map/ppermute | solution.py:31
  98.9 11.4 %collective-permute-done.3 = bf16[4,130,128]{2,1,0:T(8,128)(2,1)S(1)} collective-permute-done((bf16[4,130,128]{2,1,0:T(8,128)(2,1)S(1)}, bf16[4,130,128]{2,1,0:T(8,128)(2,1)S(1)}, u32[]{:S(2)}, u32[]{:S(2)}) %collective-permute-start.3) | collective-permute-done | bytes 133152 | tf_op jit(solution)/shard_map/ppermute | solution.py:31
  116.7 9.3 %collective-permute-done.4 = bf16[4,130,128]{2,1,0:T(8,128)(2,1)} collective-permute-done((bf16[4,130,128]{2,1,0:T(8,128)(2,1)S(1)}, bf16[4,130,128]{2,1,0:T(8,128)(2,1)}, u32[]{:S(2)}, u32[]{:S(2)}) %collective-permute-start.4) | collective-permute-done | bytes 133152 | tf_op jit(solution)/shard_map/ppermute | solution.py:31
  130.3 6.7 %convolution_convert_fusion = bf16[4096,512]{1,0:T(8,128)(2,1)} fusion(bf16[512,4096]{1,0:T(8,128)(2,1)} %bitcast.181, bf16[64,8,4,128]{3,2,1,0:T(4,128)(2,1)} %bitcast.173), kind=kOutput, calls=%fused_computation | convolution fusion | flops 2149580800 | bytes 8912896 | tf_op jit(solution)/shard_map/td,th->dh/dot_general | solution.py:114
  138.9 5.8 %fusion.76 = f32[512,512]{1,0:T(8,128)S(1)} fusion(bf16[512,4096]{1,0:T(8,128)(2,1)} %bitcast.182, bf16[4096,512]{1,0:T(8,128)(2,1)} %all-gather.5.cloned.1.call-done), kind=kOutput, calls=%fused_computation.190 | convolution fusion | flops 2147483648 | bytes 9437184 | tf_op jit(solution)/shard_map/dot_general | solution.py:120
  149.5 4.0 %collective-permute-start.5 = (bf16[4,130,128]{2,1,0:T(8,128)(2,1)S(1)}, bf16[4,130,128]{2,1,0:T(8,128)(2,1)S(1)}, u32[]{:S(2)}, u32[]{:S(2)}) collective-permute-start(bf16[4,130,128]{2,1,0:T(8,128)(2,1)S(1)} %pad_maximum_fusion), channel_id=1, source_target_pairs={{16,0},{32,16},{48,32},{64,48},{80,64},{96,80},{112,96},{128,112},... | collective-permute-start | bytes 399368 | tf_op jit(solution)/shard_map/ppermute | solution.py:31
  155.8 3.8 %collective-permute-done.5 = bf16[4,130,128]{2,1,0:T(8,128)(2,1)S(1)} collective-permute-done((bf16[4,130,128]{2,1,0:T(8,128)(2,1)S(1)}, bf16[4,130,128]{2,1,0:T(8,128)(2,1)S(1)}, u32[]{:S(2)}, u32[]{:S(2)}) %collective-permute-start.5) | collective-permute-done | bytes 133152 | tf_op jit(solution)/shard_map/ppermute | solution.py:31
  160.3 3.7 %collective-permute-start.6 = (bf16[4,130,128]{2,1,0:T(8,128)(2,1)S(1)}, bf16[4,130,128]{2,1,0:T(8,128)(2,1)S(1)}, u32[]{:S(2)}, u32[]{:S(2)}) collective-permute-start(bf16[4,130,128]{2,1,0:T(8,128)(2,1)S(1)} %pad_maximum_fusion.6), channel_id=1, source_target_pairs={{16,0},{32,16},{48,32},{64,48},{80,64},{96,80},{112,96},{128,112},... | collective-permute-start | bytes 399368 | tf_op jit(solution)/shard_map/ppermute | solution.py:31
  164.1 2.7 %convolution_bitcast_fusion.5 = f32[2,256,4,128]{3,1,2,0:T(8,128)} fusion(bf16[2,4,256,256]{3,2,1,0:T(8,128)(2,1)} %multiply_convert_fusion, bf16[2,256,4,128]{1,3,2,0:T(8,128)(2,1)S(1)} %copy-done.4), kind=kOutput, calls=%fused_computation.17 | convolution fusion | flops 134217728 | bytes 2621440 | tf_op jit(solution)/shard_map/chtu,cthe->cuhe/dot_general | solution.py:132
  172.3 4.7 %collective-permute-start.7 = (bf16[4,130,128]{2,1,0:T(8,128)(2,1)S(1)}, bf16[4,130,128]{2,1,0:T(8,128)(2,1)S(1)}, u32[]{:S(2)}, u32[]{:S(2)}) collective-permute-start(bf16[4,130,128]{2,1,0:T(8,128)(2,1)S(1)} %pad_maximum_fusion.7), channel_id=1, source_target_pairs={{32,0},{48,16},{64,32},{80,48},{96,64},{112,80},{128,96},{144,112}... | collective-permute-start | bytes 399368 | tf_op jit(solution)/shard_map/ppermute | solution.py:31
  177.0 2.7 %convolution_bitcast_fusion.6 = f32[2,256,4,128]{1,3,2,0:T(8,128)} fusion(bf16[2,4,256,256]{3,2,1,0:T(8,128)(2,1)} %multiply_convert_fusion, bf16[2,256,4,128]{3,2,1,0:T(4,128)(2,1)S(1)} %copy-done.8), kind=kOutput, calls=%fused_computation.18 | convolution fusion | flops 134217728 | bytes 2621440 | tf_op jit(solution)/shard_map/chtu,cuhe->cthe/dot_general | solution.py:131
  179.7 4.8 %collective-permute-done.7 = bf16[4,130,128]{2,1,0:T(8,128)(2,1)S(1)} collective-permute-done((bf16[4,130,128]{2,1,0:T(8,128)(2,1)S(1)}, bf16[4,130,128]{2,1,0:T(8,128)(2,1)S(1)}, u32[]{:S(2)}, u32[]{:S(2)}) %collective-permute-start.7) | collective-permute-done | bytes 133152 | tf_op jit(solution)/shard_map/ppermute | solution.py:31
  189.6 8.1 %collective-permute-start.8 = (bf16[4,130,128]{2,1,0:T(8,128)(2,1)}, bf16[4,130,128]{2,1,0:T(8,128)(2,1)}, u32[]{:S(2)}, u32[]{:S(2)}) collective-permute-start(bf16[4,130,128]{2,1,0:T(8,128)(2,1)} %pad_maximum_fusion.8), channel_id=1, source_target_pairs={{64,0},{80,16},{96,32},{112,48},{128,64},{144,80},{160,96},{176,11... | collective-permute-start | bytes 399368 | tf_op jit(solution)/shard_map/ppermute | solution.py:31
  207.3 2.5 %collective-permute-start.9 = (bf16[4,130,128]{2,1,0:T(8,128)(2,1)S(1)}, bf16[4,130,128]{2,1,0:T(8,128)(2,1)S(1)}, u32[]{:S(2)}, u32[]{:S(2)}) collective-permute-start(bf16[4,130,128]{2,1,0:T(8,128)(2,1)S(1)} %pad_maximum_fusion.9), channel_id=1, source_target_pairs={{128,0},{144,16},{160,32},{176,48},{192,64},{208,80},{224,96},{240... | collective-permute-start | bytes 399368 | tf_op jit(solution)/shard_map/ppermute | solution.py:31
  209.9 5.6 %collective-permute-done.9 = bf16[4,130,128]{2,1,0:T(8,128)(2,1)S(1)} collective-permute-done((bf16[4,130,128]{2,1,0:T(8,128)(2,1)S(1)}, bf16[4,130,128]{2,1,0:T(8,128)(2,1)S(1)}, u32[]{:S(2)}, u32[]{:S(2)}) %collective-permute-start.9) | collective-permute-done | bytes 133152 | tf_op jit(solution)/shard_map/ppermute | solution.py:31
  217.4 6.8 %reduce-scatter.2.cloned.1.call-done = bf16[256,512]{1,0:T(8,128)(2,1)} async-done(((bf16[4096,512]{1,0:T(8,128)(2,1)}), bf16[256,512]{1,0:T(8,128)(2,1)}) %reduce-scatter.2.cloned.1.call-update) | async-done | bytes 262160 | tf_op jit(solution)/shard_map/reduce_scatter | solution.py:121
  224.2 5.3 %all-to-all-start = ((bf16[4,64,512]{2,1,0:T(8,128)(2,1)}), bf16[4,64,512]{2,1,0:T(8,128)(2,1)S(1)}, u32[]{:S(2)}, u32[]{:S(2)}) async-start(bf16[4,64,512]{2,1,0:T(8,128)(2,1)} %bitcast.174), calls=%async_computation.1 | async-start | bytes 524288 | tf_op jit(solution)/shard_map/all_to_all | solution.py:123
  231.4 4.8 %all-to-all-done = bf16[4,64,512]{2,1,0:T(8,128)(2,1)S(1)} async-done(((bf16[4,64,512]{2,1,0:T(8,128)(2,1)}), bf16[4,64,512]{2,1,0:T(8,128)(2,1)S(1)}, u32[]{:S(2)}, u32[]{:S(2)}) %all-to-all-start) | async-done | bytes 262176 | tf_op jit(solution)/shard_map/all_to_all | solution.py:123
  (249 shorter events, 63.6 us)
Async XLA Ops:
  7.2 45.7 %all-gather.3.cloned.1.call-start = ((), (), s32[]{:S(2)}) async-start(), calls=%async_computation.2 | async-start | bytes 5242880 | tf_op jit(solution)/shard_map/all_gather | solution.py:73
  7.9 131.0 %all-gather.5.cloned.1.call-start = ((), (), s32[]{:S(2)}) async-start(), calls=%async_computation.3 | async-start | bytes 4456448 | tf_op jit(solution)/shard_map/all_gather | solution.py:118
  11.6 46.4 %copy-start.24 = (f32[2,4,256]{2,1,0:T(4,128)}, f32[2,4,256]{2,1,0:T(4,128)S(1)}, u32[]{:S(2)}) copy-start(f32[2,4,256]{2,1,0:T(4,128)S(1)} %reduce_window_sum.24) | copy-start | bytes 24580
  12.8 45.2 %copy-start.7 = (bf16[2,256,4,128]{3,2,1,0:T(4,128)(2,1)}, bf16[2,256,4,128]{3,2,1,0:T(4,128)(2,1)S(1)}, u32[]{:S(2)}) copy-start(bf16[2,256,4,128]{3,2,1,0:T(4,128)(2,1)S(1)} %reshape.764) | copy-start | bytes 1572868
  12.8 44.7 %copy-start.17 = (bf16[1,512,512]{2,1,0:T(8,128)(2,1)S(1)}, bf16[1,512,512]{2,1,0:T(8,128)(2,1)}, u32[]{:S(2)}) copy-start(bf16[1,512,512]{2,1,0:T(8,128)(2,1)} %param.11) | copy-start | bytes 1572868
  12.9 45.8 %copy-start.5 = (bf16[2,256,4,128]{3,2,1,0:T(4,128)(2,1)}, bf16[2,256,4,128]{3,2,1,0:T(4,128)(2,1)S(1)}, u32[]{:S(2)}) copy-start(bf16[2,256,4,128]{3,2,1,0:T(4,128)(2,1)S(1)} %reshape.768) | copy-start | bytes 1572868
  27.6 30.4 %copy-start.39 = (f32[4]{0:T(128)}, f32[4]{0:T(128)S(1)}, u32[]{:S(2)}) copy-start(f32[4]{0:T(128)S(1)} %get-tuple-element.15) | copy-start | bytes 52
  28.1 25.1 %copy-start.35 = (f32[4]{0:T(128)}, f32[4]{0:T(128)S(1)}, u32[]{:S(2)}) copy-start(f32[4]{0:T(128)S(1)} %broadcast_multiply_fusion.2) | copy-start | bytes 52
  28.1 25.0 %copy-start.22 = (f32[2,256,4]{1,2,0:T(4,128)}, f32[2,256,4]{1,2,0:T(4,128)S(1)}, u32[]{:S(2)}) copy-start(f32[2,256,4]{1,2,0:T(4,128)S(1)} %get-tuple-element.54) | copy-start | bytes 24580
  53.0 171.3 %reduce-scatter.2.cloned.1.call-start = ((), (), s32[]{:S(2)}) async-start(), calls=%async_computation.4 | async-start | bytes 4456448 | tf_op jit(solution)/shard_map/reduce_scatter | solution.py:121
  54.0 10.5 %collective-permute-start = (bf16[4,130,128]{2,1,0:T(8,128)(2,1)}, bf16[4,130,128]{2,1,0:T(8,128)(2,1)}, u32[]{:S(2)}, u32[]{:S(2)}) collective-permute-start(bf16[4,130,128]{2,1,0:T(8,128)(2,1)} %pad_maximum_fusion.1), channel_id=1, source_target_pairs={{0,16},{16,32},{32,48},{48,64},{64,80},{80,96},{96,112},{112,128},... | collective-permute-start | bytes 399368 | tf_op jit(solution)/shard_map/ppermute | solution.py:31
  57.9 69.2 %copy-start.2 = (bf16[2,256,4,128]{1,3,2,0:T(8,128)(2,1)}, bf16[2,256,4,128]{1,3,2,0:T(8,128)(2,1)S(1)}, u32[]{:S(2)}) copy-start(bf16[2,256,4,128]{1,3,2,0:T(8,128)(2,1)S(1)} %copy.165) | copy-start | bytes 1572868
  65.8 12.4 %collective-permute-start.1 = (bf16[4,130,128]{2,1,0:T(8,128)(2,1)S(1)}, bf16[4,130,128]{2,1,0:T(8,128)(2,1)S(1)}, u32[]{:S(2)}, u32[]{:S(2)}) collective-permute-start(bf16[4,130,128]{2,1,0:T(8,128)(2,1)S(1)} %pad_maximum_fusion.2), channel_id=1, source_target_pairs={{0,16},{16,32},{32,48},{48,64},{64,80},{80,96},{96,112},{112,128},... | collective-permute-start | bytes 399368 | tf_op jit(solution)/shard_map/ppermute | solution.py:31
  78.4 33.7 %copy-start.45 = (f32[4]{0:T(128)S(1)}, f32[4]{0:T(128)}, u32[]{:S(2)}) copy-start(f32[4]{0:T(128)} %get-tuple-element.16) | copy-start | bytes 52
  78.6 15.1 %collective-permute-start.2 = (bf16[4,130,128]{2,1,0:T(8,128)(2,1)S(1)}, bf16[4,130,128]{2,1,0:T(8,128)(2,1)S(1)}, u32[]{:S(2)}, u32[]{:S(2)}) collective-permute-start(bf16[4,130,128]{2,1,0:T(8,128)(2,1)S(1)} %pad_maximum_fusion.3), channel_id=1, source_target_pairs={{0,32},{16,48},{32,64},{48,80},{64,96},{80,112},{96,128},{112,144}... | collective-permute-start | bytes 399368 | tf_op jit(solution)/shard_map/ppermute | solution.py:31
  94.2 16.1 %collective-permute-start.3 = (bf16[4,130,128]{2,1,0:T(8,128)(2,1)S(1)}, bf16[4,130,128]{2,1,0:T(8,128)(2,1)S(1)}, u32[]{:S(2)}, u32[]{:S(2)}) collective-permute-start(bf16[4,130,128]{2,1,0:T(8,128)(2,1)S(1)} %pad_maximum_fusion.4), channel_id=1, source_target_pairs={{0,64},{16,80},{32,96},{48,112},{64,128},{80,144},{96,160},{112,17... | collective-permute-start | bytes 399368 | tf_op jit(solution)/shard_map/ppermute | solution.py:31
  110.8 15.2 %collective-permute-start.4 = (bf16[4,130,128]{2,1,0:T(8,128)(2,1)S(1)}, bf16[4,130,128]{2,1,0:T(8,128)(2,1)}, u32[]{:S(2)}, u32[]{:S(2)}) collective-permute-start(bf16[4,130,128]{2,1,0:T(8,128)(2,1)S(1)} %pad_maximum_fusion.5), channel_id=1, source_target_pairs={{0,128},{16,144},{32,160},{48,176},{64,192},{80,208},{96,224},{112... | collective-permute-start | bytes 399368 | tf_op jit(solution)/shard_map/ppermute | solution.py:31
  149.5 10.1 %collective-permute-start.5 = (bf16[4,130,128]{2,1,0:T(8,128)(2,1)S(1)}, bf16[4,130,128]{2,1,0:T(8,128)(2,1)S(1)}, u32[]{:S(2)}, u32[]{:S(2)}) collective-permute-start(bf16[4,130,128]{2,1,0:T(8,128)(2,1)S(1)} %pad_maximum_fusion), channel_id=1, source_target_pairs={{16,0},{32,16},{48,32},{64,48},{80,64},{96,80},{112,96},{128,112},... | collective-permute-start | bytes 399368 | tf_op jit(solution)/shard_map/ppermute | solution.py:31
  160.3 8.7 %collective-permute-start.6 = (bf16[4,130,128]{2,1,0:T(8,128)(2,1)S(1)}, bf16[4,130,128]{2,1,0:T(8,128)(2,1)S(1)}, u32[]{:S(2)}, u32[]{:S(2)}) collective-permute-start(bf16[4,130,128]{2,1,0:T(8,128)(2,1)S(1)} %pad_maximum_fusion.6), channel_id=1, source_target_pairs={{16,0},{32,16},{48,32},{64,48},{80,64},{96,80},{112,96},{128,112},... | collective-permute-start | bytes 399368 | tf_op jit(solution)/shard_map/ppermute | solution.py:31
  172.2 25.5 %copy-start.1 = (bf16[2,256,4,128]{1,3,2,0:T(8,128)(2,1)S(1)}, bf16[2,256,4,128]{1,3,2,0:T(8,128)(2,1)}, u32[]{:S(2)}) copy-start(bf16[2,256,4,128]{1,3,2,0:T(8,128)(2,1)} %copy-done) | copy-start | bytes 1572868
  172.3 12.3 %collective-permute-start.7 = (bf16[4,130,128]{2,1,0:T(8,128)(2,1)S(1)}, bf16[4,130,128]{2,1,0:T(8,128)(2,1)S(1)}, u32[]{:S(2)}, u32[]{:S(2)}) collective-permute-start(bf16[4,130,128]{2,1,0:T(8,128)(2,1)S(1)} %pad_maximum_fusion.7), channel_id=1, source_target_pairs={{32,0},{48,16},{64,32},{80,48},{96,64},{112,80},{128,96},{144,112}... | collective-permute-start | bytes 399368 | tf_op jit(solution)/shard_map/ppermute | solution.py:31
  189.6 13.8 %collective-permute-start.8 = (bf16[4,130,128]{2,1,0:T(8,128)(2,1)}, bf16[4,130,128]{2,1,0:T(8,128)(2,1)}, u32[]{:S(2)}, u32[]{:S(2)}) collective-permute-start(bf16[4,130,128]{2,1,0:T(8,128)(2,1)} %pad_maximum_fusion.8), channel_id=1, source_target_pairs={{64,0},{80,16},{96,32},{112,48},{128,64},{144,80},{160,96},{176,11... | collective-permute-start | bytes 399368 | tf_op jit(solution)/shard_map/ppermute | solution.py:31
  207.3 8.2 %collective-permute-start.9 = (bf16[4,130,128]{2,1,0:T(8,128)(2,1)S(1)}, bf16[4,130,128]{2,1,0:T(8,128)(2,1)S(1)}, u32[]{:S(2)}, u32[]{:S(2)}) collective-permute-start(bf16[4,130,128]{2,1,0:T(8,128)(2,1)S(1)} %pad_maximum_fusion.9), channel_id=1, source_target_pairs={{128,0},{144,16},{160,32},{176,48},{192,64},{208,80},{224,96},{240... | collective-permute-start | bytes 399368 | tf_op jit(solution)/shard_map/ppermute | solution.py:31
  224.2 12.0 %all-to-all-start = ((bf16[4,64,512]{2,1,0:T(8,128)(2,1)}), bf16[4,64,512]{2,1,0:T(8,128)(2,1)S(1)}, u32[]{:S(2)}, u32[]{:S(2)}) async-start(bf16[4,64,512]{2,1,0:T(8,128)(2,1)} %bitcast.174), calls=%async_computation.1 | async-start | bytes 524288 | tf_op jit(solution)/shard_map/all_to_all | solution.py:123
  (39 other events, 264.4 us)
Sparse Core Ops, SparseCore 0:
  9.8 43.0 all-gather.2
  54.7 84.1 all-gather.4
  141.4 82.7 reduce-scatter.1

commit v10 on v9

--- a/solution.py
+++ b/solution.py
@@ -37,8 +37,8 @@
 
     own = (gain, state)
     identity = (jnp.ones_like(gain), jnp.zeros_like(state))
-    total = fetch(own, 1)
-    step = 1
+    total = join(fetch(own, 1), fetch(own, 2))
+    step = 2
     while step < count:
         total = join(total, fetch(total, step))
         step *= 2

time: 245 us -> 249 us (1.016)
  waiting for transfers between devices: 103 us -> 110 us
  starting transfers between devices: 41.2 us -> 44.5 us
  other arithmetic: 20.9 us -> 17.9 us
    ppermute x10, starting transfers between devices: 35.8 us -> 39.8 us  [fetch(): got = lax.ppermute(packed, axis, pairs).astype(jnp.float32)]
    all_gather x1, waiting for transfers between devices: 23.7 us -> 27 us  [per_device(): features = lax.all_gather(out_grad, 'head', axis=2, tiled=True)[0]]
    all_gather x1, waiting for transfers between devices: 1.96 us -> 4.84 us  [per_device(): lax.all_gather(weight_part, 'ctx', axis=0, tiled=True)]
    reduce_scatter x1, waiting for transfers between devices: 6.81 us -> 9.4 us  [per_device(): by_ctx = lax.psum_scatter(partial, 'ctx', scatter_dimension=0, tiled=True)]
  transfers between devices with their start and end apart: 14 -> 14, of which waited for: 14 -> 14; matrix products, arithmetic and copies ran while one was open for 27% -> 24% of each run, Pallas kernels for 0% -> 0%
where the time goes in v10:
time: 249 us; the launch traced here: 248 us
  waiting for transfers between devices  110 us (44%)
  starting transfers between devices  44.5 us (18%)
  matrix products  27.6 us (11%)
  local copies, waits for them, and re-layouts  19 us (8%)
  other arithmetic  17.9 us (7%)
  between operations  15.5 us (6%)
  blocking collectives  13.5 us (5%)
    ppermute x10, waiting for transfers between devices, fetch(): got = lax.ppermute(packed, axis, pairs).astype(jnp.float32)  63.4 us
    ppermute x10, starting transfers between devices, fetch(): got = lax.ppermute(packed, axis, pairs).astype(jnp.float32)  39.8 us
    all_gather x1, waiting for transfers between devices, per_device(): features = lax.all_gather(out_grad, 'head', axis=2, tiled=True)[0]  27 us
    all_gather x1, blocking collectives, per_device(): lax.all_gather(out_weight.astype(jnp.bfloat16), 'fsdp', axis=0, tiled=True)  13.5 us
    reduce_scatter x1, waiting for transfers between devices, per_device(): by_ctx = lax.psum_scatter(partial, 'ctx', scatter_dimension=0, tiled=True)  9.4 us
    dot_general x1, matrix products, per_device(): jnp.einsum('td,th->dh', columns, mixed, preferred_element_type=jnp.float32)  6.67 us
    dot_general x1, matrix products, per_device(): jnp.dot(columns, weight_full, preferred_element_type=jnp.float32)  5.79 us
  transfers between devices with their start and end apart: 14, of which 14 were waited for; matrix products, arithmetic and copies ran while one was open for 24% of the time, Pallas kernels for 0%

profile of v10, /device:TPU:2, one launch (start us, length us, event | category | flops | bytes accessed | tf_op | source)
XLA Modules:
  0.0 248.1 jit_solution(4171825770924669525)
XLA Ops:
  12.4 13.5 %all_gather.10 = bf16[256,512]{1,0:T(8,128)(2,1)} all-gather(bf16[64,512]{1,0:T(8,128)(2,1)S(1)} %convert_element_type.382), channel_id=1, replica_groups=mesh['ctx'=16,'fsdp'=4,'head'=4] {'fsdp'}, dimensions={0}, use_global_device_ids=true | all-gather | bytes 327680 | tf_op jit(solution)/shard_map/all_gather | solution.py:74
  25.9 27.0 %all-gather.3.cloned.1.call-done = bf16[1,512,4096]{2,1,0:T(8,128)(2,1)} async-done(((bf16[1,512,1024]{2,1,0:T(8,128)(2,1)}), bf16[1,512,4096]{2,1,0:T(8,128)(2,1)}) %all-gather.3.cloned.1.call-update) | async-done | bytes 4194320 | tf_op jit(solution)/shard_map/all_gather | solution.py:73
  56.8 3.5 %collective-permute-start = (bf16[4,130,128]{2,1,0:T(8,128)(2,1)S(1)}, bf16[4,130,128]{2,1,0:T(8,128)(2,1)S(1)}, u32[]{:S(2)}, u32[]{:S(2)}) collective-permute-start(bf16[4,130,128]{2,1,0:T(8,128)(2,1)S(1)} %pad_maximum_fusion.1), channel_id=1, source_target_pairs={{0,16},{16,32},{32,48},{48,64},{64,80},{80,96},{96,112},{112,128},... | collective-permute-start | bytes 399368 | tf_op jit(solution)/shard_map/ppermute | solution.py:31
  60.3 4.5 %collective-permute-start.1 = (bf16[4,130,128]{2,1,0:T(8,128)(2,1)S(1)}, bf16[4,130,128]{2,1,0:T(8,128)(2,1)S(1)}, u32[]{:S(2)}, u32[]{:S(2)}) collective-permute-start(bf16[4,130,128]{2,1,0:T(8,128)(2,1)S(1)} %pad_maximum_fusion.1), channel_id=1, source_target_pairs={{0,32},{16,48},{32,64},{48,80},{64,96},{80,112},{96,128},{112,144}... | collective-permute-start | bytes 399368 | tf_op jit(solution)/shard_map/ppermute | solution.py:31
  67.0 7.9 %collective-permute-done.1 = bf16[4,130,128]{2,1,0:T(8,128)(2,1)S(1)} collective-permute-done((bf16[4,130,128]{2,1,0:T(8,128)(2,1)S(1)}, bf16[4,130,128]{2,1,0:T(8,128)(2,1)S(1)}, u32[]{:S(2)}, u32[]{:S(2)}) %collective-permute-start.1) | collective-permute-done | bytes 133152 | tf_op jit(solution)/shard_map/ppermute | solution.py:31
  75.5 3.1 %collective-permute-start.2 = (bf16[4,130,128]{2,1,0:T(8,128)(2,1)S(1)}, bf16[4,130,128]{2,1,0:T(8,128)(2,1)S(1)}, u32[]{:S(2)}, u32[]{:S(2)}) collective-permute-start(bf16[4,130,128]{2,1,0:T(8,128)(2,1)S(1)} %pad_maximum_fusion.2), channel_id=1, source_target_pairs={{0,32},{16,48},{32,64},{48,80},{64,96},{80,112},{96,128},{112,144}... | collective-permute-start | bytes 399368 | tf_op jit(solution)/shard_map/ppermute | solution.py:31
  79.4 11.7 %collective-permute-done.2 = bf16[4,130,128]{2,1,0:T(8,128)(2,1)S(1)} collective-permute-done((bf16[4,130,128]{2,1,0:T(8,128)(2,1)S(1)}, bf16[4,130,128]{2,1,0:T(8,128)(2,1)S(1)}, u32[]{:S(2)}, u32[]{:S(2)}) %collective-permute-start.2) | collective-permute-done | bytes 133152 | tf_op jit(solution)/shard_map/ppermute | solution.py:31
  91.6 7.3 %collective-permute-start.3 = (bf16[4,130,128]{2,1,0:T(8,128)(2,1)S(1)}, bf16[4,130,128]{2,1,0:T(8,128)(2,1)S(1)}, u32[]{:S(2)}, u32[]{:S(2)}) collective-permute-start(bf16[4,130,128]{2,1,0:T(8,128)(2,1)S(1)} %pad_maximum_fusion.3), channel_id=1, source_target_pairs={{0,64},{16,80},{32,96},{48,112},{64,128},{80,144},{96,160},{112,17... | collective-permute-start | bytes 399368 | tf_op jit(solution)/shard_map/ppermute | solution.py:31
  100.4 8.2 %collective-permute-done.3 = bf16[4,130,128]{2,1,0:T(8,128)(2,1)S(1)} collective-permute-done((bf16[4,130,128]{2,1,0:T(8,128)(2,1)S(1)}, bf16[4,130,128]{2,1,0:T(8,128)(2,1)S(1)}, u32[]{:S(2)}, u32[]{:S(2)}) %collective-permute-start.3) | collective-permute-done | bytes 133152 | tf_op jit(solution)/shard_map/ppermute | solution.py:31
  113.7 10.8 %collective-permute-done.4 = bf16[4,130,128]{2,1,0:T(8,128)(2,1)S(1)} collective-permute-done((bf16[4,130,128]{2,1,0:T(8,128)(2,1)S(1)}, bf16[4,130,128]{2,1,0:T(8,128)(2,1)S(1)}, u32[]{:S(2)}, u32[]{:S(2)}) %collective-permute-start.4) | collective-permute-done | bytes 133152 | tf_op jit(solution)/shard_map/ppermute | solution.py:31
  128.4 6.7 %convolution_convert_fusion = bf16[4096,512]{1,0:T(8,128)(2,1)} fusion(bf16[512,4096]{1,0:T(8,128)(2,1)} %bitcast.151, bf16[64,8,4,128]{3,2,1,0:T(4,128)(2,1)} %bitcast.143), kind=kOutput, calls=%fused_computation | convolution fusion | flops 2149580800 | bytes 8912896 | tf_op jit(solution)/shard_map/td,th->dh/dot_general | solution.py:114
  135.1 4.8 %all-gather.5.cloned.1.call-done = bf16[4096,512]{1,0:T(8,128)(2,1)} async-done(((bf16[256,512]{1,0:T(8,128)(2,1)}), bf16[4096,512]{1,0:T(8,128)(2,1)}) %all-gather.5.cloned.1.call-update) | async-done | bytes 4194320 | tf_op jit(solution)/shard_map/all_gather | solution.py:118
  142.8 5.8 %fusion.78 = f32[512,512]{1,0:T(8,128)S(1)} fusion(bf16[512,4096]{1,0:T(8,128)(2,1)} %bitcast.152, bf16[4096,512]{1,0:T(8,128)(2,1)} %all-gather.5.cloned.1.call-done), kind=kOutput, calls=%fused_computation.180 | convolution fusion | flops 2147483648 | bytes 9437184 | tf_op jit(solution)/shard_map/dot_general | solution.py:120
  153.4 4.7 %collective-permute-start.5 = (bf16[4,130,128]{2,1,0:T(8,128)(2,1)S(1)}, bf16[4,130,128]{2,1,0:T(8,128)(2,1)S(1)}, u32[]{:S(2)}, u32[]{:S(2)}) collective-permute-start(bf16[4,130,128]{2,1,0:T(8,128)(2,1)S(1)} %pad_maximum_fusion), channel_id=1, source_target_pairs={{16,0},{32,16},{48,32},{64,48},{80,64},{96,80},{112,96},{128,112},... | collective-permute-start | bytes 399368 | tf_op jit(solution)/shard_map/ppermute | solution.py:31
  164.7 5.5 %collective-permute-done.6 = bf16[4,130,128]{2,1,0:T(8,128)(2,1)S(1)} collective-permute-done((bf16[4,130,128]{2,1,0:T(8,128)(2,1)S(1)}, bf16[4,130,128]{2,1,0:T(8,128)(2,1)S(1)}, u32[]{:S(2)}, u32[]{:S(2)}) %collective-permute-start.6) | collective-permute-done | bytes 133152 | tf_op jit(solution)/shard_map/ppermute | solution.py:31
  173.5 7.8 %collective-permute-start.7 = (bf16[4,130,128]{2,1,0:T(8,128)(2,1)S(1)}, bf16[4,130,128]{2,1,0:T(8,128)(2,1)S(1)}, u32[]{:S(2)}, u32[]{:S(2)}) collective-permute-start(bf16[4,130,128]{2,1,0:T(8,128)(2,1)S(1)} %pad_maximum_fusion.5), channel_id=1, source_target_pairs={{32,0},{48,16},{64,32},{80,48},{96,64},{112,80},{128,96},{144,112}... | collective-permute-start | bytes 399368 | tf_op jit(solution)/shard_map/ppermute | solution.py:31
  181.3 2.7 %convolution_bitcast_fusion.6 = f32[2,256,4,128]{1,3,2,0:T(8,128)} fusion(bf16[2,4,256,256]{3,2,1,0:T(8,128)(2,1)} %copy-done.10, bf16[2,256,4,128]{3,2,1,0:T(4,128)(2,1)S(1)} %copy-done.7), kind=kOutput, calls=%fused_computation.18 | convolution fusion | flops 134217728 | bytes 2621440 | tf_op jit(solution)/shard_map/chtu,cuhe->cthe/dot_general | solution.py:131
  184.1 4.9 %collective-permute-done.7 = bf16[4,130,128]{2,1,0:T(8,128)(2,1)S(1)} collective-permute-done((bf16[4,130,128]{2,1,0:T(8,128)(2,1)S(1)}, bf16[4,130,128]{2,1,0:T(8,128)(2,1)S(1)}, u32[]{:S(2)}, u32[]{:S(2)}) %collective-permute-start.7) | collective-permute-done | bytes 133152 | tf_op jit(solution)/shard_map/ppermute | solution.py:31
  191.7 3.8 %collective-permute-start.8 = (bf16[4,130,128]{2,1,0:T(8,128)(2,1)S(1)}, bf16[4,130,128]{2,1,0:T(8,128)(2,1)}, u32[]{:S(2)}, u32[]{:S(2)}) collective-permute-start(bf16[4,130,128]{2,1,0:T(8,128)(2,1)S(1)} %pad_maximum_fusion.6), channel_id=1, source_target_pairs={{64,0},{80,16},{96,32},{112,48},{128,64},{144,80},{160,96},{176,11... | collective-permute-start | bytes 399368 | tf_op jit(solution)/shard_map/ppermute | solution.py:31
  200.3 5.0 %collective-permute-done.8 = bf16[4,130,128]{2,1,0:T(8,128)(2,1)} collective-permute-done((bf16[4,130,128]{2,1,0:T(8,128)(2,1)S(1)}, bf16[4,130,128]{2,1,0:T(8,128)(2,1)}, u32[]{:S(2)}, u32[]{:S(2)}) %collective-permute-start.8) | collective-permute-done | bytes 133152 | tf_op jit(solution)/shard_map/ppermute | solution.py:31
  210.5 6.3 %collective-permute-done.9 = bf16[4,130,128]{2,1,0:T(8,128)(2,1)S(1)} collective-permute-done((bf16[4,130,128]{2,1,0:T(8,128)(2,1)S(1)}, bf16[4,130,128]{2,1,0:T(8,128)(2,1)S(1)}, u32[]{:S(2)}, u32[]{:S(2)}) %collective-permute-start.9) | collective-permute-done | bytes 133152 | tf_op jit(solution)/shard_map/ppermute | solution.py:31
  220.0 9.4 %reduce-scatter.2.cloned.1.call-done = bf16[256,512]{1,0:T(8,128)(2,1)} async-done(((bf16[4096,512]{1,0:T(8,128)(2,1)}), bf16[256,512]{1,0:T(8,128)(2,1)}) %reduce-scatter.2.cloned.1.call-update) | async-done | bytes 262160 | tf_op jit(solution)/shard_map/reduce_scatter | solution.py:121
  229.4 4.5 %all-to-all-start = ((bf16[4,64,512]{2,1,0:T(8,128)(2,1)}), bf16[4,64,512]{2,1,0:T(8,128)(2,1)S(1)}, u32[]{:S(2)}, u32[]{:S(2)}) async-start(bf16[4,64,512]{2,1,0:T(8,128)(2,1)} %bitcast.144), calls=%async_computation.1 | async-start | bytes 524288 | tf_op jit(solution)/shard_map/all_to_all | solution.py:123
  235.8 4.8 %all-to-all-done = bf16[4,64,512]{2,1,0:T(8,128)(2,1)S(1)} async-done(((bf16[4,64,512]{2,1,0:T(8,128)(2,1)}), bf16[4,64,512]{2,1,0:T(8,128)(2,1)S(1)}, u32[]{:S(2)}, u32[]{:S(2)}) %all-to-all-start) | async-done | bytes 262176 | tf_op jit(solution)/shard_map/all_to_all | solution.py:123
  (231 shorter events, 58.2 us)
Async XLA Ops:
  7.2 45.9 %copy-start.16 = (bf16[1,512,512]{2,1,0:T(8,128)(2,1)S(1)}, bf16[1,512,512]{2,1,0:T(8,128)(2,1)}, u32[]{:S(2)}) copy-start(bf16[1,512,512]{2,1,0:T(8,128)(2,1)} %param.12) | copy-start | bytes 1572868
  7.2 46.1 %copy-start.17 = (bf16[1,512,512]{2,1,0:T(8,128)(2,1)S(1)}, bf16[1,512,512]{2,1,0:T(8,128)(2,1)}, u32[]{:S(2)}) copy-start(bf16[1,512,512]{2,1,0:T(8,128)(2,1)} %param.13) | copy-start | bytes 1572868
  7.2 45.7 %all-gather.3.cloned.1.call-start = ((), (), s32[]{:S(2)}) async-start(), calls=%async_computation.2 | async-start | bytes 5242880 | tf_op jit(solution)/shard_map/all_gather | solution.py:73
  7.9 132.0 %all-gather.5.cloned.1.call-start = ((), (), s32[]{:S(2)}) async-start(), calls=%async_computation.3 | async-start | bytes 4456448 | tf_op jit(solution)/shard_map/all_gather | solution.py:118
  53.0 176.5 %reduce-scatter.2.cloned.1.call-start = ((), (), s32[]{:S(2)}) async-start(), calls=%async_computation.4 | async-start | bytes 4456448 | tf_op jit(solution)/shard_map/reduce_scatter | solution.py:121
  53.1 25.6 %copy-start.25 = (f32[2,4,256]{2,1,0:T(4,128)}, f32[2,4,256]{2,1,0:T(4,128)S(1)}, u32[]{:S(2)}) copy-start(f32[2,4,256]{2,1,0:T(4,128)S(1)} %reduce_window_sum.24) | copy-start | bytes 24580
  53.3 25.4 %copy-start.6 = (bf16[2,256,4,128]{3,2,1,0:T(4,128)(2,1)}, bf16[2,256,4,128]{3,2,1,0:T(4,128)(2,1)S(1)}, u32[]{:S(2)}) copy-start(bf16[2,256,4,128]{3,2,1,0:T(4,128)(2,1)S(1)} %reshape.708) | copy-start | bytes 1572868
  53.4 45.5 %copy-start.4 = (bf16[2,256,4,128]{3,2,1,0:T(4,128)(2,1)}, bf16[2,256,4,128]{3,2,1,0:T(4,128)(2,1)S(1)}, u32[]{:S(2)}) copy-start(bf16[2,256,4,128]{3,2,1,0:T(4,128)(2,1)S(1)} %reshape.712) | copy-start | bytes 1572868
  56.8 10.2 %collective-permute-start = (bf16[4,130,128]{2,1,0:T(8,128)(2,1)S(1)}, bf16[4,130,128]{2,1,0:T(8,128)(2,1)S(1)}, u32[]{:S(2)}, u32[]{:S(2)}) collective-permute-start(bf16[4,130,128]{2,1,0:T(8,128)(2,1)S(1)} %pad_maximum_fusion.1), channel_id=1, source_target_pairs={{0,16},{16,32},{32,48},{48,64},{64,80},{80,96},{96,112},{112,128},... | collective-permute-start | bytes 399368 | tf_op jit(solution)/shard_map/ppermute | solution.py:31
  60.3 14.6 %collective-permute-start.1 = (bf16[4,130,128]{2,1,0:T(8,128)(2,1)S(1)}, bf16[4,130,128]{2,1,0:T(8,128)(2,1)S(1)}, u32[]{:S(2)}, u32[]{:S(2)}) collective-permute-start(bf16[4,130,128]{2,1,0:T(8,128)(2,1)S(1)} %pad_maximum_fusion.1), channel_id=1, source_target_pairs={{0,32},{16,48},{32,64},{48,80},{64,96},{80,112},{96,128},{112,144}... | collective-permute-start | bytes 399368 | tf_op jit(solution)/shard_map/ppermute | solution.py:31
  65.2 60.0 %copy-start.2 = (bf16[2,256,4,128]{1,3,2,0:T(8,128)(2,1)}, bf16[2,256,4,128]{1,3,2,0:T(8,128)(2,1)S(1)}, u32[]{:S(2)}) copy-start(bf16[2,256,4,128]{1,3,2,0:T(8,128)(2,1)S(1)} %copy.158) | copy-start | bytes 1572868
  75.5 15.6 %collective-permute-start.2 = (bf16[4,130,128]{2,1,0:T(8,128)(2,1)S(1)}, bf16[4,130,128]{2,1,0:T(8,128)(2,1)S(1)}, u32[]{:S(2)}, u32[]{:S(2)}) collective-permute-start(bf16[4,130,128]{2,1,0:T(8,128)(2,1)S(1)} %pad_maximum_fusion.2), channel_id=1, source_target_pairs={{0,32},{16,48},{32,64},{48,80},{64,96},{80,112},{96,128},{112,144}... | collective-permute-start | bytes 399368 | tf_op jit(solution)/shard_map/ppermute | solution.py:31
  79.4 29.2 %copy-start.8 = (bf16[2,4,256,256]{3,2,1,0:T(8,128)(2,1)}, bf16[2,4,256,256]{3,2,1,0:T(8,128)(2,1)S(1)}, u32[]{:S(2)}) copy-start(bf16[2,4,256,256]{3,2,1,0:T(8,128)(2,1)S(1)} %multiply_convert_fusion.1) | copy-start | bytes 3145732
  91.6 19.3 %copy-start.33 = (f32[4]{0:T(128)S(1)}, f32[4]{0:T(128)}, u32[]{:S(2)}) copy-start(f32[4]{0:T(128)} %copy-done.32) | copy-start | bytes 52
  91.6 17.0 %collective-permute-start.3 = (bf16[4,130,128]{2,1,0:T(8,128)(2,1)S(1)}, bf16[4,130,128]{2,1,0:T(8,128)(2,1)S(1)}, u32[]{:S(2)}, u32[]{:S(2)}) collective-permute-start(bf16[4,130,128]{2,1,0:T(8,128)(2,1)S(1)} %pad_maximum_fusion.3), channel_id=1, source_target_pairs={{0,64},{16,80},{32,96},{48,112},{64,128},{80,144},{96,160},{112,17... | collective-permute-start | bytes 399368 | tf_op jit(solution)/shard_map/ppermute | solution.py:31
  109.6 15.0 %collective-permute-start.4 = (bf16[4,130,128]{2,1,0:T(8,128)(2,1)S(1)}, bf16[4,130,128]{2,1,0:T(8,128)(2,1)S(1)}, u32[]{:S(2)}, u32[]{:S(2)}) collective-permute-start(bf16[4,130,128]{2,1,0:T(8,128)(2,1)S(1)} %pad_maximum_fusion.4), channel_id=1, source_target_pairs={{0,128},{16,144},{32,160},{48,176},{64,192},{80,208},{96,224},{112... | collective-permute-start | bytes 399368 | tf_op jit(solution)/shard_map/ppermute | solution.py:31
  153.4 11.3 %collective-permute-start.5 = (bf16[4,130,128]{2,1,0:T(8,128)(2,1)S(1)}, bf16[4,130,128]{2,1,0:T(8,128)(2,1)S(1)}, u32[]{:S(2)}, u32[]{:S(2)}) collective-permute-start(bf16[4,130,128]{2,1,0:T(8,128)(2,1)S(1)} %pad_maximum_fusion), channel_id=1, source_target_pairs={{16,0},{32,16},{48,32},{64,48},{80,64},{96,80},{112,96},{128,112},... | collective-permute-start | bytes 399368 | tf_op jit(solution)/shard_map/ppermute | solution.py:31
  158.1 12.1 %collective-permute-start.6 = (bf16[4,130,128]{2,1,0:T(8,128)(2,1)S(1)}, bf16[4,130,128]{2,1,0:T(8,128)(2,1)S(1)}, u32[]{:S(2)}, u32[]{:S(2)}) collective-permute-start(bf16[4,130,128]{2,1,0:T(8,128)(2,1)S(1)} %pad_maximum_fusion), channel_id=1, source_target_pairs={{32,0},{48,16},{64,32},{80,48},{96,64},{112,80},{128,96},{144,112}... | collective-permute-start | bytes 399368 | tf_op jit(solution)/shard_map/ppermute | solution.py:31
  171.5 18.9 %copy-start.29 = (f32[4]{0:T(128)}, f32[4]{0:T(128)S(1)}, u32[]{:S(2)}) copy-start(f32[4]{0:T(128)S(1)} %get-tuple-element.35) | copy-start | bytes 52
  173.5 22.0 %copy-start.1 = (bf16[2,256,4,128]{1,3,2,0:T(8,128)(2,1)S(1)}, bf16[2,256,4,128]{1,3,2,0:T(8,128)(2,1)}, u32[]{:S(2)}) copy-start(bf16[2,256,4,128]{1,3,2,0:T(8,128)(2,1)} %copy-done) | copy-start | bytes 1572868
  173.5 15.5 %collective-permute-start.7 = (bf16[4,130,128]{2,1,0:T(8,128)(2,1)S(1)}, bf16[4,130,128]{2,1,0:T(8,128)(2,1)S(1)}, u32[]{:S(2)}, u32[]{:S(2)}) collective-permute-start(bf16[4,130,128]{2,1,0:T(8,128)(2,1)S(1)} %pad_maximum_fusion.5), channel_id=1, source_target_pairs={{32,0},{48,16},{64,32},{80,48},{96,64},{112,80},{128,96},{144,112}... | collective-permute-start | bytes 399368 | tf_op jit(solution)/shard_map/ppermute | solution.py:31
  191.7 13.6 %collective-permute-start.8 = (bf16[4,130,128]{2,1,0:T(8,128)(2,1)S(1)}, bf16[4,130,128]{2,1,0:T(8,128)(2,1)}, u32[]{:S(2)}, u32[]{:S(2)}) collective-permute-start(bf16[4,130,128]{2,1,0:T(8,128)(2,1)S(1)} %pad_maximum_fusion.6), channel_id=1, source_target_pairs={{64,0},{80,16},{96,32},{112,48},{128,64},{144,80},{160,96},{176,11... | collective-permute-start | bytes 399368 | tf_op jit(solution)/shard_map/ppermute | solution.py:31
  209.1 7.7 %collective-permute-start.9 = (bf16[4,130,128]{2,1,0:T(8,128)(2,1)S(1)}, bf16[4,130,128]{2,1,0:T(8,128)(2,1)S(1)}, u32[]{:S(2)}, u32[]{:S(2)}) collective-permute-start(bf16[4,130,128]{2,1,0:T(8,128)(2,1)S(1)} %pad_maximum_fusion.7), channel_id=1, source_target_pairs={{128,0},{144,16},{160,32},{176,48},{192,64},{208,80},{224,96},{240... | collective-permute-start | bytes 399368 | tf_op jit(solution)/shard_map/ppermute | solution.py:31
  229.4 11.2 %all-to-all-start = ((bf16[4,64,512]{2,1,0:T(8,128)(2,1)}), bf16[4,64,512]{2,1,0:T(8,128)(2,1)S(1)}, u32[]{:S(2)}, u32[]{:S(2)}) async-start(bf16[4,64,512]{2,1,0:T(8,128)(2,1)} %bitcast.144), calls=%async_computation.1 | async-start | bytes 524288 | tf_op jit(solution)/shard_map/all_to_all | solution.py:123
  (36 other events, 275.1 us)
Sparse Core Ops, SparseCore 0:
  9.8 43.0 all-gather.2
  54.7 85.1 all-gather.4
  142.5 86.8 reduce-scatter.1
